TPU v7x, 256 devices: a whole 4x4x8 slice. The times are simulated.
256 devices in a mesh: dp: 64 (over y, z, core), tensor: 4 (over x).
Axes of the slice: x: 4, y: 4, z: 8, core: 2. Of those that a mesh axis runs over, the one named last changes fastest.
Arguments:
- query: bfloat16 [4096, 2560], P('dp', 'tensor'), may hold values from -18 to 18
- new_kv: bfloat16 [2, 4096, 512], P(None, 'dp', 'tensor'), may hold values from -7 to 7
- key_value_pages: bfloat16 [2, 6080, 128, 512], P(None, 'dp', None, 'tensor'), may hold values from -7 to 7
- page_table: int32 [4096, 32], P('dp'), may hold values from 0 to 6079, as said below
- cache_len: int32 [4096], P('dp'), may hold values from 1 to 4096, as said below
- residual: bfloat16 [4096, 2560], P('dp'), may hold values from -6 to 6
- out_weight: bfloat16 [2560, 2560], P('tensor'), may hold values from -0.125 to 0.125
- norm_gain: float32 [2560], replicated, may hold values from 0.25 to 1.75
- expert_ids: int32 [4096, 6], P('dp'), may hold values from 0 to 63, all different within a row; in each aligned block of 64 rows (0 to 63, 64 to 127, ...) at most 9 rows name the same one
- combine_weights: float32 [4096, 6], P('dp'), may hold values from 0.1 to 1
- expert_w1: bfloat16 [64, 2560, 2, 1536], P('dp', None, None, 'tensor'), may hold values from -0.125 to 0.125
- expert_w2: bfloat16 [64, 1536, 2560], P('dp', 'tensor'), may hold values from -0.15625 to 0.15625
Outputs:
- layer_out: bfloat16 [4096, 2560], P('dp', 'tensor')
Inputs may be any that keep to these rules, and one draw needn't show every extreme that they name: `page_table`: entry j of a request's row is the page holding its cache positions j * 128 to (j + 1) * 128 - 1; the pages of request r are among the 95 pages from (r // 64) * 95 on; no page serves two requests; entries past the last used page repeat it. `cache_len`: 6 requests, in 6 different blocks of 64 requests, hold more than (31) * 128 tokens, one of them exactly 4096; all others hold fewer than 64. `expert_ids`: each row names 6 different experts; among the rows of one device (aligned blocks of 64 rows) no expert is named more than 9 times.
All inputs are finite; a program needn't handle non-finite values.
Results may differ from a plain program's by a relative error of at most 0.012.
Values may be sent and summed in bfloat16 or wider, within the bound.
No kernel may reach another device: no remote copies, remote signals or barrier semaphores. Data moves between devices by JAX's collectives and lax.ppermute only.
A program may use at most 128 MiB of HBM per device.

v0:
```python
import math

import jax
import jax.numpy as jnp
from jax import lax
from jax.experimental import pallas as pl
from jax.experimental.pallas import tpu as pltpu
from jax.sharding import PartitionSpec as P

HEAD_SIZE = 128
SHORT = 64


def attention_kernel(
    table_ref, len_ref, base_ref, q_ref, new_k_ref, new_v_ref, kv_hbm, o_ref,
    short_k, short_v, long_k, long_v, sem,
):
    rows = q_ref.shape[0]
    head_dim = new_k_ref.shape[1]
    groups = q_ref.shape[1] // head_dim
    table_width = table_ref.shape[1]
    pool_pages = kv_hbm.shape[1]
    page_size = kv_hbm.shape[2]
    chunk = 16
    scale_of_score = 1.0 / math.sqrt(head_dim)
    base = base_ref[0]

    def local_page(r, j):
        return jnp.minimum(jnp.maximum(table_ref[r, j] - base, 0), pool_pages - 1)

    def longest(r, carry):
        best_row, best_len = carry
        length = len_ref[r]
        better = length > best_len
        return jnp.where(better, r, best_row), jnp.where(better, length, best_len)

    long_row, long_len = lax.fori_loop(0, rows, longest, (jnp.int32(0), len_ref[0]))

    def short_copy(r, which, buf):
        return pltpu.make_async_copy(
            kv_hbm.at[which, local_page(r, 0), pl.ds(0, SHORT), :],
            buf.at[pl.ds(r * SHORT, SHORT), :],
            sem.at[which, r],
        )

    def long_copy(j, which, buf):
        return pltpu.make_async_copy(
            kv_hbm.at[which, local_page(long_row, j)],
            buf.at[pl.ds(j * page_size, page_size), :],
            sem.at[2 + which, j],
        )

    @pl.loop(0, rows)
    def _(r):
        short_copy(r, 0, short_k).start()
        short_copy(r, 1, short_v).start()

    @pl.loop(0, table_width)
    def _(j):
        long_copy(j, 0, long_k).start()
        long_copy(j, 1, long_v).start()

    @pl.loop(0, rows)
    def _(r):
        short_copy(r, 0, short_k).wait()
        short_copy(r, 1, short_v).wait()

    def attend(qh, keys, values, valid, new_k, new_v):
        scores = lax.dot_general(
            qh, keys, (((1,), (1,)), ((), ())), preferred_element_type=jnp.float32
        ) * scale_of_score
        fresh = jnp.sum(
            qh.astype(jnp.float32) * new_k.astype(jnp.float32), axis=1, keepdims=True
        ) * scale_of_score
        scores = jnp.where(valid, scores, -1e30)
        row_max = jnp.maximum(jnp.max(scores, axis=1, keepdims=True), fresh)
        weights = jnp.where(valid, jnp.exp(scores - row_max), 0.0)
        weight_new = jnp.exp(fresh - row_max)
        denominator = jnp.sum(weights, axis=1, keepdims=True) + weight_new
        numerator = jnp.dot(
            weights.astype(jnp.bfloat16), values, preferred_element_type=jnp.float32
        )
        numerator = numerator + (
            weight_new.astype(jnp.bfloat16).astype(jnp.float32) * new_v.astype(jnp.float32)
        )
        return (numerator / denominator).astype(o_ref.dtype)

    width = chunk * SHORT
    row = lax.broadcasted_iota(jnp.int32, (chunk, width), 0)
    col = lax.broadcasted_iota(jnp.int32, (chunk, width), 1)

    @pl.loop(0, rows // chunk)
    def _(c):
        r0 = pl.multiple_of(c * chunk, chunk)
        k0 = pl.multiple_of(c * width, width)
        keys = short_k[pl.ds(k0, width), :]
        values = short_v[pl.ds(k0, width), :]
        lengths = jnp.zeros((chunk, 1), jnp.int32)
        for i in range(chunk):
            lengths = jnp.where(row[:, :1] == i, jnp.minimum(len_ref[r0 + i], SHORT), lengths)
        valid = (col >= row * SHORT) & (col < row * SHORT + lengths)
        new_k = new_k_ref[pl.ds(r0, chunk), :]
        new_v = new_v_ref[pl.ds(r0, chunk), :]
        for h in range(groups):
            qh = q_ref[pl.ds(r0, chunk), h * head_dim:(h + 1) * head_dim]
            o_ref[pl.ds(r0, chunk), h * head_dim:(h + 1) * head_dim] = attend(
                qh, keys, values, valid, new_k, new_v
            )

    @pl.loop(0, table_width)
    def _(j):
        long_copy(j, 0, long_k).wait()
        long_copy(j, 1, long_v).wait()

    long_col = lax.broadcasted_iota(jnp.int32, (chunk, table_width * page_size), 1)
    long_valid = long_col < long_len
    own_row = lax.broadcasted_iota(jnp.int32, (chunk, 1), 0)

    @pl.when(long_len >= SHORT)
    def _():
        r0 = pl.multiple_of((long_row // chunk) * chunk, chunk)
        new_k = new_k_ref[pl.ds(r0, chunk), :]
        new_v = new_v_ref[pl.ds(r0, chunk), :]
        chosen = (own_row + r0) == long_row
        for h in range(groups):
            qh = q_ref[pl.ds(r0, chunk), h * head_dim:(h + 1) * head_dim]
            result = attend(qh, long_k[...], long_v[...], long_valid, new_k, new_v)
            current = o_ref[pl.ds(r0, chunk), h * head_dim:(h + 1) * head_dim]
            o_ref[pl.ds(r0, chunk), h * head_dim:(h + 1) * head_dim] = jnp.where(
                chosen, result, current
            )


def local_attention(query, new_kv, key_value_pages, page_table, cache_len):
    row_count = query.shape[0]
    pool_pages = key_value_pages.shape[1]
    page_size = key_value_pages.shape[2]
    head_dim = HEAD_SIZE
    table_width = page_table.shape[1]
    base = jnp.full((1,), lax.axis_index("dp") * pool_pages, jnp.int32)
    smem = pl.BlockSpec(memory_space=pltpu.SMEM)
    vmem = pl.BlockSpec(memory_space=pltpu.VMEM)
    rows = row_count * SHORT + table_width * page_size
    return pl.pallas_call(
        attention_kernel,
        out_shape=jax.ShapeDtypeStruct(query.shape, jnp.bfloat16),
        in_specs=[smem, smem, smem, vmem, vmem, vmem, pl.BlockSpec(memory_space=pl.ANY)],
        out_specs=vmem,
        scratch_shapes=[
            pltpu.VMEM((row_count * SHORT, head_dim), key_value_pages.dtype),
            pltpu.VMEM((row_count * SHORT, head_dim), key_value_pages.dtype),
            pltpu.VMEM((table_width * page_size, head_dim), key_value_pages.dtype),
            pltpu.VMEM((table_width * page_size, head_dim), key_value_pages.dtype),
            pltpu.SemaphoreType.DMA((4, row_count)),
        ],
        cost_estimate=pl.CostEstimate(
            flops=4 * 16 * query.shape[1] * rows,
            transcendentals=16 * query.shape[1] // head_dim * rows,
            bytes_accessed=2 * 2 * head_dim * rows,
        ),
    )(page_table, cache_len, base, query, new_kv[0], new_kv[1], key_value_pages)


def ring_shift(x, shift, axis_name, size):
    return lax.ppermute(x, axis_name, [(i, (i + shift) % size) for i in range(size)])


def ring_reduce_scatter(blocks, axis_name, size, index):
    total = lax.dynamic_index_in_dim(blocks, index, 0, keepdims=False).astype(jnp.float32)
    for shift in range(1, size):
        outgoing = lax.dynamic_index_in_dim(blocks, (index + shift) % size, 0, keepdims=False)
        total = total + ring_shift(outgoing, shift, axis_name, size).astype(jnp.float32)
    return total


def ring_all_gather(x, axis_name, size):
    return [x] + [ring_shift(x, shift, axis_name, size) for shift in range(1, size)]


def dense_all_to_all(x, axis_name):
    lanes = 128
    flat = x.reshape(x.shape[0], x.shape[1] * x.shape[2] // lanes, lanes)
    moved = lax.all_to_all(flat, axis_name, split_axis=0, concat_axis=0, tiled=True)
    return moved.reshape(x.shape)


def per_device(
    query,
    new_kv,
    key_value_pages,
    page_table,
    cache_len,
    residual,
    out_weight,
    norm_gain,
    expert_ids,
    combine_weights,
    expert_w1,
    expert_w2,
):
    tensor_size = lax.axis_size("tensor")
    tensor_index = lax.axis_index("tensor")
    attn = local_attention(query, new_kv, key_value_pages, page_table, cache_len)
    row_count, model_width = residual.shape
    share_width = model_width // tensor_size
    share_start = tensor_index * share_width

    split_weight = out_weight.reshape(out_weight.shape[0], tensor_size, share_width)
    partial_proj = jnp.einsum(
        "rk,kuc->urc", attn, split_weight, preferred_element_type=jnp.float32
    )
    summed = ring_reduce_scatter(partial_proj, "tensor", tensor_size, tensor_index)
    residual_share = lax.dynamic_slice_in_dim(residual, share_start, share_width, 1)
    state = residual_share.astype(jnp.float32) + summed
    square_sum = sum(ring_all_gather(jnp.sum(state * state, axis=1, keepdims=True), "tensor", tensor_size))
    mean_square = square_sum / model_width
    gain_share = lax.dynamic_slice_in_dim(norm_gain, share_start, share_width, 0)
    normed = (state * lax.rsqrt(mean_square + 1e-05) * gain_share).astype(jnp.bfloat16)

    local_experts = expert_w1.shape[0]
    top_count = expert_ids.shape[1]
    experts = local_experts * lax.axis_size("dp")
    capacity = min(
        row_count, max(3, (3 * row_count * top_count + 2 * experts - 1) // (2 * experts))
    )
    flat_ids = expert_ids.reshape(-1)
    choice_rows = flat_ids.shape[0]
    row_iota = jnp.arange(choice_rows, dtype=jnp.int32)
    choice_hot = (flat_ids[:, None] == jnp.arange(experts, dtype=jnp.int32)[None, :]).astype(
        jnp.bfloat16
    )
    strictly_lower = (row_iota[:, None] > row_iota[None, :]).astype(jnp.bfloat16)
    earlier = jnp.dot(strictly_lower, choice_hot, preferred_element_type=jnp.float32)
    slot_rank = jnp.sum(earlier * choice_hot.astype(jnp.float32), axis=1).astype(jnp.int32)
    slot_index = (flat_ids * capacity + slot_rank).reshape(row_count, top_count)
    slot_ids = jnp.arange(experts * capacity, dtype=jnp.int32)
    hit = slot_index[:, :, None] == slot_ids[None, None, :]
    placing = jnp.any(hit, axis=1).astype(jnp.bfloat16)
    mixing = jnp.sum(jnp.where(hit, combine_weights[:, :, None], 0.0), axis=1)

    outgoing = jnp.dot(placing.T, normed, preferred_element_type=jnp.float32)
    outgoing = outgoing.astype(jnp.bfloat16).reshape(experts, capacity, share_width)
    mixing = mixing.reshape(row_count, experts, capacity)
    split_w1 = expert_w1.reshape(tensor_size, share_width, 2, expert_w1.shape[-1])
    split_w2 = expert_w2[0].reshape(expert_w2.shape[1], tensor_size, share_width)

    expert_mix = None
    streams = 1
    bounds = [capacity * i // streams for i in range(streams + 1)]
    for lo, hi in zip(bounds[:-1], bounds[1:]):
        slots = hi - lo
        arrived = dense_all_to_all(outgoing[:, lo:hi], "dp")
        pieces = ring_all_gather(arrived, "tensor", tensor_size)
        gate_up = None
        for shift, piece in enumerate(pieces):
            weight = lax.dynamic_index_in_dim(
                split_w1, (tensor_index - shift) % tensor_size, 0, keepdims=False
            )
            term = jnp.einsum("snc,cgf->sngf", piece, weight, preferred_element_type=jnp.float32)
            gate_up = term if gate_up is None else gate_up + term
        activated = (jax.nn.silu(gate_up[:, :, 0, :]) * gate_up[:, :, 1, :]).astype(
            jnp.bfloat16
        )
        partial_out = jnp.einsum(
            "snf,fuc->usnc", activated, split_w2, preferred_element_type=jnp.float32
        ).astype(jnp.bfloat16)
        expert_sum = ring_reduce_scatter(partial_out, "tensor", tensor_size, tensor_index)
        expert_sum = expert_sum.astype(jnp.bfloat16)
        returned_rows = dense_all_to_all(expert_sum, "dp")
        part_mix = jnp.dot(
            mixing[:, :, lo:hi].reshape(row_count, experts * slots),
            returned_rows.reshape(experts * slots, share_width).astype(jnp.float32),
            precision=lax.Precision.HIGHEST,
        )
        expert_mix = part_mix if expert_mix is None else expert_mix + part_mix
    return (state + expert_mix).astype(jnp.bfloat16)


def solution(mesh):
    return jax.shard_map(
        per_device,
        mesh=mesh,
        in_specs=(
            P("dp", "tensor"),
            P(None, "dp", "tensor"),
            P(None, "dp", None, "tensor"),
            P("dp", None),
            P("dp"),
            P("dp", None),
            P("tensor", None),
            P(),
            P("dp", None),
            P("dp", None),
            P("dp", None, None, "tensor"),
            P("dp", "tensor", None),
        ),
        out_specs=P("dp", "tensor"),
        check_vma=False,
    )
```

profile of v0, /device:TPU:1, one launch (start us, length us, event | category | flops | bytes accessed | tf_op | source)
XLA Modules:
  0.0 188.6 jit_solution(14760633907040629083)
XLA Ops:
  0.0 1.3 slice_bitcast_fusion
  1.3 1.4 copy.54.table_ref
  2.7 13.3 %shard_map.118 = bf16[64,640]{1,0:T(8,128)(2,1)} custom-call(s32[64,32]{1,0:T(8,128)} %copy.54.table_ref, s32[64]{0:T(128)} %len_ref.1, s32[1]{0:T(128)} %bitcast.base_ref, bf16[64,640]{1,0:T(8,128)(2,1)} %q_ref.1, bf16[64,128]{1,0:T(8,128)(2,1)} %get-tuple-element.18.new_k_ref, bf16[64,128]{1,0:T(8,128)(2,1)} %get-tuple-element.17.new_v_ref, ...), custom_call_target="tpu_custom_call" | custom-call | flops 335544320 | bytes 4194304 | tf_op jit(solution)/shard_map/pallas_call | solution.py:144
  16.0 1.6 fusion
  18.5 2.1 %collective-permute-start = (f32[64,640]{1,0:T(8,128)S(1)}, f32[64,640]{1,0:T(8,128)S(1)}, u32[]{:S(2)}, u32[]{:S(2)}) collective-permute-start(f32[64,640]{1,0:T(8,128)S(1)} %get-tuple-element.14), channel_id=1, source_target_pairs={{0,1},{1,2},{2,3},{3,0},{4,5},{5,6},{6,7},{7,4},{8,9},{9,10},{10,1... | collective-permute-start | bytes 491528 | tf_op jit(solution)/shard_map/ppermute | solution.py:165
  20.6 2.5 %collective-permute-start.1 = (f32[64,640]{1,0:T(8,128)S(1)}, f32[64,640]{1,0:T(8,128)S(1)}, u32[]{:S(2)}, u32[]{:S(2)}) collective-permute-start(f32[64,640]{1,0:T(8,128)S(1)} %get-tuple-element.16), channel_id=1, source_target_pairs={{0,2},{1,3},{2,0},{3,1},{4,6},{5,7},{6,4},{7,5},{8,10},{9,11},{10,... | collective-permute-start | bytes 491528 | tf_op jit(solution)/shard_map/ppermute | solution.py:165
  23.1 1.2 collective-permute-start.2
  24.9 5.3 %collective-permute-done.1 = f32[64,640]{1,0:T(8,128)S(1)} collective-permute-done((f32[64,640]{1,0:T(8,128)S(1)}, f32[64,640]{1,0:T(8,128)S(1)}, u32[]{:S(2)}, u32[]{:S(2)}) %collective-permute-start.1) | collective-permute-done | bytes 163872 | tf_op jit(solution)/shard_map/ppermute | solution.py:165
  30.3 1.1 multiply_reduce_fusion
  31.4 1.0 collective-permute-start.3
  32.4 1.9 %collective-permute-start.4 = (f32[64,1]{0,1:T(1,128)S(1)}, f32[64,1]{0,1:T(1,128)S(1)}, u32[]{:S(2)}, u32[]{:S(2)}) collective-permute-start(f32[64,1]{0,1:T(1,128)S(1)} %bitcast.91), channel_id=1, source_target_pairs={{0,2},{1,3},{2,0},{3,1},{4,6},{5,7},{6,4},{7,5},{8,10},{9,11},{10,... | collective-permute-start | bytes 776 | tf_op jit(solution)/shard_map/ppermute | solution.py:165
  34.3 1.3 collective-permute-start.5
  37.8 38.8 %all_to_all.10 = bf16[64,45,128]{2,1,0:T(8,128)(2,1)S(1)} all-to-all(bf16[64,45,128]{2,1,0:T(8,128)(2,1)S(1)} %reshape_reshape.6), channel_id=1, replica_groups=mesh['dp'=64,'tensor'=4] {'dp'}, dimensions={0} | all-to-all | bytes 1474560 | tf_op jit(solution)/shard_map/all_to_all | solution.py:183
  77.2 1.0 copy.60
  78.2 3.3 %collective-permute-start.7 = (bf16[64,9,640]{2,0,1:T(8,128)(2,1)}, bf16[64,9,640]{2,0,1:T(8,128)(2,1)}, u32[]{:S(2)}, u32[]{:S(2)}) collective-permute-start(bf16[64,9,640]{2,0,1:T(8,128)(2,1)} %copy.60), channel_id=1, source_target_pairs={{0,2},{1,3},{2,0},{3,1},{4,6},{5,7},{6,4},{7,5},{8,10},{9,11},{10,... | collective-permute-start | bytes 2211848 | tf_op jit(solution)/shard_map/ppermute | solution.py:165
  81.5 5.2 %constant_dynamic-slice_fusion = (bf16[1,640,2,384]{3,2,1,0:T(2,128)(2,1)S(1)}, bf16[1,640,2,384]{3,2,1,0:T(2,128)(2,1)S(1)}, bf16[1,640,2,384]{3,2,1,0:T(2,128)(2,1)}, bf16[1,640,2,384]{3,2,1,0:T(2,128)(2,1)}) fusion(bf16[4,640,2,384]{3,2,1,0:T(2,128)(2,1)} %bitcast.88, s32[]{:T(128)S(6)} %select_n.92, s32[]{:T(128)S(6)} %select_n.90, s32[]{:T(128)S(6)} %select_n.88, ...), kind=kLoop, calls=%fused_computation.56 | loop fusion | bytes 7864336 | tf_op jit(solution)/shard_map/jit(dynamic_index_in_dim)/dynamic_slice | solution.py:256
  86.7 4.4 %reshape_squeeze.3 = bf16[384,4,640]{2,1,0:T(4,128)(2,1)} reshape(bf16[1,384,2560]{2,1,0:T(8,128)(2,1)} %param.23) | data formatting | bytes 3932160 | tf_op jit(solution)/shard_map/reshape;squeeze | solution.py:245
  91.1 2.1 %fusion.13 = f32[64,9,2,384]{3,0,2,1:T(8,128)S(1)} fusion(bf16[1,640,2,384]{3,2,1,0:T(2,128)(2,1)} %get-tuple-element.10, bf16[64,9,640,1]{2,1,0,3:T(8,128)(2,1)S(1)} %bitcast.87), kind=kOutput, calls=%fused_computation.23 | convolution fusion | flops 566231040 | bytes 3489792 | tf_op jit(solution)/shard_map/snc,cgf->sngf/dot_general | solution.py:259
  93.2 4.2 %collective-permute-done.6 = bf16[64,9,640]{2,0,1:T(8,128)(2,1)} collective-permute-done((bf16[64,9,640]{2,0,1:T(8,128)(2,1)}, bf16[64,9,640]{2,0,1:T(8,128)(2,1)}, u32[]{:S(2)}, u32[]{:S(2)}) %collective-permute-start.6) | collective-permute-done | bytes 737312 | tf_op jit(solution)/shard_map/ppermute | solution.py:165
  97.4 2.0 %fusion.12 = f32[64,9,2,384]{3,0,2,1:T(8,128)S(1)} fusion(bf16[1,640,2,384]{3,2,1,0:T(2,128)(2,1)S(1)} %copy-done, bf16[64,9,640]{2,0,1:T(8,128)(2,1)} %collective-permute-done.6), kind=kOutput, calls=%fused_computation.21 | convolution fusion | flops 566231040 | bytes 3489792 | tf_op jit(solution)/shard_map/snc,cgf->sngf/dot_general | solution.py:259
  99.4 14.4 %collective-permute-done.7 = bf16[64,9,640]{2,0,1:T(8,128)(2,1)} collective-permute-done((bf16[64,9,640]{2,0,1:T(8,128)(2,1)}, bf16[64,9,640]{2,0,1:T(8,128)(2,1)}, u32[]{:S(2)}, u32[]{:S(2)}) %collective-permute-start.7) | collective-permute-done | bytes 737312 | tf_op jit(solution)/shard_map/ppermute | solution.py:165
  113.8 2.0 %fusion.11 = f32[64,9,2,384]{3,0,2,1:T(8,128)S(1)} fusion(bf16[1,640,2,384]{3,2,1,0:T(2,128)(2,1)S(1)} %get-tuple-element.8, bf16[64,9,640]{2,0,1:T(8,128)(2,1)} %collective-permute-done.7), kind=kOutput, calls=%fused_computation.19 | convolution fusion | flops 566231040 | bytes 3489792 | tf_op jit(solution)/shard_map/snc,cgf->sngf/dot_general | solution.py:259
  115.8 0.9 add_add_fusion
  117.4 1.7 convolution_convert_fusion
  119.4 1.6 collective-permute-start.11
  121.0 16.7 %collective-permute-done.10 = bf16[64,9,640]{2,0,1:T(8,128)(2,1)S(1)} collective-permute-done((bf16[64,9,640]{2,0,1:T(8,128)(2,1)S(1)}, bf16[64,9,640]{2,0,1:T(8,128)(2,1)S(1)}, u32[]{:S(2)}, u32[]{:S(2)}) %collective-permute-start.10) | collective-permute-done | bytes 737312 | tf_op jit(solution)/shard_map/ppermute | solution.py:165
  137.7 15.2 %collective-permute-done.11 = bf16[64,9,640]{2,0,1:T(8,128)(2,1)S(1)} collective-permute-done((bf16[64,9,640]{2,0,1:T(8,128)(2,1)S(1)}, bf16[64,9,640]{2,0,1:T(8,128)(2,1)S(1)}, u32[]{:S(2)}, u32[]{:S(2)}) %collective-permute-start.11) | collective-permute-done | bytes 737312 | tf_op jit(solution)/shard_map/ppermute | solution.py:165
  152.9 2.2 %collective-permute-done.9 = bf16[64,9,640]{2,0,1:T(8,128)(2,1)S(1)} collective-permute-done((bf16[64,9,640]{2,0,1:T(8,128)(2,1)S(1)}, bf16[64,9,640]{2,0,1:T(8,128)(2,1)S(1)}, u32[]{:S(2)}, u32[]{:S(2)}) %collective-permute-start.9) | collective-permute-done | bytes 737312 | tf_op jit(solution)/shard_map/ppermute | solution.py:165
  156.0 1.4 reshape.47
  157.4 6.5 %all-to-all-start.1 = ((bf16[64,45,128]{2,1,0:T(8,128)(2,1)}), bf16[64,45,128]{2,1,0:T(8,128)(2,1)S(1)}, u32[]{:S(2)}, u32[]{:S(2)}) async-start(bf16[64,45,128]{2,1,0:T(8,128)(2,1)} %reshape.47), calls=%async_computation.1 | async-start | bytes 1572864 | tf_op jit(solution)/shard_map/all_to_all | solution.py:183
  164.1 22.7 %all-to-all-done.1 = bf16[64,45,128]{2,1,0:T(8,128)(2,1)S(1)} async-done(((bf16[64,45,128]{2,1,0:T(8,128)(2,1)}), bf16[64,45,128]{2,1,0:T(8,128)(2,1)S(1)}, u32[]{:S(2)}, u32[]{:S(2)}) %all-to-all-start.1) | async-done | bytes 737312 | tf_op jit(solution)/shard_map/all_to_all | solution.py:183
  187.4 1.1 fusion.8
  (41 shorter events, 7.0 us)
Async XLA Ops:
  2.7 13.3 %copy-start.1 = (bf16[640,2560]{1,0:T(8,128)(2,1)S(1)}, bf16[640,2560]{1,0:T(8,128)(2,1)}, u32[]{:S(2)}) copy-start(bf16[640,2560]{1,0:T(8,128)(2,1)} %param.18) | copy-start | bytes 9830404
  16.0 8.2 %copy-start.4 = (s32[64,6]{0,1:T(8,128)S(1)}, s32[64,6]{0,1:T(8,128)}, u32[]{:S(2)}) copy-start(s32[64,6]{0,1:T(8,128)} %param.20) | copy-start | bytes 4612
  17.6 0.9 copy-start.2
  18.5 6.4 %collective-permute-start = (f32[64,640]{1,0:T(8,128)S(1)}, f32[64,640]{1,0:T(8,128)S(1)}, u32[]{:S(2)}, u32[]{:S(2)}) collective-permute-start(f32[64,640]{1,0:T(8,128)S(1)} %get-tuple-element.14), channel_id=1, source_target_pairs={{0,1},{1,2},{2,3},{3,0},{4,5},{5,6},{6,7},{7,4},{8,9},{9,10},{10,1... | collective-permute-start | bytes 491528 | tf_op jit(solution)/shard_map/ppermute | solution.py:165
  20.6 9.6 %collective-permute-start.1 = (f32[64,640]{1,0:T(8,128)S(1)}, f32[64,640]{1,0:T(8,128)S(1)}, u32[]{:S(2)}, u32[]{:S(2)}) collective-permute-start(f32[64,640]{1,0:T(8,128)S(1)} %get-tuple-element.16), channel_id=1, source_target_pairs={{0,2},{1,3},{2,0},{3,1},{4,6},{5,7},{6,4},{7,5},{8,10},{9,11},{10,... | collective-permute-start | bytes 491528 | tf_op jit(solution)/shard_map/ppermute | solution.py:165
  23.1 7.2 %collective-permute-start.2 = (f32[64,640]{1,0:T(8,128)S(1)}, f32[64,640]{1,0:T(8,128)S(1)}, u32[]{:S(2)}, u32[]{:S(2)}) collective-permute-start(f32[64,640]{1,0:T(8,128)S(1)} %get-tuple-element.15), channel_id=1, source_target_pairs={{0,3},{1,0},{2,1},{3,2},{4,7},{5,4},{6,5},{7,6},{8,11},{9,8},{10,9... | collective-permute-start | bytes 491528 | tf_op jit(solution)/shard_map/ppermute | solution.py:165
  31.4 5.2 %collective-permute-start.3 = (f32[64,1]{0,1:T(1,128)S(1)}, f32[64,1]{0,1:T(1,128)S(1)}, u32[]{:S(2)}, u32[]{:S(2)}) collective-permute-start(f32[64,1]{0,1:T(1,128)S(1)} %bitcast.90), channel_id=1, source_target_pairs={{0,1},{1,2},{2,3},{3,0},{4,5},{5,6},{6,7},{7,4},{8,9},{9,10},{10,1... | collective-permute-start | bytes 776 | tf_op jit(solution)/shard_map/ppermute | solution.py:165
  32.4 4.2 %collective-permute-start.4 = (f32[64,1]{0,1:T(1,128)S(1)}, f32[64,1]{0,1:T(1,128)S(1)}, u32[]{:S(2)}, u32[]{:S(2)}) collective-permute-start(f32[64,1]{0,1:T(1,128)S(1)} %bitcast.91), channel_id=1, source_target_pairs={{0,2},{1,3},{2,0},{3,1},{4,6},{5,7},{6,4},{7,5},{8,10},{9,11},{10,... | collective-permute-start | bytes 776 | tf_op jit(solution)/shard_map/ppermute | solution.py:165
  34.3 2.4 %collective-permute-start.5 = (f32[64,1]{0,1:T(1,128)S(1)}, f32[64,1]{0,1:T(1,128)S(1)}, u32[]{:S(2)}, u32[]{:S(2)}) collective-permute-start(f32[64,1]{0,1:T(1,128)S(1)} %bitcast.92), channel_id=1, source_target_pairs={{0,3},{1,0},{2,1},{3,2},{4,7},{5,4},{6,5},{7,6},{8,11},{9,8},{10,9... | collective-permute-start | bytes 776 | tf_op jit(solution)/shard_map/ppermute | solution.py:165
  78.2 19.2 %collective-permute-start.6 = (bf16[64,9,640]{2,0,1:T(8,128)(2,1)}, bf16[64,9,640]{2,0,1:T(8,128)(2,1)}, u32[]{:S(2)}, u32[]{:S(2)}) collective-permute-start(bf16[64,9,640]{2,0,1:T(8,128)(2,1)} %copy.60), channel_id=1, source_target_pairs={{0,1},{1,2},{2,3},{3,0},{4,5},{5,6},{6,7},{7,4},{8,9},{9,10},{10,1... | collective-permute-start | bytes 2211848 | tf_op jit(solution)/shard_map/ppermute | solution.py:165
  78.2 35.6 %collective-permute-start.7 = (bf16[64,9,640]{2,0,1:T(8,128)(2,1)}, bf16[64,9,640]{2,0,1:T(8,128)(2,1)}, u32[]{:S(2)}, u32[]{:S(2)}) collective-permute-start(bf16[64,9,640]{2,0,1:T(8,128)(2,1)} %copy.60), channel_id=1, source_target_pairs={{0,2},{1,3},{2,0},{3,1},{4,6},{5,7},{6,4},{7,5},{8,10},{9,11},{10,... | collective-permute-start | bytes 2211848 | tf_op jit(solution)/shard_map/ppermute | solution.py:165
  91.1 6.3 %copy-start = (bf16[1,640,2,384]{3,2,1,0:T(2,128)(2,1)S(1)}, bf16[1,640,2,384]{3,2,1,0:T(2,128)(2,1)}, u32[]{:S(2)}) copy-start(bf16[1,640,2,384]{3,2,1,0:T(2,128)(2,1)} %get-tuple-element.9) | copy-start | bytes 2949124
  91.1 24.7 %collective-permute-start.8 = (bf16[64,9,640]{2,0,1:T(8,128)(2,1)}, bf16[64,9,640]{2,0,1:T(8,128)(2,1)S(1)}, u32[]{:S(2)}, u32[]{:S(2)}) collective-permute-start(bf16[64,9,640]{2,0,1:T(8,128)(2,1)} %copy.60), channel_id=1, source_target_pairs={{0,3},{1,0},{2,1},{3,2},{4,7},{5,4},{6,5},{7,6},{8,11},{9,8},{10,9... | collective-permute-start | bytes 2211848 | tf_op jit(solution)/shard_map/ppermute | solution.py:165
  115.8 1.5 copy-start.3
  119.3 18.4 %collective-permute-start.10 = (bf16[64,9,640]{2,0,1:T(8,128)(2,1)S(1)}, bf16[64,9,640]{2,0,1:T(8,128)(2,1)S(1)}, u32[]{:S(2)}, u32[]{:S(2)}) collective-permute-start(bf16[64,9,640]{2,0,1:T(8,128)(2,1)S(1)} %get-tuple-element.13), channel_id=1, source_target_pairs={{0,2},{1,3},{2,0},{3,1},{4,6},{5,7},{6,4},{7,5},{8,10},{9,11},{10,... | collective-permute-start | bytes 2211848 | tf_op jit(solution)/shard_map/ppermute | solution.py:165
  119.4 33.5 %collective-permute-start.11 = (bf16[64,9,640]{2,0,1:T(8,128)(2,1)S(1)}, bf16[64,9,640]{2,0,1:T(8,128)(2,1)S(1)}, u32[]{:S(2)}, u32[]{:S(2)}) collective-permute-start(bf16[64,9,640]{2,0,1:T(8,128)(2,1)S(1)} %get-tuple-element.12), channel_id=1, source_target_pairs={{0,3},{1,0},{2,1},{3,2},{4,7},{5,4},{6,5},{7,6},{8,11},{9,8},{10,9... | collective-permute-start | bytes 2211848 | tf_op jit(solution)/shard_map/ppermute | solution.py:165
  121.0 34.1 %collective-permute-start.9 = (bf16[64,9,640]{2,0,1:T(8,128)(2,1)S(1)}, bf16[64,9,640]{2,0,1:T(8,128)(2,1)S(1)}, u32[]{:S(2)}, u32[]{:S(2)}) collective-permute-start(bf16[64,9,640]{2,0,1:T(8,128)(2,1)S(1)} %get-tuple-element.11), channel_id=1, source_target_pairs={{0,1},{1,2},{2,3},{3,0},{4,5},{5,6},{6,7},{7,4},{8,9},{9,10},{10,1... | collective-permute-start | bytes 2211848 | tf_op jit(solution)/shard_map/ppermute | solution.py:165
  156.0 7.9 %copy-start.5 = (f32[64,6]{0,1:T(8,128)S(1)}, f32[64,6]{0,1:T(8,128)}, u32[]{:S(2)}) copy-start(f32[64,6]{0,1:T(8,128)} %param.21) | copy-start | bytes 4612
  157.4 29.4 %all-to-all-start.1 = ((bf16[64,45,128]{2,1,0:T(8,128)(2,1)}), bf16[64,45,128]{2,1,0:T(8,128)(2,1)S(1)}, u32[]{:S(2)}, u32[]{:S(2)}) async-start(bf16[64,45,128]{2,1,0:T(8,128)(2,1)} %reshape.47), calls=%async_computation.1 | async-start | bytes 1572864 | tf_op jit(solution)/shard_map/all_to_all | solution.py:183
where the time goes:
time: 189 us
  waiting for transfers between devices  80.9 us (43%)
  blocking collectives  38.8 us (21%)
  starting transfers between devices  21.5 us (11%)
  local copies, waits for them, and re-layouts  20 us (11%)
  Pallas kernels  13.3 us (7%)
  matrix products  12.1 us (6%)
  other arithmetic  1.93 us (1%)
    ppermute x12, waiting for transfers between devices, ring_shift(): lax.ppermute(x, axis_name, [(i, (i + shift) % size) for i in range(size)])  58.1 us
    all_to_all x1, blocking collectives, dense_all_to_all(): lax.all_to_all(flat, axis_name, split_axis=0, concat_axis=0, tiled=True)  38.8 us
    all_to_all x1, waiting for transfers between devices, dense_all_to_all(): lax.all_to_all(flat, axis_name, split_axis=0, concat_axis=0, tiled=True)  22.7 us
    ppermute x12, starting transfers between devices, ring_shift(): lax.ppermute(x, axis_name, [(i, (i + shift) % size) for i in range(size)])  15 us
    pallas_call x1, Pallas kernels, local_attention(): pl.pallas_call(attention_kernel, out_shape=jax.ShapeDtypeStruct(query.sha...  13.3 us
    dot_general x4, matrix products, per_device(): jnp.einsum('snc,cgf->sngf', piece, weight, preferred_element_type=jnp.flo...  6.97 us
    all_to_all x1, starting transfers between devices, dense_all_to_all(): lax.all_to_all(flat, axis_name, split_axis=0, concat_axis=0, tiled=True)  6.47 us
    dynamic_slice x1, local copies, waits for them, and re-layouts, per_device(): lax.dynamic_index_in_dim(split_w1, (tensor_index - shift) % tensor_size,...  5.16 us
  transfers between devices with their start and end apart: 13, of which 8 were waited for; matrix products, arithmetic and copies ran while one was open for 9% of the time, Pallas kernels for 0%

commit v1 on v0

--- a/solution.py
+++ b/solution.py
@@ -245,8 +245,7 @@
     split_w2 = expert_w2[0].reshape(expert_w2.shape[1], tensor_size, share_width)
 
     expert_mix = None
-    streams = 1
-    bounds = [capacity * i // streams for i in range(streams + 1)]
+    bounds = [0, capacity // 3, capacity]
     for lo, hi in zip(bounds[:-1], bounds[1:]):
         slots = hi - lo
         arrived = dense_all_to_all(outgoing[:, lo:hi], "dp")

time: 189 us -> 200 us (1.058)
  starting transfers between devices: 21.5 us -> 63 us
  blocking collectives: 38.8 us -> 0 us
  local copies, waits for them, and re-layouts: 20 us -> 29.3 us
  waiting for transfers between devices: 80.9 us -> 76.5 us
    all_to_all x1 -> x4, starting transfers between devices: 6.47 us -> 46.3 us  [dense_all_to_all(): lax.all_to_all(flat, axis_name, split_axis=0, concat_axis=0, tiled=True)]
    all_to_all x1 -> x0, blocking collectives: 38.8 us -> none  [dense_all_to_all(): lax.all_to_all(flat, axis_name, split_axis=0, concat_axis=0, tiled=True)]
    all_to_all x1 -> x4, waiting for transfers between devices: 22.7 us -> 17.4 us  [dense_all_to_all(): lax.all_to_all(flat, axis_name, split_axis=0, concat_axis=0, tiled=True)]
    reshape x1 -> x4, local copies, waits for them, and re-layouts: 1.39 us -> 5.36 us  [dense_all_to_all(): flat = x.reshape(x.shape[0], x.shape[1] * x.shape[2] // lanes, lanes)]
    reshape x2 -> x4, local copies, waits for them, and re-layouts: 1.62 us -> 4.49 us  [dense_all_to_all(): return moved.reshape(x.shape)]
    squeeze x2 -> x3, local copies, waits for them, and re-layouts: 0.25 us -> 2.32 us  [ring_reduce_scatter(): lax.dynamic_index_in_dim(blocks, (index + shift) % size, 0, keepdims=False)]
    dot_general x4 -> x8, matrix products: 6.97 us -> 4.97 us  [per_device(): jnp.einsum('snc,cgf->sngf', piece, weight, preferred_element_type=jnp.flo...]
    ppermute x12 -> x18, starting transfers between devices: 15 us -> 16.7 us  [ring_shift(): lax.ppermute(x, axis_name, [(i, (i + shift) % size) for i in range(size)])]
  transfers between devices with their start and end apart: 13 -> 22, of which waited for: 8 -> 12; matrix products, arithmetic and copies ran while one was open for 9% -> 15% of each run, Pallas kernels for 0% -> 0%
where the time goes in v1:
time: 200 us; the launch traced here: 199 us
  waiting for transfers between devices  76.5 us (38%)
  starting transfers between devices  63 us (32%)
  local copies, waits for them, and re-layouts  29.3 us (15%)
  Pallas kernels  13.3 us (7%)
  matrix products  13.1 us (7%)
  other arithmetic  3.2 us (2%)
    ppermute x18, waiting for transfers between devices, ring_shift(): lax.ppermute(x, axis_name, [(i, (i + shift) % size) for i in range(size)])  59 us
    all_to_all x4, starting transfers between devices, dense_all_to_all(): lax.all_to_all(flat, axis_name, split_axis=0, concat_axis=0, tiled=True)  46.3 us
    all_to_all x4, waiting for transfers between devices, dense_all_to_all(): lax.all_to_all(flat, axis_name, split_axis=0, concat_axis=0, tiled=True)  17.4 us
    ppermute x18, starting transfers between devices, ring_shift(): lax.ppermute(x, axis_name, [(i, (i + shift) % size) for i in range(size)])  16.7 us
    pallas_call x1, Pallas kernels, local_attention(): pl.pallas_call(attention_kernel, out_shape=jax.ShapeDtypeStruct(query.sha...  13.3 us
    reshape x4, local copies, waits for them, and re-layouts, dense_all_to_all(): flat = x.reshape(x.shape[0], x.shape[1] * x.shape[2] // lanes, lanes)  5.36 us
    dynamic_slice x1, local copies, waits for them, and re-layouts, per_device(): lax.dynamic_index_in_dim(split_w1, (tensor_index - shift) % tensor_size,...  5.09 us
    dot_general x8, matrix products, per_device(): jnp.einsum('snc,cgf->sngf', piece, weight, preferred_element_type=jnp.flo...  4.97 us
  transfers between devices with their start and end apart: 22, of which 12 were waited for; matrix products, arithmetic and copies ran while one was open for 15% of the time, Pallas kernels for 0%

profile of v1, /device:TPU:1, one launch (start us, length us, event | category | flops | bytes accessed | tf_op | source)
XLA Modules:
  0.0 198.8 jit_solution(12117410949924394819)
XLA Ops:
  0.0 1.4 copy.68.table_ref
  1.4 1.3 slice_bitcast_fusion
  2.8 13.3 %shard_map.118 = bf16[64,640]{1,0:T(8,128)(2,1)} custom-call(s32[64,32]{1,0:T(8,128)} %copy.68.table_ref, s32[64]{0:T(128)} %len_ref.1, s32[1]{0:T(128)} %bitcast.base_ref, bf16[64,640]{1,0:T(8,128)(2,1)} %q_ref.1, bf16[64,128]{1,0:T(8,128)(2,1)} %get-tuple-element.21.new_k_ref, bf16[64,128]{1,0:T(8,128)(2,1)} %get-tuple-element.20.new_v_ref, ...), custom_call_target="tpu_custom_call" | custom-call | flops 335544320 | bytes 4194304 | tf_op jit(solution)/shard_map/pallas_call | solution.py:144
  16.0 2.4 %fusion = f32[64,4,640]{2,0,1:T(8,128)} fusion(bf16[80,4,8,640]{3,2,1,0:T(8,128)(2,1)S(1)} %bitcast.137, bf16[64,640]{1,0:T(8,128)(2,1)} %shard_map.118), kind=kOutput, calls=%fused_computation | convolution fusion | flops 209715200 | bytes 4014080 | tf_op jit(solution)/shard_map/rk,kuc->urc/dot_general | solution.py:209
  19.6 3.4 %collective-permute-start.2 = (f32[64,640]{1,0:T(8,128)S(1)}, f32[64,640]{1,0:T(8,128)S(1)}, u32[]{:S(2)}, u32[]{:S(2)}) collective-permute-start(f32[64,640]{1,0:T(8,128)S(1)} %get-tuple-element.18), channel_id=1, source_target_pairs={{0,3},{1,0},{2,1},{3,2},{4,7},{5,4},{6,5},{7,6},{8,11},{9,8},{10,9... | collective-permute-start | bytes 491528 | tf_op jit(solution)/shard_map/ppermute | solution.py:165
  24.8 2.9 %collective-permute-done.2 = f32[64,640]{1,0:T(8,128)S(1)} collective-permute-done((f32[64,640]{1,0:T(8,128)S(1)}, f32[64,640]{1,0:T(8,128)S(1)}, u32[]{:S(2)}, u32[]{:S(2)}) %collective-permute-start.2) | collective-permute-done | bytes 163872 | tf_op jit(solution)/shard_map/ppermute | solution.py:165
  27.6 1.7 collective-permute-done.1
  29.3 4.8 %collective-permute-done = f32[64,640]{1,0:T(8,128)S(1)} collective-permute-done((f32[64,640]{1,0:T(8,128)S(1)}, f32[64,640]{1,0:T(8,128)S(1)}, u32[]{:S(2)}, u32[]{:S(2)}) %collective-permute-start) | collective-permute-done | bytes 163872 | tf_op jit(solution)/shard_map/ppermute | solution.py:165
  37.7 1.6 collective-permute-done.4
  42.0 13.6 %all-to-all-start = ((bf16[64,15,128]{2,1,0:T(8,128)(2,1)}), bf16[64,15,128]{2,1,0:T(8,128)(2,1)S(1)}, u32[]{:S(2)}, u32[]{:S(2)}) async-start(bf16[64,15,128]{2,1,0:T(8,128)(2,1)} %reshape.84), calls=%async_computation | async-start | bytes 524288 | tf_op jit(solution)/shard_map/all_to_all | solution.py:183
  55.7 4.4 %reshape_squeeze.3 = bf16[384,4,640]{2,1,0:T(4,128)(2,1)} reshape(bf16[1,384,2560]{2,1,0:T(8,128)(2,1)} %param.23) | data formatting | bytes 3932160 | tf_op jit(solution)/shard_map/reshape;squeeze | solution.py:245
  60.1 5.1 %constant_dynamic-slice_fusion.1 = (bf16[1,640,2,384]{3,2,1,0:T(2,128)(2,1)S(1)}, bf16[1,640,2,384]{3,2,1,0:T(2,128)(2,1)S(1)}, bf16[1,640,2,384]{3,2,1,0:T(2,128)(2,1)S(1)}, bf16[1,640,2,384]{3,2,1,0:T(2,128)(2,1)}) fusion(bf16[4,640,2,384]{3,2,1,0:T(2,128)(2,1)} %bitcast.136, s32[]{:T(128)S(6)} %select_n.113, s32[]{:T(128)S(6)} %select_n.111, ...), kind=kLoop, calls=%fused_computation.81 | loop fusion | bytes 7864336 | tf_op jit(solution)/shard_map/jit(dynamic_index_in_dim)/dynamic_slice | solution.py:255
  66.3 2.2 %reshape.89 = bf16[64,30,128]{2,1,0:T(8,128)(2,1)} reshape(bf16[64,6,640]{2,1,0:T(8,128)(2,1)} %slice.45) | data formatting | bytes 983040 | tf_op jit(solution)/shard_map/reshape | solution.py:182
  69.2 10.5 %all-to-all-start.2 = ((bf16[64,30,128]{2,1,0:T(8,128)(2,1)}), bf16[64,30,128]{2,1,0:T(8,128)(2,1)}, u32[]{:S(2)}, u32[]{:S(2)}) async-start(bf16[64,30,128]{2,1,0:T(8,128)(2,1)} %reshape.89), calls=%async_computation.2 | async-start | bytes 1048576 | tf_op jit(solution)/shard_map/all_to_all | solution.py:183
  80.8 1.8 collective-permute-start.8
  82.6 1.3 collective-permute-start.7
  84.3 11.6 %collective-permute-done.6 = bf16[64,3,640]{2,0,1:T(8,128)(2,1)S(1)} collective-permute-done((bf16[64,3,640]{2,0,1:T(8,128)(2,1)S(1)}, bf16[64,3,640]{2,0,1:T(8,128)(2,1)S(1)}, u32[]{:S(2)}, u32[]{:S(2)}) %collective-permute-start.6) | collective-permute-done | bytes 245792 | tf_op jit(solution)/shard_map/ppermute | solution.py:165
  96.8 1.2 fusion.16
  98.0 2.2 %reshape.90 = bf16[64,6,640]{2,1,0:T(8,128)(2,1)} reshape(bf16[64,30,128]{2,1,0:T(8,128)(2,1)} %all-to-all-done.2) | data formatting | bytes 983040 | tf_op jit(solution)/shard_map/reshape | solution.py:184
  102.1 2.5 %fusion.12 = bf16[64,3,4,640]{3,0,2,1:T(8,128)(2,1)S(1)} fusion(bf16[384,4,640]{2,1,0:T(4,128)(2,1)} %reshape_squeeze.3, f32[64,3,2,384]{3,0,2,1:T(8,128)} %fusion.16), kind=kOutput, calls=%fused_computation.10 | convolution fusion | flops 378421248 | bytes 3538944 | tf_op jit(solution)/shard_map/snf,fuc->usnc/dot_general | solution.py:263
  104.8 2.6 %collective-permute-start.10 = (bf16[64,3,640]{2,0,1:T(8,128)(2,1)S(1)}, bf16[64,3,640]{2,0,1:T(8,128)(2,1)S(1)}, u32[]{:S(2)}, u32[]{:S(2)}) collective-permute-start(bf16[64,3,640]{2,0,1:T(8,128)(2,1)S(1)} %get-tuple-element.16), channel_id=1, source_target_pairs={{0,2},{1,3},{2,0},{3,1},{4,6},{5,7},{6,4},{7,5},{8,10},{9,11},{10,... | collective-permute-start | bytes 737288 | tf_op jit(solution)/shard_map/ppermute | solution.py:165
  108.1 4.6 %collective-permute-done.14 = bf16[64,6,640]{2,0,1:T(8,128)(2,1)S(1)} collective-permute-done((bf16[64,6,640]{2,0,1:T(8,128)(2,1)S(1)}, bf16[64,6,640]{2,0,1:T(8,128)(2,1)S(1)}, u32[]{:S(2)}, u32[]{:S(2)}) %collective-permute-start.14) | collective-permute-done | bytes 491552 | tf_op jit(solution)/shard_map/ppermute | solution.py:165
  112.7 1.2 collective-permute-start.13
  114.6 15.7 %collective-permute-done.12 = bf16[64,6,640]{2,0,1:T(8,128)(2,1)S(1)} collective-permute-done((bf16[64,6,640]{2,0,1:T(8,128)(2,1)S(1)}, bf16[64,6,640]{2,0,1:T(8,128)(2,1)S(1)}, u32[]{:S(2)}, u32[]{:S(2)}) %collective-permute-start.12) | collective-permute-done | bytes 491552 | tf_op jit(solution)/shard_map/ppermute | solution.py:165
  130.9 7.9 %collective-permute-done.13 = bf16[64,6,640]{2,0,1:T(8,128)(2,1)S(1)} collective-permute-done((bf16[64,6,640]{2,0,1:T(8,128)(2,1)S(1)}, bf16[64,6,640]{2,0,1:T(8,128)(2,1)S(1)}, u32[]{:S(2)}, u32[]{:S(2)}) %collective-permute-start.13) | collective-permute-done | bytes 491552 | tf_op jit(solution)/shard_map/ppermute | solution.py:165
  141.8 1.9 collective-permute-start.16
  145.9 13.8 %all-to-all-start.1 = ((bf16[64,15,128]{2,1,0:T(8,128)(2,1)}), bf16[64,15,128]{2,1,0:T(8,128)(2,1)S(1)}, u32[]{:S(2)}, u32[]{:S(2)}) async-start(bf16[64,15,128]{2,1,0:T(8,128)(2,1)} %reshape.87), calls=%async_computation.1 | async-start | bytes 524288 | tf_op jit(solution)/shard_map/all_to_all | solution.py:183
  159.6 7.6 %collective-permute-done.15 = bf16[64,6,640]{2,0,1:T(8,128)(2,1)} collective-permute-done((bf16[64,6,640]{2,0,1:T(8,128)(2,1)S(1)}, bf16[64,6,640]{2,0,1:T(8,128)(2,1)}, u32[]{:S(2)}, u32[]{:S(2)}) %collective-permute-start.15) | collective-permute-done | bytes 491552 | tf_op jit(solution)/shard_map/ppermute | solution.py:165
  167.3 1.6 fusion.22
  170.4 1.2 all-to-all-done.1
  171.6 8.4 %all-to-all-start.3 = ((bf16[64,30,128]{2,1,0:T(8,128)(2,1)}), bf16[64,30,128]{2,1,0:T(8,128)(2,1)S(1)}, u32[]{:S(2)}, u32[]{:S(2)}) async-start(bf16[64,30,128]{2,1,0:T(8,128)(2,1)} %reshape.91), calls=%async_computation.3 | async-start | bytes 1048576 | tf_op jit(solution)/shard_map/all_to_all | solution.py:183
  181.1 16.2 %all-to-all-done.3 = bf16[64,30,128]{2,1,0:T(8,128)(2,1)S(1)} async-done(((bf16[64,30,128]{2,1,0:T(8,128)(2,1)}), bf16[64,30,128]{2,1,0:T(8,128)(2,1)S(1)}, u32[]{:S(2)}, u32[]{:S(2)}) %all-to-all-start.3) | async-done | bytes 491552 | tf_op jit(solution)/shard_map/all_to_all | solution.py:183
  (89 shorter events, 26.5 us)
Async XLA Ops:
  2.8 13.3 %copy-start.5 = (bf16[640,2560]{1,0:T(8,128)(2,1)S(1)}, bf16[640,2560]{1,0:T(8,128)(2,1)}, u32[]{:S(2)}) copy-start(bf16[640,2560]{1,0:T(8,128)(2,1)} %param.18) | copy-start | bytes 9830404
  16.0 8.1 %copy-start.8 = (s32[64,6]{0,1:T(8,128)S(1)}, s32[64,6]{0,1:T(8,128)}, u32[]{:S(2)}) copy-start(s32[64,6]{0,1:T(8,128)} %param.20) | copy-start | bytes 4612
  19.6 8.1 %collective-permute-start.2 = (f32[64,640]{1,0:T(8,128)S(1)}, f32[64,640]{1,0:T(8,128)S(1)}, u32[]{:S(2)}, u32[]{:S(2)}) collective-permute-start(f32[64,640]{1,0:T(8,128)S(1)} %get-tuple-element.18), channel_id=1, source_target_pairs={{0,3},{1,0},{2,1},{3,2},{4,7},{5,4},{6,5},{7,6},{8,11},{9,8},{10,9... | collective-permute-start | bytes 491528 | tf_op jit(solution)/shard_map/ppermute | solution.py:165
  23.0 6.3 %collective-permute-start.1 = (f32[64,640]{1,0:T(8,128)S(1)}, f32[64,640]{1,0:T(8,128)S(1)}, u32[]{:S(2)}, u32[]{:S(2)}) collective-permute-start(f32[64,640]{1,0:T(8,128)S(1)} %get-tuple-element.19), channel_id=1, source_target_pairs={{0,2},{1,3},{2,0},{3,1},{4,6},{5,7},{6,4},{7,5},{8,10},{9,11},{10,... | collective-permute-start | bytes 491528 | tf_op jit(solution)/shard_map/ppermute | solution.py:165
  23.5 10.6 %collective-permute-start = (f32[64,640]{1,0:T(8,128)S(1)}, f32[64,640]{1,0:T(8,128)S(1)}, u32[]{:S(2)}, u32[]{:S(2)}) collective-permute-start(f32[64,640]{1,0:T(8,128)S(1)} %get-tuple-element.17), channel_id=1, source_target_pairs={{0,1},{1,2},{2,3},{3,0},{4,5},{5,6},{6,7},{7,4},{8,9},{9,10},{10,1... | collective-permute-start | bytes 491528 | tf_op jit(solution)/shard_map/ppermute | solution.py:165
  35.2 2.5 %collective-permute-start.5 = (f32[64,1]{0,1:T(1,128)S(1)}, f32[64,1]{0,1:T(1,128)S(1)}, u32[]{:S(2)}, u32[]{:S(2)}) collective-permute-start(f32[64,1]{0,1:T(1,128)S(1)} %bitcast.139), channel_id=1, source_target_pairs={{0,3},{1,0},{2,1},{3,2},{4,7},{5,4},{6,5},{7,6},{8,11},{9,8},{10,9... | collective-permute-start | bytes 776 | tf_op jit(solution)/shard_map/ppermute | solution.py:165
  35.3 4.0 %collective-permute-start.4 = (f32[64,1]{0,1:T(1,128)S(1)}, f32[64,1]{0,1:T(1,128)S(1)}, u32[]{:S(2)}, u32[]{:S(2)}) collective-permute-start(f32[64,1]{0,1:T(1,128)S(1)} %bitcast.140), channel_id=1, source_target_pairs={{0,2},{1,3},{2,0},{3,1},{4,6},{5,7},{6,4},{7,5},{8,10},{9,11},{10,... | collective-permute-start | bytes 776 | tf_op jit(solution)/shard_map/ppermute | solution.py:165
  35.7 4.4 %collective-permute-start.3 = (f32[64,1]{0,1:T(1,128)S(1)}, f32[64,1]{0,1:T(1,128)S(1)}, u32[]{:S(2)}, u32[]{:S(2)}) collective-permute-start(f32[64,1]{0,1:T(1,128)S(1)} %bitcast.141), channel_id=1, source_target_pairs={{0,1},{1,2},{2,3},{3,0},{4,5},{5,6},{6,7},{7,4},{8,9},{9,10},{10,1... | collective-permute-start | bytes 776 | tf_op jit(solution)/shard_map/ppermute | solution.py:165
  40.8 19.3 %copy-start.3 = (bf16[64,9,640]{2,1,0:T(8,128)(2,1)}, bf16[64,9,640]{2,1,0:T(8,128)(2,1)S(1)}, u32[]{:S(2)}) copy-start(bf16[64,9,640]{2,1,0:T(8,128)(2,1)S(1)} %reshape.83) | copy-start | bytes 2211844
  42.0 26.5 %all-to-all-start = ((bf16[64,15,128]{2,1,0:T(8,128)(2,1)}), bf16[64,15,128]{2,1,0:T(8,128)(2,1)S(1)}, u32[]{:S(2)}, u32[]{:S(2)}) async-start(bf16[64,15,128]{2,1,0:T(8,128)(2,1)} %reshape.84), calls=%async_computation | async-start | bytes 524288 | tf_op jit(solution)/shard_map/all_to_all | solution.py:183
  60.1 5.1 %copy-start.4 = (bf16[64,9,640]{2,1,0:T(8,128)(2,1)S(1)}, bf16[64,9,640]{2,1,0:T(8,128)(2,1)}, u32[]{:S(2)}) copy-start(bf16[64,9,640]{2,1,0:T(8,128)(2,1)} %copy-done.3) | copy-start | bytes 2211844
  68.5 0.7 copy-start.7
  69.2 28.8 %all-to-all-start.2 = ((bf16[64,30,128]{2,1,0:T(8,128)(2,1)}), bf16[64,30,128]{2,1,0:T(8,128)(2,1)}, u32[]{:S(2)}, u32[]{:S(2)}) async-start(bf16[64,30,128]{2,1,0:T(8,128)(2,1)} %reshape.89), calls=%async_computation.2 | async-start | bytes 1048576 | tf_op jit(solution)/shard_map/all_to_all | solution.py:183
  80.8 15.5 %collective-permute-start.8 = (bf16[64,3,640]{2,0,1:T(8,128)(2,1)S(1)}, bf16[64,3,640]{2,0,1:T(8,128)(2,1)S(1)}, u32[]{:S(2)}, u32[]{:S(2)}) collective-permute-start(bf16[64,3,640]{2,0,1:T(8,128)(2,1)S(1)} %copy.75), channel_id=1, source_target_pairs={{0,3},{1,0},{2,1},{3,2},{4,7},{5,4},{6,5},{7,6},{8,11},{9,8},{10,9... | collective-permute-start | bytes 737288 | tf_op jit(solution)/shard_map/ppermute | solution.py:165
  82.6 13.3 %collective-permute-start.6 = (bf16[64,3,640]{2,0,1:T(8,128)(2,1)S(1)}, bf16[64,3,640]{2,0,1:T(8,128)(2,1)S(1)}, u32[]{:S(2)}, u32[]{:S(2)}) collective-permute-start(bf16[64,3,640]{2,0,1:T(8,128)(2,1)S(1)} %copy.75), channel_id=1, source_target_pairs={{0,1},{1,2},{2,3},{3,0},{4,5},{5,6},{6,7},{7,4},{8,9},{9,10},{10,1... | collective-permute-start | bytes 737288 | tf_op jit(solution)/shard_map/ppermute | solution.py:165
  82.6 14.1 %collective-permute-start.7 = (bf16[64,3,640]{2,0,1:T(8,128)(2,1)S(1)}, bf16[64,3,640]{2,0,1:T(8,128)(2,1)S(1)}, u32[]{:S(2)}, u32[]{:S(2)}) collective-permute-start(bf16[64,3,640]{2,0,1:T(8,128)(2,1)S(1)} %copy.75), channel_id=1, source_target_pairs={{0,2},{1,3},{2,0},{3,1},{4,6},{5,7},{6,4},{7,5},{8,10},{9,11},{10,... | collective-permute-start | bytes 737288 | tf_op jit(solution)/shard_map/ppermute | solution.py:165
  83.9 12.4 %copy-start = (bf16[1,640,2,384]{3,2,1,0:T(2,128)(2,1)S(1)}, bf16[1,640,2,384]{3,2,1,0:T(2,128)(2,1)}, u32[]{:S(2)}) copy-start(bf16[1,640,2,384]{3,2,1,0:T(2,128)(2,1)} %get-tuple-element.10) | copy-start | bytes 2949124
  101.4 6.1 %copy-start.2 = (bf16[64,6,640]{2,1,0:T(8,128)(2,1)S(1)}, bf16[64,6,640]{2,1,0:T(8,128)(2,1)}, u32[]{:S(2)}) copy-start(bf16[64,6,640]{2,1,0:T(8,128)(2,1)} %reshape.90) | copy-start | bytes 1474564
  101.4 11.3 %collective-permute-start.14 = (bf16[64,6,640]{2,0,1:T(8,128)(2,1)S(1)}, bf16[64,6,640]{2,0,1:T(8,128)(2,1)S(1)}, u32[]{:S(2)}, u32[]{:S(2)}) collective-permute-start(bf16[64,6,640]{2,0,1:T(8,128)(2,1)S(1)} %copy.84), channel_id=1, source_target_pairs={{0,3},{1,0},{2,1},{3,2},{4,7},{5,4},{6,5},{7,6},{8,11},{9,8},{10,9... | collective-permute-start | bytes 1474568 | tf_op jit(solution)/shard_map/ppermute | solution.py:165
  104.7 9.3 %copy-start.1 = (bf16[1,640,2,384]{3,2,1,0:T(2,128)(2,1)S(1)}, bf16[1,640,2,384]{3,2,1,0:T(2,128)(2,1)}, u32[]{:S(2)}) copy-start(bf16[1,640,2,384]{3,2,1,0:T(2,128)(2,1)} %get-tuple-element.10) | copy-start | bytes 2949124
  104.7 39.1 %collective-permute-start.11 = (bf16[64,3,640]{2,0,1:T(8,128)(2,1)S(1)}, bf16[64,3,640]{2,0,1:T(8,128)(2,1)S(1)}, u32[]{:S(2)}, u32[]{:S(2)}) collective-permute-start(bf16[64,3,640]{2,0,1:T(8,128)(2,1)S(1)} %get-tuple-element.15), channel_id=1, source_target_pairs={{0,3},{1,0},{2,1},{3,2},{4,7},{5,4},{6,5},{7,6},{8,11},{9,8},{10,9... | collective-permute-start | bytes 737288 | tf_op jit(solution)/shard_map/ppermute | solution.py:165
  104.8 39.8 %collective-permute-start.10 = (bf16[64,3,640]{2,0,1:T(8,128)(2,1)S(1)}, bf16[64,3,640]{2,0,1:T(8,128)(2,1)S(1)}, u32[]{:S(2)}, u32[]{:S(2)}) collective-permute-start(bf16[64,3,640]{2,0,1:T(8,128)(2,1)S(1)} %get-tuple-element.16), channel_id=1, source_target_pairs={{0,2},{1,3},{2,0},{3,1},{4,6},{5,7},{6,4},{7,5},{8,10},{9,11},{10,... | collective-permute-start | bytes 737288 | tf_op jit(solution)/shard_map/ppermute | solution.py:165
  107.4 37.2 %collective-permute-start.9 = (bf16[64,3,640]{2,0,1:T(8,128)(2,1)S(1)}, bf16[64,3,640]{2,0,1:T(8,128)(2,1)S(1)}, u32[]{:S(2)}, u32[]{:S(2)}) collective-permute-start(bf16[64,3,640]{2,0,1:T(8,128)(2,1)S(1)} %get-tuple-element.14), channel_id=1, source_target_pairs={{0,1},{1,2},{2,3},{3,0},{4,5},{5,6},{6,7},{7,4},{8,9},{9,10},{10,1... | collective-permute-start | bytes 737288 | tf_op jit(solution)/shard_map/ppermute | solution.py:165
  107.4 22.9 %collective-permute-start.12 = (bf16[64,6,640]{2,0,1:T(8,128)(2,1)S(1)}, bf16[64,6,640]{2,0,1:T(8,128)(2,1)S(1)}, u32[]{:S(2)}, u32[]{:S(2)}) collective-permute-start(bf16[64,6,640]{2,0,1:T(8,128)(2,1)S(1)} %copy.84), channel_id=1, source_target_pairs={{0,1},{1,2},{2,3},{3,0},{4,5},{5,6},{6,7},{7,4},{8,9},{9,10},{10,1... | collective-permute-start | bytes 1474568 | tf_op jit(solution)/shard_map/ppermute | solution.py:165
  112.7 26.1 %collective-permute-start.13 = (bf16[64,6,640]{2,0,1:T(8,128)(2,1)S(1)}, bf16[64,6,640]{2,0,1:T(8,128)(2,1)S(1)}, u32[]{:S(2)}, u32[]{:S(2)}) collective-permute-start(bf16[64,6,640]{2,0,1:T(8,128)(2,1)S(1)} %copy.84), channel_id=1, source_target_pairs={{0,2},{1,3},{2,0},{3,1},{4,6},{5,7},{6,4},{7,5},{8,10},{9,11},{10,... | collective-permute-start | bytes 1474568 | tf_op jit(solution)/shard_map/ppermute | solution.py:165
  130.9 8.5 %copy-start.6 = (bf16[384,4,640]{2,1,0:T(4,128)(2,1)S(1)}, bf16[384,4,640]{2,1,0:T(4,128)(2,1)}, u32[]{:S(2)}) copy-start(bf16[384,4,640]{2,1,0:T(4,128)(2,1)} %reshape_squeeze.3) | copy-start | bytes 5898244
  141.8 17.8 %collective-permute-start.17 = (bf16[64,6,640]{2,0,1:T(8,128)(2,1)}, bf16[64,6,640]{2,0,1:T(8,128)(2,1)}, u32[]{:S(2)}, u32[]{:S(2)}) collective-permute-start(bf16[64,6,640]{2,0,1:T(8,128)(2,1)} %get-tuple-element.12), channel_id=1, source_target_pairs={{0,3},{1,0},{2,1},{3,2},{4,7},{5,4},{6,5},{7,6},{8,11},{9,8},{10,9... | collective-permute-start | bytes 1474568 | tf_op jit(solution)/shard_map/ppermute | solution.py:165
  141.8 17.8 %collective-permute-start.16 = (bf16[64,6,640]{2,0,1:T(8,128)(2,1)}, bf16[64,6,640]{2,0,1:T(8,128)(2,1)}, u32[]{:S(2)}, u32[]{:S(2)}) collective-permute-start(bf16[64,6,640]{2,0,1:T(8,128)(2,1)} %get-tuple-element.13), channel_id=1, source_target_pairs={{0,2},{1,3},{2,0},{3,1},{4,6},{5,7},{6,4},{7,5},{8,10},{9,11},{10,... | collective-permute-start | bytes 1474568 | tf_op jit(solution)/shard_map/ppermute | solution.py:165
  143.7 23.6 %collective-permute-start.15 = (bf16[64,6,640]{2,0,1:T(8,128)(2,1)S(1)}, bf16[64,6,640]{2,0,1:T(8,128)(2,1)}, u32[]{:S(2)}, u32[]{:S(2)}) collective-permute-start(bf16[64,6,640]{2,0,1:T(8,128)(2,1)S(1)} %get-tuple-element.11), channel_id=1, source_target_pairs={{0,1},{1,2},{2,3},{3,0},{4,5},{5,6},{6,7},{7,4},{8,9},{9,10},{10,1... | collective-permute-start | bytes 1474568 | tf_op jit(solution)/shard_map/ppermute | solution.py:165
  145.9 25.7 %all-to-all-start.1 = ((bf16[64,15,128]{2,1,0:T(8,128)(2,1)}), bf16[64,15,128]{2,1,0:T(8,128)(2,1)S(1)}, u32[]{:S(2)}, u32[]{:S(2)}) async-start(bf16[64,15,128]{2,1,0:T(8,128)(2,1)} %reshape.87), calls=%async_computation.1 | async-start | bytes 524288 | tf_op jit(solution)/shard_map/all_to_all | solution.py:183
  168.9 11.2 %copy-start.9 = (f32[64,6]{0,1:T(8,128)S(1)}, f32[64,6]{0,1:T(8,128)}, u32[]{:S(2)}) copy-start(f32[64,6]{0,1:T(8,128)} %param.21) | copy-start | bytes 4612
  171.6 25.7 %all-to-all-start.3 = ((bf16[64,30,128]{2,1,0:T(8,128)(2,1)}), bf16[64,30,128]{2,1,0:T(8,128)(2,1)S(1)}, u32[]{:S(2)}, u32[]{:S(2)}) async-start(bf16[64,30,128]{2,1,0:T(8,128)(2,1)} %reshape.91), calls=%async_computation.3 | async-start | bytes 1048576 | tf_op jit(solution)/shard_map/all_to_all | solution.py:183

commit v2 on v0

--- a/solution.py
+++ b/solution.py
@@ -184,6 +184,36 @@
     return moved.reshape(x.shape)
 
 
+def ring_all_gather_two_step(x, axis_name, size, index):
+    half = x.shape[0] // 2
+    from_left = ring_shift(x, 1, axis_name, size)
+    from_right = ring_shift(x, size - 1, axis_name, size)
+    far = jnp.concatenate(
+        [
+            ring_shift(from_left[:half], 1, axis_name, size),
+            ring_shift(from_right[half:], size - 1, axis_name, size),
+        ],
+        axis=0,
+    )
+    return [x, from_left, far, from_right]
+
+
+def ring_reduce_scatter_two_step(blocks, axis_name, size, index):
+    def block(shift):
+        return lax.dynamic_index_in_dim(blocks, (index + shift) % size, 0, keepdims=False)
+
+    far = block(2)
+    half = far.shape[0] // 2
+    to_left_far = ring_shift(far[:half], 1, axis_name, size)
+    to_right_far = ring_shift(far[half:], size - 1, axis_name, size)
+    from_left = ring_shift(block(1), 1, axis_name, size).astype(jnp.float32)
+    from_right = ring_shift(block(size - 1), size - 1, axis_name, size).astype(jnp.float32)
+    far_first = ring_shift(to_left_far, 1, axis_name, size).astype(jnp.float32)
+    far_second = ring_shift(to_right_far, size - 1, axis_name, size).astype(jnp.float32)
+    total = block(0).astype(jnp.float32) + from_left + from_right
+    return total + jnp.concatenate([far_first, far_second], axis=0)
+
+
 def per_device(
     query,
     new_kv,
@@ -250,7 +280,7 @@
     for lo, hi in zip(bounds[:-1], bounds[1:]):
         slots = hi - lo
         arrived = dense_all_to_all(outgoing[:, lo:hi], "dp")
-        pieces = ring_all_gather(arrived, "tensor", tensor_size)
+        pieces = ring_all_gather_two_step(arrived, "tensor", tensor_size, tensor_index)
         gate_up = None
         for shift, piece in enumerate(pieces):
             weight = lax.dynamic_index_in_dim(
@@ -264,7 +294,9 @@
         partial_out = jnp.einsum(
             "snf,fuc->usnc", activated, split_w2, preferred_element_type=jnp.float32
         ).astype(jnp.bfloat16)
-        expert_sum = ring_reduce_scatter(partial_out, "tensor", tensor_size, tensor_index)
+        expert_sum = ring_reduce_scatter_two_step(
+            partial_out, "tensor", tensor_size, tensor_index
+        )
         expert_sum = expert_sum.astype(jnp.bfloat16)
         returned_rows = dense_all_to_all(expert_sum, "dp")
         part_mix = jnp.dot(

time: 189 us -> 185 us (0.979)
  waiting for transfers between devices: 80.9 us -> 64 us
  starting transfers between devices: 21.5 us -> 34.5 us
  local copies, waits for them, and re-layouts: 20 us -> 18.1 us
    ppermute x12 -> x16, waiting for transfers between devices: 58.1 us -> 41.3 us  [ring_shift(): lax.ppermute(x, axis_name, [(i, (i + shift) % size) for i in range(size)])]
    ppermute x12 -> x16, starting transfers between devices: 15 us -> 25 us  [ring_shift(): lax.ppermute(x, axis_name, [(i, (i + shift) % size) for i in range(size)])]
    all_to_all x1, starting transfers between devices: 6.47 us -> 9.55 us  [dense_all_to_all(): lax.all_to_all(flat, axis_name, split_axis=0, concat_axis=0, tiled=True)]
    another operation x1, local copies, waits for them, and re-layouts: 4.39 us -> 1.98 us  [per_device(): expert_w2[0].reshape(expert_w2.shape[1], tensor_size, share_width)]
    slice x0 -> x3, local copies, waits for them, and re-layouts: none -> 2.11 us  [the longest x1 1.03 us: ring_all_gather_two_step(): from_right[half:]]
  transfers between devices with their start and end apart: 13 -> 17, of which waited for: 8 -> 7; matrix products, arithmetic and copies ran while one was open for 9% -> 7% of each run, Pallas kernels for 0% -> 0%
where the time goes in v2:
time: 185 us; the launch traced here: 183 us
  waiting for transfers between devices  64 us (35%)
  blocking collectives  40.1 us (22%)
  starting transfers between devices  34.5 us (19%)
  local copies, waits for them, and re-layouts  18.1 us (10%)
  Pallas kernels  13.3 us (7%)
  matrix products  10.9 us (6%)
  other arithmetic  1.94 us (1%)
    ppermute x16, waiting for transfers between devices, ring_shift(): lax.ppermute(x, axis_name, [(i, (i + shift) % size) for i in range(size)])  41.3 us
    all_to_all x1, blocking collectives, dense_all_to_all(): lax.all_to_all(flat, axis_name, split_axis=0, concat_axis=0, tiled=True)  40.1 us
    ppermute x16, starting transfers between devices, ring_shift(): lax.ppermute(x, axis_name, [(i, (i + shift) % size) for i in range(size)])  25 us
    all_to_all x1, waiting for transfers between devices, dense_all_to_all(): lax.all_to_all(flat, axis_name, split_axis=0, concat_axis=0, tiled=True)  22.7 us
    pallas_call x1, Pallas kernels, local_attention(): pl.pallas_call(attention_kernel, out_shape=jax.ShapeDtypeStruct(query.sha...  13.3 us
    all_to_all x1, starting transfers between devices, dense_all_to_all(): lax.all_to_all(flat, axis_name, split_axis=0, concat_axis=0, tiled=True)  9.55 us
    dot_general x4, matrix products, per_device(): jnp.einsum('snc,cgf->sngf', piece, weight, preferred_element_type=jnp.flo...  5.84 us
    dynamic_slice x1, local copies, waits for them, and re-layouts, per_device(): lax.dynamic_index_in_dim(split_w1, (tensor_index - shift) % tensor_size,...  4.22 us
  transfers between devices with their start and end apart: 17, of which 7 were waited for; matrix products, arithmetic and copies ran while one was open for 7% of the time, Pallas kernels for 0%

profile of v2, /device:TPU:1, one launch (start us, length us, event | category | flops | bytes accessed | tf_op | source)
XLA Modules:
  0.0 183.2 jit_solution(3702739048080050249)
XLA Ops:
  0.0 1.3 slice_bitcast_fusion.2
  1.3 1.4 copy.52.table_ref
  2.8 13.3 %shard_map.118 = bf16[64,640]{1,0:T(8,128)(2,1)} custom-call(s32[64,32]{1,0:T(8,128)} %copy.52.table_ref, s32[64]{0:T(128)} %len_ref.1, s32[1]{0:T(128)} %bitcast.base_ref, bf16[64,640]{1,0:T(8,128)(2,1)} %q_ref.1, bf16[64,128]{1,0:T(8,128)(2,1)} %get-tuple-element.20.new_k_ref, bf16[64,128]{1,0:T(8,128)(2,1)} %get-tuple-element.19.new_v_ref, ...), custom_call_target="tpu_custom_call" | custom-call | flops 335544320 | bytes 4194304 | tf_op jit(solution)/shard_map/pallas_call | solution.py:144
  16.1 1.6 fusion
  18.5 2.1 %collective-permute-start = (f32[64,640]{1,0:T(8,128)S(1)}, f32[64,640]{1,0:T(8,128)S(1)}, u32[]{:S(2)}, u32[]{:S(2)}) collective-permute-start(f32[64,640]{1,0:T(8,128)S(1)} %get-tuple-element.16), channel_id=1, source_target_pairs={{0,1},{1,2},{2,3},{3,0},{4,5},{5,6},{6,7},{7,4},{8,9},{9,10},{10,1... | collective-permute-start | bytes 491528 | tf_op jit(solution)/shard_map/ppermute | solution.py:165
  20.6 2.5 %collective-permute-start.1 = (f32[64,640]{1,0:T(8,128)S(1)}, f32[64,640]{1,0:T(8,128)S(1)}, u32[]{:S(2)}, u32[]{:S(2)}) collective-permute-start(f32[64,640]{1,0:T(8,128)S(1)} %get-tuple-element.18), channel_id=1, source_target_pairs={{0,2},{1,3},{2,0},{3,1},{4,6},{5,7},{6,4},{7,5},{8,10},{9,11},{10,... | collective-permute-start | bytes 491528 | tf_op jit(solution)/shard_map/ppermute | solution.py:165
  23.1 1.2 collective-permute-start.2
  24.9 2.6 %collective-permute-done.1 = f32[64,640]{1,0:T(8,128)S(1)} collective-permute-done((f32[64,640]{1,0:T(8,128)S(1)}, f32[64,640]{1,0:T(8,128)S(1)}, u32[]{:S(2)}, u32[]{:S(2)}) %collective-permute-start.1) | collective-permute-done | bytes 163872 | tf_op jit(solution)/shard_map/ppermute | solution.py:165
  27.5 1.1 multiply_reduce_fusion
  28.7 1.3 collective-permute-start.3
  30.0 2.0 %collective-permute-start.4 = (f32[64,1]{0,1:T(1,128)S(1)}, f32[64,1]{0,1:T(1,128)S(1)}, u32[]{:S(2)}, u32[]{:S(2)}) collective-permute-start(f32[64,1]{0,1:T(1,128)S(1)} %bitcast.95), channel_id=1, source_target_pairs={{0,2},{1,3},{2,0},{3,1},{4,6},{5,7},{6,4},{7,5},{8,10},{9,11},{10,... | collective-permute-start | bytes 776 | tf_op jit(solution)/shard_map/ppermute | solution.py:165
  32.0 1.5 collective-permute-start.5
  35.6 40.1 %all_to_all.10 = bf16[64,45,128]{2,1,0:T(8,128)(2,1)S(1)} all-to-all(bf16[64,45,128]{2,1,0:T(8,128)(2,1)S(1)} %reshape_reshape.6), channel_id=1, replica_groups=mesh['dp'=64,'tensor'=4] {'dp'}, dimensions={0} | all-to-all | bytes 1474560 | tf_op jit(solution)/shard_map/all_to_all | solution.py:183
  77.5 2.5 %collective-permute-start.8 = (bf16[64,9,640]{2,0,1:T(8,128)(2,1)}, bf16[64,9,640]{2,0,1:T(8,128)(2,1)}, u32[]{:S(2)}, u32[]{:S(2)}) collective-permute-start(bf16[64,9,640]{2,0,1:T(8,128)(2,1)} %copy.58), channel_id=1, source_target_pairs={{0,3},{1,0},{2,1},{3,2},{4,7},{5,4},{6,5},{7,6},{8,11},{9,8},{10,9... | collective-permute-start | bytes 2211848 | tf_op jit(solution)/shard_map/ppermute | solution.py:165
  80.0 2.0 %reshape_squeeze.3 = bf16[384,4,640]{2,1,0:T(4,128)(2,1)} reshape(bf16[1,384,2560]{2,1,0:T(8,128)(2,1)S(1)} %copy-done.2) | data formatting | bytes 3932160 | tf_op jit(solution)/shard_map/reshape;squeeze | solution.py:275
  82.0 4.2 %constant_dynamic-slice_fusion = (bf16[1,640,2,384]{3,2,1,0:T(2,128)(2,1)S(1)}, bf16[1,640,2,384]{3,2,1,0:T(2,128)(2,1)S(1)}, bf16[1,640,2,384]{3,2,1,0:T(2,128)(2,1)S(1)}, bf16[1,640,2,384]{3,2,1,0:T(2,128)(2,1)S(1)}) fusion(bf16[4,640,2,384]{3,2,1,0:T(2,128)(2,1)} %bitcast.92, s32[]{:T(128)S(6)} %select_n.94, s32[]{:T(128)S(6)} %select_n.92, ...), kind=kLoop, calls=%fused_computation.60 | loop fusion | bytes 7864336 | tf_op jit(solution)/shard_map/jit(dynamic_index_in_dim)/dynamic_slice | solution.py:286
  86.2 10.3 %collective-permute-done.6 = bf16[64,9,640]{2,0,1:T(8,128)(2,1)} collective-permute-done((bf16[64,9,640]{2,0,1:T(8,128)(2,1)}, bf16[64,9,640]{2,0,1:T(8,128)(2,1)}, u32[]{:S(2)}, u32[]{:S(2)}) %collective-permute-start.6) | collective-permute-done | bytes 737312 | tf_op jit(solution)/shard_map/ppermute | solution.py:165
  97.6 1.0 slice.41
  98.7 2.7 %collective-permute-start.9 = (bf16[32,9,640]{2,0,1:T(8,128)(2,1)S(1)}, bf16[32,9,640]{2,0,1:T(8,128)(2,1)S(1)}, u32[]{:S(2)}, u32[]{:S(2)}) collective-permute-start(bf16[32,9,640]{2,0,1:T(8,128)(2,1)S(1)} %slice.41), channel_id=1, source_target_pairs={{0,3},{1,0},{2,1},{3,2},{4,7},{5,4},{6,5},{7,6},{8,11},{9,8},{10,9... | collective-permute-start | bytes 1105928 | tf_op jit(solution)/shard_map/ppermute | solution.py:165
  102.2 2.0 %fusion.12 = f32[64,9,2,384]{3,0,2,1:T(8,128)S(1)} fusion(bf16[1,640,2,384]{3,2,1,0:T(2,128)(2,1)S(1)} %get-tuple-element.9, bf16[64,9,640]{2,0,1:T(8,128)(2,1)} %collective-permute-done.6), kind=kOutput, calls=%fused_computation.21 | convolution fusion | flops 566231040 | bytes 3489792 | tf_op jit(solution)/shard_map/snc,cgf->sngf/dot_general | solution.py:289
  104.2 3.5 %collective-permute-done.7 = bf16[32,9,640]{2,0,1:T(8,128)(2,1)S(1)} collective-permute-done((bf16[32,9,640]{2,0,1:T(8,128)(2,1)S(1)}, bf16[32,9,640]{2,0,1:T(8,128)(2,1)S(1)}, u32[]{:S(2)}, u32[]{:S(2)}) %collective-permute-start.7) | collective-permute-done | bytes 368672 | tf_op jit(solution)/shard_map/ppermute | solution.py:165
  108.7 2.1 %add_add_fusion = f32[64,9,2,384]{3,0,2,1:T(8,128)S(1)} fusion(f32[64,9,2,384]{3,0,2,1:T(8,128)S(1)} %fusion.11, f32[64,9,2,384]{3,0,2,1:T(8,128)S(1)} %fusion.13, f32[64,9,2,384]{3,0,2,1:T(8,128)S(1)} %fusion.12, bf16[1,640,2,384]{3,2,1,0:T(2,128)(2,1)S(1)} %get-tuple-element.7, bf16[64,9,640]{2,0,1:T(8,128)(2,1)} %collective-permute-done.8), kind=kOutput, calls=%fused_computation.6 | convolution fusion | flops 567558144 | bytes 8798208 | tf_op jit(solution)/shard_map/snc,cgf->sngf/dot_general | solution.py:289
  110.8 1.7 convolution_convert_fusion
  113.5 3.0 %collective-permute-start.14 = (bf16[32,9,640]{2,0,1:T(8,128)(2,1)S(1)}, bf16[32,9,640]{2,0,1:T(8,128)(2,1)S(1)}, u32[]{:S(2)}, u32[]{:S(2)}) collective-permute-start(bf16[32,9,640]{2,0,1:T(8,128)(2,1)S(1)} %get-tuple-element.15), channel_id=1, source_target_pairs={{0,3},{1,0},{2,1},{3,2},{4,7},{5,4},{6,5},{7,6},{8,11},{9,8},{10,9... | collective-permute-start | bytes 1105928 | tf_op jit(solution)/shard_map/ppermute | solution.py:165
  116.5 2.7 %collective-permute-start.11 = (bf16[64,9,640]{2,0,1:T(8,128)(2,1)S(1)}, bf16[64,9,640]{2,0,1:T(8,128)(2,1)S(1)}, u32[]{:S(2)}, u32[]{:S(2)}) collective-permute-start(bf16[64,9,640]{2,0,1:T(8,128)(2,1)S(1)} %get-tuple-element.12), channel_id=1, source_target_pairs={{0,3},{1,0},{2,1},{3,2},{4,7},{5,4},{6,5},{7,6},{8,11},{9,8},{10,9... | collective-permute-start | bytes 2211848 | tf_op jit(solution)/shard_map/ppermute | solution.py:165
  119.1 3.8 %collective-permute-done.12 = bf16[32,9,640]{2,0,1:T(8,128)(2,1)S(1)} collective-permute-done((bf16[32,9,640]{2,0,1:T(8,128)(2,1)S(1)}, bf16[32,9,640]{2,0,1:T(8,128)(2,1)S(1)}, u32[]{:S(2)}, u32[]{:S(2)}) %collective-permute-start.12) | collective-permute-done | bytes 368672 | tf_op jit(solution)/shard_map/ppermute | solution.py:165
  122.9 2.7 %collective-permute-start.15 = (bf16[32,9,640]{2,0,1:T(8,128)(2,1)S(1)}, bf16[32,9,640]{2,0,1:T(8,128)(2,1)S(1)}, u32[]{:S(2)}, u32[]{:S(2)}) collective-permute-start(bf16[32,9,640]{2,0,1:T(8,128)(2,1)S(1)} %collective-permute-done.14), channel_id=1, source_target_pairs={{0,3},{1,0},{2,1},{3,2},{4,7},{5,4},{6,5},{7,6},{8,11},{9,8},{10,9... | collective-permute-start | bytes 1105928 | tf_op jit(solution)/shard_map/ppermute | solution.py:165
  125.6 21.0 %collective-permute-done.13 = bf16[32,9,640]{2,0,1:T(8,128)(2,1)S(1)} collective-permute-done((bf16[32,9,640]{2,0,1:T(8,128)(2,1)S(1)}, bf16[32,9,640]{2,0,1:T(8,128)(2,1)S(1)}, u32[]{:S(2)}, u32[]{:S(2)}) %collective-permute-start.13) | collective-permute-done | bytes 368672 | tf_op jit(solution)/shard_map/ppermute | solution.py:165
  147.6 1.4 reshape.48
  148.9 9.6 %all-to-all-start.1 = ((bf16[64,45,128]{2,1,0:T(8,128)(2,1)}), bf16[64,45,128]{2,1,0:T(8,128)(2,1)S(1)}, u32[]{:S(2)}, u32[]{:S(2)}) async-start(bf16[64,45,128]{2,1,0:T(8,128)(2,1)} %reshape.48), calls=%async_computation.1 | async-start | bytes 1572864 | tf_op jit(solution)/shard_map/all_to_all | solution.py:183
  158.7 22.7 %all-to-all-done.1 = bf16[64,45,128]{2,1,0:T(8,128)(2,1)S(1)} async-done(((bf16[64,45,128]{2,1,0:T(8,128)(2,1)}), bf16[64,45,128]{2,1,0:T(8,128)(2,1)S(1)}, u32[]{:S(2)}, u32[]{:S(2)}) %all-to-all-start.1) | async-done | bytes 737312 | tf_op jit(solution)/shard_map/all_to_all | solution.py:183
  182.1 1.1 fusion.8
  (52 shorter events, 10.8 us)
Async XLA Ops:
  2.8 13.3 %copy-start = (bf16[640,2560]{1,0:T(8,128)(2,1)S(1)}, bf16[640,2560]{1,0:T(8,128)(2,1)}, u32[]{:S(2)}) copy-start(bf16[640,2560]{1,0:T(8,128)(2,1)} %param.18) | copy-start | bytes 9830404
  16.0 8.2 %copy-start.4 = (s32[64,6]{0,1:T(8,128)S(1)}, s32[64,6]{0,1:T(8,128)}, u32[]{:S(2)}) copy-start(s32[64,6]{0,1:T(8,128)} %param.20) | copy-start | bytes 4612
  17.6 0.8 copy-start.1
  18.5 6.4 %collective-permute-start = (f32[64,640]{1,0:T(8,128)S(1)}, f32[64,640]{1,0:T(8,128)S(1)}, u32[]{:S(2)}, u32[]{:S(2)}) collective-permute-start(f32[64,640]{1,0:T(8,128)S(1)} %get-tuple-element.16), channel_id=1, source_target_pairs={{0,1},{1,2},{2,3},{3,0},{4,5},{5,6},{6,7},{7,4},{8,9},{9,10},{10,1... | collective-permute-start | bytes 491528 | tf_op jit(solution)/shard_map/ppermute | solution.py:165
  20.6 6.9 %collective-permute-start.1 = (f32[64,640]{1,0:T(8,128)S(1)}, f32[64,640]{1,0:T(8,128)S(1)}, u32[]{:S(2)}, u32[]{:S(2)}) collective-permute-start(f32[64,640]{1,0:T(8,128)S(1)} %get-tuple-element.18), channel_id=1, source_target_pairs={{0,2},{1,3},{2,0},{3,1},{4,6},{5,7},{6,4},{7,5},{8,10},{9,11},{10,... | collective-permute-start | bytes 491528 | tf_op jit(solution)/shard_map/ppermute | solution.py:165
  23.1 4.5 %collective-permute-start.2 = (f32[64,640]{1,0:T(8,128)S(1)}, f32[64,640]{1,0:T(8,128)S(1)}, u32[]{:S(2)}, u32[]{:S(2)}) collective-permute-start(f32[64,640]{1,0:T(8,128)S(1)} %get-tuple-element.17), channel_id=1, source_target_pairs={{0,3},{1,0},{2,1},{3,2},{4,7},{5,4},{6,5},{7,6},{8,11},{9,8},{10,9... | collective-permute-start | bytes 491528 | tf_op jit(solution)/shard_map/ppermute | solution.py:165
  28.7 5.8 %collective-permute-start.3 = (f32[64,1]{0,1:T(1,128)S(1)}, f32[64,1]{0,1:T(1,128)S(1)}, u32[]{:S(2)}, u32[]{:S(2)}) collective-permute-start(f32[64,1]{0,1:T(1,128)S(1)} %bitcast.94), channel_id=1, source_target_pairs={{0,1},{1,2},{2,3},{3,0},{4,5},{5,6},{6,7},{7,4},{8,9},{9,10},{10,1... | collective-permute-start | bytes 776 | tf_op jit(solution)/shard_map/ppermute | solution.py:165
  30.0 4.5 %collective-permute-start.4 = (f32[64,1]{0,1:T(1,128)S(1)}, f32[64,1]{0,1:T(1,128)S(1)}, u32[]{:S(2)}, u32[]{:S(2)}) collective-permute-start(f32[64,1]{0,1:T(1,128)S(1)} %bitcast.95), channel_id=1, source_target_pairs={{0,2},{1,3},{2,0},{3,1},{4,6},{5,7},{6,4},{7,5},{8,10},{9,11},{10,... | collective-permute-start | bytes 776 | tf_op jit(solution)/shard_map/ppermute | solution.py:165
  32.0 2.5 %collective-permute-start.5 = (f32[64,1]{0,1:T(1,128)S(1)}, f32[64,1]{0,1:T(1,128)S(1)}, u32[]{:S(2)}, u32[]{:S(2)}) collective-permute-start(f32[64,1]{0,1:T(1,128)S(1)} %bitcast.96), channel_id=1, source_target_pairs={{0,3},{1,0},{2,1},{3,2},{4,7},{5,4},{6,5},{7,6},{8,11},{9,8},{10,9... | collective-permute-start | bytes 776 | tf_op jit(solution)/shard_map/ppermute | solution.py:165
  76.3 3.7 %copy-start.2 = (bf16[1,384,2560]{2,1,0:T(8,128)(2,1)S(1)}, bf16[1,384,2560]{2,1,0:T(8,128)(2,1)}, u32[]{:S(2)}) copy-start(bf16[1,384,2560]{2,1,0:T(8,128)(2,1)} %param.23) | copy-start | bytes 5898244
  77.3 19.2 %collective-permute-start.6 = (bf16[64,9,640]{2,0,1:T(8,128)(2,1)}, bf16[64,9,640]{2,0,1:T(8,128)(2,1)}, u32[]{:S(2)}, u32[]{:S(2)}) collective-permute-start(bf16[64,9,640]{2,0,1:T(8,128)(2,1)} %copy.58), channel_id=1, source_target_pairs={{0,1},{1,2},{2,3},{3,0},{4,5},{5,6},{6,7},{7,4},{8,9},{9,10},{10,1... | collective-permute-start | bytes 2211848 | tf_op jit(solution)/shard_map/ppermute | solution.py:165
  77.5 20.2 %collective-permute-start.8 = (bf16[64,9,640]{2,0,1:T(8,128)(2,1)}, bf16[64,9,640]{2,0,1:T(8,128)(2,1)}, u32[]{:S(2)}, u32[]{:S(2)}) collective-permute-start(bf16[64,9,640]{2,0,1:T(8,128)(2,1)} %copy.58), channel_id=1, source_target_pairs={{0,3},{1,0},{2,1},{3,2},{4,7},{5,4},{6,5},{7,6},{8,11},{9,8},{10,9... | collective-permute-start | bytes 2211848 | tf_op jit(solution)/shard_map/ppermute | solution.py:165
  97.5 10.2 %collective-permute-start.7 = (bf16[32,9,640]{2,0,1:T(8,128)(2,1)S(1)}, bf16[32,9,640]{2,0,1:T(8,128)(2,1)S(1)}, u32[]{:S(2)}, u32[]{:S(2)}) collective-permute-start(bf16[32,9,640]{2,0,1:T(8,128)(2,1)S(1)} %slice.40), channel_id=1, source_target_pairs={{0,1},{1,2},{2,3},{3,0},{4,5},{5,6},{6,7},{7,4},{8,9},{9,10},{10,1... | collective-permute-start | bytes 1105928 | tf_op jit(solution)/shard_map/ppermute | solution.py:165
  98.7 9.1 %collective-permute-start.9 = (bf16[32,9,640]{2,0,1:T(8,128)(2,1)S(1)}, bf16[32,9,640]{2,0,1:T(8,128)(2,1)S(1)}, u32[]{:S(2)}, u32[]{:S(2)}) collective-permute-start(bf16[32,9,640]{2,0,1:T(8,128)(2,1)S(1)} %slice.41), channel_id=1, source_target_pairs={{0,3},{1,0},{2,1},{3,2},{4,7},{5,4},{6,5},{7,6},{8,11},{9,8},{10,9... | collective-permute-start | bytes 1105928 | tf_op jit(solution)/shard_map/ppermute | solution.py:165
  108.7 2.2 %copy-start.3 = (bf16[384,4,640]{2,1,0:T(4,128)(2,1)S(1)}, bf16[384,4,640]{2,1,0:T(4,128)(2,1)}, u32[]{:S(2)}) copy-start(bf16[384,4,640]{2,1,0:T(4,128)(2,1)} %reshape_squeeze.3) | copy-start | bytes 5898244
  112.9 10.1 %collective-permute-start.12 = (bf16[32,9,640]{2,0,1:T(8,128)(2,1)S(1)}, bf16[32,9,640]{2,0,1:T(8,128)(2,1)S(1)}, u32[]{:S(2)}, u32[]{:S(2)}) collective-permute-start(bf16[32,9,640]{2,0,1:T(8,128)(2,1)S(1)} %get-tuple-element.14), channel_id=1, source_target_pairs={{0,1},{1,2},{2,3},{3,0},{4,5},{5,6},{6,7},{7,4},{8,9},{9,10},{10,1... | collective-permute-start | bytes 1105928 | tf_op jit(solution)/shard_map/ppermute | solution.py:165
  113.5 9.5 %collective-permute-start.14 = (bf16[32,9,640]{2,0,1:T(8,128)(2,1)S(1)}, bf16[32,9,640]{2,0,1:T(8,128)(2,1)S(1)}, u32[]{:S(2)}, u32[]{:S(2)}) collective-permute-start(bf16[32,9,640]{2,0,1:T(8,128)(2,1)S(1)} %get-tuple-element.15), channel_id=1, source_target_pairs={{0,3},{1,0},{2,1},{3,2},{4,7},{5,4},{6,5},{7,6},{8,11},{9,8},{10,9... | collective-permute-start | bytes 1105928 | tf_op jit(solution)/shard_map/ppermute | solution.py:165
  116.5 30.2 %collective-permute-start.10 = (bf16[64,9,640]{2,0,1:T(8,128)(2,1)S(1)}, bf16[64,9,640]{2,0,1:T(8,128)(2,1)S(1)}, u32[]{:S(2)}, u32[]{:S(2)}) collective-permute-start(bf16[64,9,640]{2,0,1:T(8,128)(2,1)S(1)} %get-tuple-element.13), channel_id=1, source_target_pairs={{0,1},{1,2},{2,3},{3,0},{4,5},{5,6},{6,7},{7,4},{8,9},{9,10},{10,1... | collective-permute-start | bytes 2211848 | tf_op jit(solution)/shard_map/ppermute | solution.py:165
  116.5 30.2 %collective-permute-start.11 = (bf16[64,9,640]{2,0,1:T(8,128)(2,1)S(1)}, bf16[64,9,640]{2,0,1:T(8,128)(2,1)S(1)}, u32[]{:S(2)}, u32[]{:S(2)}) collective-permute-start(bf16[64,9,640]{2,0,1:T(8,128)(2,1)S(1)} %get-tuple-element.12), channel_id=1, source_target_pairs={{0,3},{1,0},{2,1},{3,2},{4,7},{5,4},{6,5},{7,6},{8,11},{9,8},{10,9... | collective-permute-start | bytes 2211848 | tf_op jit(solution)/shard_map/ppermute | solution.py:165
  122.9 23.7 %collective-permute-start.13 = (bf16[32,9,640]{2,0,1:T(8,128)(2,1)S(1)}, bf16[32,9,640]{2,0,1:T(8,128)(2,1)S(1)}, u32[]{:S(2)}, u32[]{:S(2)}) collective-permute-start(bf16[32,9,640]{2,0,1:T(8,128)(2,1)S(1)} %collective-permute-done.12), channel_id=1, source_target_pairs={{0,1},{1,2},{2,3},{3,0},{4,5},{5,6},{6,7},{7,4},{8,9},{9,10},{10,1... | collective-permute-start | bytes 1105928 | tf_op jit(solution)/shard_map/ppermute | solution.py:165
  122.9 23.7 %collective-permute-start.15 = (bf16[32,9,640]{2,0,1:T(8,128)(2,1)S(1)}, bf16[32,9,640]{2,0,1:T(8,128)(2,1)S(1)}, u32[]{:S(2)}, u32[]{:S(2)}) collective-permute-start(bf16[32,9,640]{2,0,1:T(8,128)(2,1)S(1)} %collective-permute-done.14), channel_id=1, source_target_pairs={{0,3},{1,0},{2,1},{3,2},{4,7},{5,4},{6,5},{7,6},{8,11},{9,8},{10,9... | collective-permute-start | bytes 1105928 | tf_op jit(solution)/shard_map/ppermute | solution.py:165
  147.5 11.0 %copy-start.5 = (f32[64,6]{0,1:T(8,128)S(1)}, f32[64,6]{0,1:T(8,128)}, u32[]{:S(2)}) copy-start(f32[64,6]{0,1:T(8,128)} %param.21) | copy-start | bytes 4612
  148.9 32.5 %all-to-all-start.1 = ((bf16[64,45,128]{2,1,0:T(8,128)(2,1)}), bf16[64,45,128]{2,1,0:T(8,128)(2,1)S(1)}, u32[]{:S(2)}, u32[]{:S(2)}) async-start(bf16[64,45,128]{2,1,0:T(8,128)(2,1)} %reshape.48), calls=%async_computation.1 | async-start | bytes 1572864 | tf_op jit(solution)/shard_map/all_to_all | solution.py:183

commit v3 on v2

--- a/solution.py
+++ b/solution.py
@@ -294,17 +294,18 @@
         partial_out = jnp.einsum(
             "snf,fuc->usnc", activated, split_w2, preferred_element_type=jnp.float32
         ).astype(jnp.bfloat16)
-        expert_sum = ring_reduce_scatter_two_step(
-            partial_out, "tensor", tensor_size, tensor_index
-        )
-        expert_sum = expert_sum.astype(jnp.bfloat16)
-        returned_rows = dense_all_to_all(expert_sum, "dp")
-        part_mix = jnp.dot(
-            mixing[:, :, lo:hi].reshape(row_count, experts * slots),
-            returned_rows.reshape(experts * slots, share_width).astype(jnp.float32),
-            precision=lax.Precision.HIGHEST,
-        )
-        expert_mix = part_mix if expert_mix is None else expert_mix + part_mix
+        for first, last in ((0, capacity // 3), (capacity // 3, capacity)):
+            expert_sum = ring_reduce_scatter_two_step(
+                partial_out[:, :, first:last], "tensor", tensor_size, tensor_index
+            )
+            expert_sum = expert_sum.astype(jnp.bfloat16)
+            returned_rows = dense_all_to_all(expert_sum, "dp")
+            part_mix = jnp.dot(
+                mixing[:, :, lo + first:lo + last].reshape(row_count, experts * (last - first)),
+                returned_rows.reshape(experts * (last - first), share_width).astype(jnp.float32),
+                precision=lax.Precision.HIGHEST,
+            )
+            expert_mix = part_mix if expert_mix is None else expert_mix + part_mix
     return (state + expert_mix).astype(jnp.bfloat16)
 
 

time: 185 us -> 188 us (1.016); the launches traced: 183 us -> 188 us
  starting transfers between devices: 34.5 us -> 47.8 us
  waiting for transfers between devices: 64 us -> 52.6 us
  local copies, waits for them, and re-layouts: 18.1 us -> 20.3 us
    ppermute x16 -> x22, waiting for transfers between devices: 41.3 us -> 27.5 us  [ring_shift(): lax.ppermute(x, axis_name, [(i, (i + shift) % size) for i in range(size)])]
    all_to_all x1 -> x2, starting transfers between devices: 9.55 us -> 18.9 us  [dense_all_to_all(): lax.all_to_all(flat, axis_name, split_axis=0, concat_axis=0, tiled=True)]
    ppermute x16 -> x22, starting transfers between devices: 25 us -> 28.9 us  [ring_shift(): lax.ppermute(x, axis_name, [(i, (i + shift) % size) for i in range(size)])]
    all_to_all x1 -> x2, waiting for transfers between devices: 22.7 us -> 25 us  [dense_all_to_all(): lax.all_to_all(flat, axis_name, split_axis=0, concat_axis=0, tiled=True)]
  transfers between devices with their start and end apart: 17 -> 24, of which waited for: 7 -> 9; matrix products, arithmetic and copies ran while one was open for 7% -> 10% of each run, Pallas kernels for 0% -> 0%
where the time goes in v3:
time: 188 us
  waiting for transfers between devices  52.6 us (28%)
  starting transfers between devices  47.8 us (25%)
  blocking collectives  39.5 us (21%)
  local copies, waits for them, and re-layouts  20.3 us (11%)
  Pallas kernels  13.3 us (7%)
  matrix products  11.2 us (6%)
  other arithmetic  3.2 us (2%)
    all_to_all x1, blocking collectives, dense_all_to_all(): lax.all_to_all(flat, axis_name, split_axis=0, concat_axis=0, tiled=True)  39.5 us
    ppermute x22, starting transfers between devices, ring_shift(): lax.ppermute(x, axis_name, [(i, (i + shift) % size) for i in range(size)])  28.9 us
    ppermute x22, waiting for transfers between devices, ring_shift(): lax.ppermute(x, axis_name, [(i, (i + shift) % size) for i in range(size)])  27.5 us
    all_to_all x2, waiting for transfers between devices, dense_all_to_all(): lax.all_to_all(flat, axis_name, split_axis=0, concat_axis=0, tiled=True)  25 us
    all_to_all x2, starting transfers between devices, dense_all_to_all(): lax.all_to_all(flat, axis_name, split_axis=0, concat_axis=0, tiled=True)  18.9 us
    pallas_call x1, Pallas kernels, local_attention(): pl.pallas_call(attention_kernel, out_shape=jax.ShapeDtypeStruct(query.sha...  13.3 us
    dot_general x4, matrix products, per_device(): jnp.einsum('snc,cgf->sngf', piece, weight, preferred_element_type=jnp.flo...  5.84 us
    dynamic_slice x1, local copies, waits for them, and re-layouts, per_device(): lax.dynamic_index_in_dim(split_w1, (tensor_index - shift) % tensor_size,...  4.22 us
  transfers between devices with their start and end apart: 24, of which 9 were waited for; matrix products, arithmetic and copies ran while one was open for 10% of the time, Pallas kernels for 0%

profile of v3, /device:TPU:1, one launch (start us, length us, event | category | flops | bytes accessed | tf_op | source)
XLA Modules:
  0.0 188.3 jit_solution(7298953384858788185)
XLA Ops:
  0.0 1.3 slice_bitcast_fusion.2
  1.3 1.4 copy.67.table_ref
  2.8 13.3 %shard_map.118 = bf16[64,640]{1,0:T(8,128)(2,1)} custom-call(s32[64,32]{1,0:T(8,128)} %copy.67.table_ref, s32[64]{0:T(128)} %len_ref.1, s32[1]{0:T(128)} %bitcast.base_ref, bf16[64,640]{1,0:T(8,128)(2,1)} %q_ref.1, bf16[64,128]{1,0:T(8,128)(2,1)} %get-tuple-element.21.new_k_ref, bf16[64,128]{1,0:T(8,128)(2,1)} %get-tuple-element.20.new_v_ref, ...), custom_call_target="tpu_custom_call" | custom-call | flops 335544320 | bytes 4194304 | tf_op jit(solution)/shard_map/pallas_call | solution.py:144
  16.0 1.6 fusion
  18.5 2.1 %collective-permute-start = (f32[64,640]{1,0:T(8,128)S(1)}, f32[64,640]{1,0:T(8,128)S(1)}, u32[]{:S(2)}, u32[]{:S(2)}) collective-permute-start(f32[64,640]{1,0:T(8,128)S(1)} %get-tuple-element.17), channel_id=1, source_target_pairs={{0,1},{1,2},{2,3},{3,0},{4,5},{5,6},{6,7},{7,4},{8,9},{9,10},{10,1... | collective-permute-start | bytes 491528 | tf_op jit(solution)/shard_map/ppermute | solution.py:165
  20.6 2.5 %collective-permute-start.1 = (f32[64,640]{1,0:T(8,128)S(1)}, f32[64,640]{1,0:T(8,128)S(1)}, u32[]{:S(2)}, u32[]{:S(2)}) collective-permute-start(f32[64,640]{1,0:T(8,128)S(1)} %get-tuple-element.19), channel_id=1, source_target_pairs={{0,2},{1,3},{2,0},{3,1},{4,6},{5,7},{6,4},{7,5},{8,10},{9,11},{10,... | collective-permute-start | bytes 491528 | tf_op jit(solution)/shard_map/ppermute | solution.py:165
  23.1 1.2 collective-permute-start.2
  24.9 5.3 %collective-permute-done.1 = f32[64,640]{1,0:T(8,128)S(1)} collective-permute-done((f32[64,640]{1,0:T(8,128)S(1)}, f32[64,640]{1,0:T(8,128)S(1)}, u32[]{:S(2)}, u32[]{:S(2)}) %collective-permute-start.1) | collective-permute-done | bytes 163872 | tf_op jit(solution)/shard_map/ppermute | solution.py:165
  32.4 1.9 %collective-permute-start.4 = (f32[64,1]{0,1:T(1,128)S(1)}, f32[64,1]{0,1:T(1,128)S(1)}, u32[]{:S(2)}, u32[]{:S(2)}) collective-permute-start(f32[64,1]{0,1:T(1,128)S(1)} %bitcast.122), channel_id=1, source_target_pairs={{0,2},{1,3},{2,0},{3,1},{4,6},{5,7},{6,4},{7,5},{8,10},{9,11},{10,... | collective-permute-start | bytes 776 | tf_op jit(solution)/shard_map/ppermute | solution.py:165
  34.3 1.3 collective-permute-start.5
  37.8 39.5 %all_to_all.15 = bf16[64,45,128]{2,1,0:T(8,128)(2,1)S(1)} all-to-all(bf16[64,45,128]{2,1,0:T(8,128)(2,1)S(1)} %reshape_reshape.9), channel_id=1, replica_groups=mesh['dp'=64,'tensor'=4] {'dp'}, dimensions={0} | all-to-all | bytes 1474560 | tf_op jit(solution)/shard_map/all_to_all | solution.py:183
  79.1 2.5 %collective-permute-start.8 = (bf16[64,9,640]{2,0,1:T(8,128)(2,1)}, bf16[64,9,640]{2,0,1:T(8,128)(2,1)}, u32[]{:S(2)}, u32[]{:S(2)}) collective-permute-start(bf16[64,9,640]{2,0,1:T(8,128)(2,1)} %copy.74), channel_id=1, source_target_pairs={{0,3},{1,0},{2,1},{3,2},{4,7},{5,4},{6,5},{7,6},{8,11},{9,8},{10,9... | collective-permute-start | bytes 2211848 | tf_op jit(solution)/shard_map/ppermute | solution.py:165
  81.7 2.0 %reshape_squeeze.3 = bf16[384,4,640]{2,1,0:T(4,128)(2,1)} reshape(bf16[1,384,2560]{2,1,0:T(8,128)(2,1)S(1)} %copy-done.2) | data formatting | bytes 3932160 | tf_op jit(solution)/shard_map/reshape;squeeze | solution.py:275
  83.7 4.2 %constant_dynamic-slice_fusion = (bf16[1,640,2,384]{3,2,1,0:T(2,128)(2,1)S(1)}, bf16[1,640,2,384]{3,2,1,0:T(2,128)(2,1)S(1)}, bf16[1,640,2,384]{3,2,1,0:T(2,128)(2,1)S(1)}, bf16[1,640,2,384]{3,2,1,0:T(2,128)(2,1)S(1)}) fusion(bf16[4,640,2,384]{3,2,1,0:T(2,128)(2,1)} %bitcast.119, s32[]{:T(128)S(6)} %select_n.107, s32[]{:T(128)S(6)} %select_n.105, ...), kind=kLoop, calls=%fused_computation.69 | loop fusion | bytes 7864336 | tf_op jit(solution)/shard_map/jit(dynamic_index_in_dim)/dynamic_slice | solution.py:286
  87.9 10.3 %collective-permute-done.6 = bf16[64,9,640]{2,0,1:T(8,128)(2,1)} collective-permute-done((bf16[64,9,640]{2,0,1:T(8,128)(2,1)}, bf16[64,9,640]{2,0,1:T(8,128)(2,1)}, u32[]{:S(2)}, u32[]{:S(2)}) %collective-permute-start.6) | collective-permute-done | bytes 737312 | tf_op jit(solution)/shard_map/ppermute | solution.py:165
  100.3 2.7 %collective-permute-start.9 = (bf16[32,9,640]{2,0,1:T(8,128)(2,1)S(1)}, bf16[32,9,640]{2,0,1:T(8,128)(2,1)S(1)}, u32[]{:S(2)}, u32[]{:S(2)}) collective-permute-start(bf16[32,9,640]{2,0,1:T(8,128)(2,1)S(1)} %slice.74), channel_id=1, source_target_pairs={{0,3},{1,0},{2,1},{3,2},{4,7},{5,4},{6,5},{7,6},{8,11},{9,8},{10,9... | collective-permute-start | bytes 1105928 | tf_op jit(solution)/shard_map/ppermute | solution.py:165
  103.9 2.0 %fusion.10 = f32[64,9,2,384]{3,0,2,1:T(8,128)S(1)} fusion(bf16[1,640,2,384]{3,2,1,0:T(2,128)(2,1)S(1)} %get-tuple-element.9, bf16[64,9,640]{2,0,1:T(8,128)(2,1)} %collective-permute-done.6), kind=kOutput, calls=%fused_computation.18 | convolution fusion | flops 566231040 | bytes 3489792 | tf_op jit(solution)/shard_map/snc,cgf->sngf/dot_general | solution.py:289
  105.9 3.5 %collective-permute-done.7 = bf16[32,9,640]{2,0,1:T(8,128)(2,1)S(1)} collective-permute-done((bf16[32,9,640]{2,0,1:T(8,128)(2,1)S(1)}, bf16[32,9,640]{2,0,1:T(8,128)(2,1)S(1)}, u32[]{:S(2)}, u32[]{:S(2)}) %collective-permute-start.7) | collective-permute-done | bytes 368672 | tf_op jit(solution)/shard_map/ppermute | solution.py:165
  110.3 2.1 %add_add_fusion = f32[64,9,2,384]{3,0,2,1:T(8,128)S(1)} fusion(f32[64,9,2,384]{3,0,2,1:T(8,128)S(1)} %fusion.9, f32[64,9,2,384]{3,0,2,1:T(8,128)S(1)} %fusion.11, f32[64,9,2,384]{3,0,2,1:T(8,128)S(1)} %fusion.10, bf16[1,640,2,384]{3,2,1,0:T(2,128)(2,1)S(1)} %get-tuple-element.7, bf16[64,9,640]{2,0,1:T(8,128)(2,1)} %collective-permute-done.8), kind=kOutput, calls=%fused_computation.6 | convolution fusion | flops 567558144 | bytes 8798208 | tf_op jit(solution)/shard_map/snc,cgf->sngf/dot_general | solution.py:289
  112.5 1.7 convert_bitcast_fusion
  116.1 3.0 %collective-permute-start.20 = (bf16[32,6,640]{2,0,1:T(8,128)(2,1)S(1)}, bf16[32,6,640]{2,0,1:T(8,128)(2,1)}, u32[]{:S(2)}, u32[]{:S(2)}) collective-permute-start(bf16[32,6,640]{2,0,1:T(8,128)(2,1)S(1)} %dynamic-slice_bitcast_fusion.3), channel_id=1, source_target_pairs={{0,3},{1,0},{2,1},{3,2},{4,7},{5,4},{6,5},{7,6},{8,11},{9,8},{10,9... | collective-permute-start | bytes 737288 | tf_op jit(solution)/shard_map/ppermute | solution.py:165
  119.3 2.7 %collective-permute-start.14 = (bf16[32,3,640]{2,0,1:T(8,128)(2,1)S(1)}, bf16[32,3,640]{2,0,1:T(8,128)(2,1)S(1)}, u32[]{:S(2)}, u32[]{:S(2)}) collective-permute-start(bf16[32,3,640]{2,0,1:T(8,128)(2,1)S(1)} %dynamic-slice_bitcast_fusion.10), channel_id=1, source_target_pairs={{0,3},{1,0},{2,1},{3,2},{4,7},{5,4},{6,5},{7,6},{8,11},{9,8},{10,9... | collective-permute-start | bytes 368648 | tf_op jit(solution)/shard_map/ppermute | solution.py:165
  122.1 3.9 %collective-permute-done.12 = bf16[32,3,640]{2,0,1:T(8,128)(2,1)S(1)} collective-permute-done((bf16[32,3,640]{2,0,1:T(8,128)(2,1)S(1)}, bf16[32,3,640]{2,0,1:T(8,128)(2,1)S(1)}, u32[]{:S(2)}, u32[]{:S(2)}) %collective-permute-start.12) | collective-permute-done | bytes 122912 | tf_op jit(solution)/shard_map/ppermute | solution.py:165
  127.4 2.1 %collective-permute-start.15 = (bf16[32,3,640]{2,0,1:T(8,128)(2,1)S(1)}, bf16[32,3,640]{2,0,1:T(8,128)(2,1)S(1)}, u32[]{:S(2)}, u32[]{:S(2)}) collective-permute-start(bf16[32,3,640]{2,0,1:T(8,128)(2,1)S(1)} %collective-permute-done.14), channel_id=1, source_target_pairs={{0,3},{1,0},{2,1},{3,2},{4,7},{5,4},{6,5},{7,6},{8,11},{9,8},{10,9... | collective-permute-start | bytes 368648 | tf_op jit(solution)/shard_map/ppermute | solution.py:165
  129.6 4.3 %collective-permute-done.13 = bf16[32,3,640]{2,0,1:T(8,128)(2,1)S(1)} collective-permute-done((bf16[32,3,640]{2,0,1:T(8,128)(2,1)S(1)}, bf16[32,3,640]{2,0,1:T(8,128)(2,1)S(1)}, u32[]{:S(2)}, u32[]{:S(2)}) %collective-permute-start.13) | collective-permute-done | bytes 122912 | tf_op jit(solution)/shard_map/ppermute | solution.py:165
  135.4 2.0 %collective-permute-start.21 = (bf16[32,6,640]{2,0,1:T(8,128)(2,1)}, bf16[32,6,640]{2,0,1:T(8,128)(2,1)S(1)}, u32[]{:S(2)}, u32[]{:S(2)}) collective-permute-start(bf16[32,6,640]{2,0,1:T(8,128)(2,1)} %collective-permute-done.20), channel_id=1, source_target_pairs={{0,3},{1,0},{2,1},{3,2},{4,7},{5,4},{6,5},{7,6},{8,11},{9,8},{10,9... | collective-permute-start | bytes 737288 | tf_op jit(solution)/shard_map/ppermute | solution.py:165
  138.6 12.9 %all-to-all-start.1 = ((bf16[64,15,128]{2,1,0:T(8,128)(2,1)}), bf16[64,15,128]{2,1,0:T(8,128)(2,1)S(1)}, u32[]{:S(2)}, u32[]{:S(2)}) async-start(bf16[64,15,128]{2,1,0:T(8,128)(2,1)} %reshape.58), calls=%async_computation.1 | async-start | bytes 524288 | tf_op jit(solution)/shard_map/all_to_all | solution.py:183
  151.6 1.6 fusion.14
  153.4 1.2 reshape.60
  154.6 8.9 %all-to-all-done.1 = bf16[64,15,128]{2,1,0:T(8,128)(2,1)S(1)} async-done(((bf16[64,15,128]{2,1,0:T(8,128)(2,1)}), bf16[64,15,128]{2,1,0:T(8,128)(2,1)S(1)}, u32[]{:S(2)}, u32[]{:S(2)}) %all-to-all-start.1) | async-done | bytes 245792 | tf_op jit(solution)/shard_map/all_to_all | solution.py:183
  163.5 6.0 %all-to-all-start.2 = ((bf16[64,30,128]{2,1,0:T(8,128)(2,1)}), bf16[64,30,128]{2,1,0:T(8,128)(2,1)S(1)}, u32[]{:S(2)}, u32[]{:S(2)}) async-start(bf16[64,30,128]{2,1,0:T(8,128)(2,1)} %reshape.60), calls=%async_computation.2 | async-start | bytes 1048576 | tf_op jit(solution)/shard_map/all_to_all | solution.py:183
  170.7 16.2 %all-to-all-done.2 = bf16[64,30,128]{2,1,0:T(8,128)(2,1)S(1)} async-done(((bf16[64,30,128]{2,1,0:T(8,128)(2,1)}), bf16[64,30,128]{2,1,0:T(8,128)(2,1)S(1)}, u32[]{:S(2)}, u32[]{:S(2)}) %all-to-all-start.2) | async-done | bytes 491552 | tf_op jit(solution)/shard_map/all_to_all | solution.py:183
  (83 shorter events, 20.7 us)
Async XLA Ops:
  2.8 13.3 %copy-start = (bf16[640,2560]{1,0:T(8,128)(2,1)S(1)}, bf16[640,2560]{1,0:T(8,128)(2,1)}, u32[]{:S(2)}) copy-start(bf16[640,2560]{1,0:T(8,128)(2,1)} %param.18) | copy-start | bytes 9830404
  16.0 8.2 %copy-start.4 = (s32[64,6]{0,1:T(8,128)S(1)}, s32[64,6]{0,1:T(8,128)}, u32[]{:S(2)}) copy-start(s32[64,6]{0,1:T(8,128)} %param.20) | copy-start | bytes 4612
  17.6 0.9 copy-start.1
  18.5 6.4 %collective-permute-start = (f32[64,640]{1,0:T(8,128)S(1)}, f32[64,640]{1,0:T(8,128)S(1)}, u32[]{:S(2)}, u32[]{:S(2)}) collective-permute-start(f32[64,640]{1,0:T(8,128)S(1)} %get-tuple-element.17), channel_id=1, source_target_pairs={{0,1},{1,2},{2,3},{3,0},{4,5},{5,6},{6,7},{7,4},{8,9},{9,10},{10,1... | collective-permute-start | bytes 491528 | tf_op jit(solution)/shard_map/ppermute | solution.py:165
  20.6 9.6 %collective-permute-start.1 = (f32[64,640]{1,0:T(8,128)S(1)}, f32[64,640]{1,0:T(8,128)S(1)}, u32[]{:S(2)}, u32[]{:S(2)}) collective-permute-start(f32[64,640]{1,0:T(8,128)S(1)} %get-tuple-element.19), channel_id=1, source_target_pairs={{0,2},{1,3},{2,0},{3,1},{4,6},{5,7},{6,4},{7,5},{8,10},{9,11},{10,... | collective-permute-start | bytes 491528 | tf_op jit(solution)/shard_map/ppermute | solution.py:165
  23.1 7.2 %collective-permute-start.2 = (f32[64,640]{1,0:T(8,128)S(1)}, f32[64,640]{1,0:T(8,128)S(1)}, u32[]{:S(2)}, u32[]{:S(2)}) collective-permute-start(f32[64,640]{1,0:T(8,128)S(1)} %get-tuple-element.18), channel_id=1, source_target_pairs={{0,3},{1,0},{2,1},{3,2},{4,7},{5,4},{6,5},{7,6},{8,11},{9,8},{10,9... | collective-permute-start | bytes 491528 | tf_op jit(solution)/shard_map/ppermute | solution.py:165
  31.4 5.2 %collective-permute-start.3 = (f32[64,1]{0,1:T(1,128)S(1)}, f32[64,1]{0,1:T(1,128)S(1)}, u32[]{:S(2)}, u32[]{:S(2)}) collective-permute-start(f32[64,1]{0,1:T(1,128)S(1)} %bitcast.121), channel_id=1, source_target_pairs={{0,1},{1,2},{2,3},{3,0},{4,5},{5,6},{6,7},{7,4},{8,9},{9,10},{10,1... | collective-permute-start | bytes 776 | tf_op jit(solution)/shard_map/ppermute | solution.py:165
  32.4 4.2 %collective-permute-start.4 = (f32[64,1]{0,1:T(1,128)S(1)}, f32[64,1]{0,1:T(1,128)S(1)}, u32[]{:S(2)}, u32[]{:S(2)}) collective-permute-start(f32[64,1]{0,1:T(1,128)S(1)} %bitcast.122), channel_id=1, source_target_pairs={{0,2},{1,3},{2,0},{3,1},{4,6},{5,7},{6,4},{7,5},{8,10},{9,11},{10,... | collective-permute-start | bytes 776 | tf_op jit(solution)/shard_map/ppermute | solution.py:165
  34.3 2.4 %collective-permute-start.5 = (f32[64,1]{0,1:T(1,128)S(1)}, f32[64,1]{0,1:T(1,128)S(1)}, u32[]{:S(2)}, u32[]{:S(2)}) collective-permute-start(f32[64,1]{0,1:T(1,128)S(1)} %bitcast.123), channel_id=1, source_target_pairs={{0,3},{1,0},{2,1},{3,2},{4,7},{5,4},{6,5},{7,6},{8,11},{9,8},{10,9... | collective-permute-start | bytes 776 | tf_op jit(solution)/shard_map/ppermute | solution.py:165
  77.9 3.7 %copy-start.2 = (bf16[1,384,2560]{2,1,0:T(8,128)(2,1)S(1)}, bf16[1,384,2560]{2,1,0:T(8,128)(2,1)}, u32[]{:S(2)}) copy-start(bf16[1,384,2560]{2,1,0:T(8,128)(2,1)} %param.23) | copy-start | bytes 5898244
  79.0 19.2 %collective-permute-start.6 = (bf16[64,9,640]{2,0,1:T(8,128)(2,1)}, bf16[64,9,640]{2,0,1:T(8,128)(2,1)}, u32[]{:S(2)}, u32[]{:S(2)}) collective-permute-start(bf16[64,9,640]{2,0,1:T(8,128)(2,1)} %copy.74), channel_id=1, source_target_pairs={{0,1},{1,2},{2,3},{3,0},{4,5},{5,6},{6,7},{7,4},{8,9},{9,10},{10,1... | collective-permute-start | bytes 2211848 | tf_op jit(solution)/shard_map/ppermute | solution.py:165
  79.1 20.2 %collective-permute-start.8 = (bf16[64,9,640]{2,0,1:T(8,128)(2,1)}, bf16[64,9,640]{2,0,1:T(8,128)(2,1)}, u32[]{:S(2)}, u32[]{:S(2)}) collective-permute-start(bf16[64,9,640]{2,0,1:T(8,128)(2,1)} %copy.74), channel_id=1, source_target_pairs={{0,3},{1,0},{2,1},{3,2},{4,7},{5,4},{6,5},{7,6},{8,11},{9,8},{10,9... | collective-permute-start | bytes 2211848 | tf_op jit(solution)/shard_map/ppermute | solution.py:165
  99.2 10.2 %collective-permute-start.7 = (bf16[32,9,640]{2,0,1:T(8,128)(2,1)S(1)}, bf16[32,9,640]{2,0,1:T(8,128)(2,1)S(1)}, u32[]{:S(2)}, u32[]{:S(2)}) collective-permute-start(bf16[32,9,640]{2,0,1:T(8,128)(2,1)S(1)} %slice.73), channel_id=1, source_target_pairs={{0,1},{1,2},{2,3},{3,0},{4,5},{5,6},{6,7},{7,4},{8,9},{9,10},{10,1... | collective-permute-start | bytes 1105928 | tf_op jit(solution)/shard_map/ppermute | solution.py:165
  100.3 9.1 %collective-permute-start.9 = (bf16[32,9,640]{2,0,1:T(8,128)(2,1)S(1)}, bf16[32,9,640]{2,0,1:T(8,128)(2,1)S(1)}, u32[]{:S(2)}, u32[]{:S(2)}) collective-permute-start(bf16[32,9,640]{2,0,1:T(8,128)(2,1)S(1)} %slice.74), channel_id=1, source_target_pairs={{0,3},{1,0},{2,1},{3,2},{4,7},{5,4},{6,5},{7,6},{8,11},{9,8},{10,9... | collective-permute-start | bytes 1105928 | tf_op jit(solution)/shard_map/ppermute | solution.py:165
  110.3 2.2 %copy-start.3 = (bf16[384,4,640]{2,1,0:T(4,128)(2,1)S(1)}, bf16[384,4,640]{2,1,0:T(4,128)(2,1)}, u32[]{:S(2)}) copy-start(bf16[384,4,640]{2,1,0:T(4,128)(2,1)} %reshape_squeeze.3) | copy-start | bytes 5898244
  115.5 11.9 %collective-permute-start.18 = (bf16[32,6,640]{2,0,1:T(8,128)(2,1)S(1)}, bf16[32,6,640]{2,0,1:T(8,128)(2,1)}, u32[]{:S(2)}, u32[]{:S(2)}) collective-permute-start(bf16[32,6,640]{2,0,1:T(8,128)(2,1)S(1)} %slice_bitcast_fusion), channel_id=1, source_target_pairs={{0,1},{1,2},{2,3},{3,0},{4,5},{5,6},{6,7},{7,4},{8,9},{9,10},{10,1... | collective-permute-start | bytes 737288 | tf_op jit(solution)/shard_map/ppermute | solution.py:165
  116.1 13.4 %collective-permute-start.20 = (bf16[32,6,640]{2,0,1:T(8,128)(2,1)S(1)}, bf16[32,6,640]{2,0,1:T(8,128)(2,1)}, u32[]{:S(2)}, u32[]{:S(2)}) collective-permute-start(bf16[32,6,640]{2,0,1:T(8,128)(2,1)S(1)} %dynamic-slice_bitcast_fusion.3), channel_id=1, source_target_pairs={{0,3},{1,0},{2,1},{3,2},{4,7},{5,4},{6,5},{7,6},{8,11},{9,8},{10,9... | collective-permute-start | bytes 737288 | tf_op jit(solution)/shard_map/ppermute | solution.py:165
  119.2 6.7 %collective-permute-start.12 = (bf16[32,3,640]{2,0,1:T(8,128)(2,1)S(1)}, bf16[32,3,640]{2,0,1:T(8,128)(2,1)S(1)}, u32[]{:S(2)}, u32[]{:S(2)}) collective-permute-start(bf16[32,3,640]{2,0,1:T(8,128)(2,1)S(1)} %slice_bitcast_fusion.1), channel_id=1, source_target_pairs={{0,1},{1,2},{2,3},{3,0},{4,5},{5,6},{6,7},{7,4},{8,9},{9,10},{10,1... | collective-permute-start | bytes 368648 | tf_op jit(solution)/shard_map/ppermute | solution.py:165
  119.3 7.5 %collective-permute-start.14 = (bf16[32,3,640]{2,0,1:T(8,128)(2,1)S(1)}, bf16[32,3,640]{2,0,1:T(8,128)(2,1)S(1)}, u32[]{:S(2)}, u32[]{:S(2)}) collective-permute-start(bf16[32,3,640]{2,0,1:T(8,128)(2,1)S(1)} %dynamic-slice_bitcast_fusion.10), channel_id=1, source_target_pairs={{0,3},{1,0},{2,1},{3,2},{4,7},{5,4},{6,5},{7,6},{8,11},{9,8},{10,9... | collective-permute-start | bytes 368648 | tf_op jit(solution)/shard_map/ppermute | solution.py:165
  122.1 12.6 %collective-permute-start.10 = (bf16[64,3,640]{2,0,1:T(8,128)(2,1)S(1)}, bf16[64,3,640]{2,0,1:T(8,128)(2,1)S(1)}, u32[]{:S(2)}, u32[]{:S(2)}) collective-permute-start(bf16[64,3,640]{2,0,1:T(8,128)(2,1)S(1)} %get-tuple-element.16), channel_id=1, source_target_pairs={{0,1},{1,2},{2,3},{3,0},{4,5},{5,6},{6,7},{7,4},{8,9},{9,10},{10,1... | collective-permute-start | bytes 737288 | tf_op jit(solution)/shard_map/ppermute | solution.py:165
  126.0 9.4 %collective-permute-start.11 = (bf16[64,3,640]{2,0,1:T(8,128)(2,1)S(1)}, bf16[64,3,640]{2,0,1:T(8,128)(2,1)S(1)}, u32[]{:S(2)}, u32[]{:S(2)}) collective-permute-start(bf16[64,3,640]{2,0,1:T(8,128)(2,1)S(1)} %get-tuple-element.15), channel_id=1, source_target_pairs={{0,3},{1,0},{2,1},{3,2},{4,7},{5,4},{6,5},{7,6},{8,11},{9,8},{10,9... | collective-permute-start | bytes 737288 | tf_op jit(solution)/shard_map/ppermute | solution.py:165
  126.9 7.0 %collective-permute-start.13 = (bf16[32,3,640]{2,0,1:T(8,128)(2,1)S(1)}, bf16[32,3,640]{2,0,1:T(8,128)(2,1)S(1)}, u32[]{:S(2)}, u32[]{:S(2)}) collective-permute-start(bf16[32,3,640]{2,0,1:T(8,128)(2,1)S(1)} %collective-permute-done.12), channel_id=1, source_target_pairs={{0,1},{1,2},{2,3},{3,0},{4,5},{5,6},{6,7},{7,4},{8,9},{9,10},{10,1... | collective-permute-start | bytes 368648 | tf_op jit(solution)/shard_map/ppermute | solution.py:165
  127.4 9.9 %collective-permute-start.15 = (bf16[32,3,640]{2,0,1:T(8,128)(2,1)S(1)}, bf16[32,3,640]{2,0,1:T(8,128)(2,1)S(1)}, u32[]{:S(2)}, u32[]{:S(2)}) collective-permute-start(bf16[32,3,640]{2,0,1:T(8,128)(2,1)S(1)} %collective-permute-done.14), channel_id=1, source_target_pairs={{0,3},{1,0},{2,1},{3,2},{4,7},{5,4},{6,5},{7,6},{8,11},{9,8},{10,9... | collective-permute-start | bytes 368648 | tf_op jit(solution)/shard_map/ppermute | solution.py:165
  129.5 22.0 %collective-permute-start.16 = (bf16[64,6,640]{2,0,1:T(8,128)(2,1)}, bf16[64,6,640]{2,0,1:T(8,128)(2,1)}, u32[]{:S(2)}, u32[]{:S(2)}) collective-permute-start(bf16[64,6,640]{2,0,1:T(8,128)(2,1)} %get-tuple-element.13), channel_id=1, source_target_pairs={{0,1},{1,2},{2,3},{3,0},{4,5},{5,6},{6,7},{7,4},{8,9},{9,10},{10,1... | collective-permute-start | bytes 1474568 | tf_op jit(solution)/shard_map/ppermute | solution.py:165
  133.9 17.7 %collective-permute-start.17 = (bf16[64,6,640]{2,0,1:T(8,128)(2,1)S(1)}, bf16[64,6,640]{2,0,1:T(8,128)(2,1)}, u32[]{:S(2)}, u32[]{:S(2)}) collective-permute-start(bf16[64,6,640]{2,0,1:T(8,128)(2,1)S(1)} %get-tuple-element.12), channel_id=1, source_target_pairs={{0,3},{1,0},{2,1},{3,2},{4,7},{5,4},{6,5},{7,6},{8,11},{9,8},{10,9... | collective-permute-start | bytes 1474568 | tf_op jit(solution)/shard_map/ppermute | solution.py:165
  134.7 16.9 %collective-permute-start.19 = (bf16[32,6,640]{2,0,1:T(8,128)(2,1)}, bf16[32,6,640]{2,0,1:T(8,128)(2,1)}, u32[]{:S(2)}, u32[]{:S(2)}) collective-permute-start(bf16[32,6,640]{2,0,1:T(8,128)(2,1)} %collective-permute-done.18), channel_id=1, source_target_pairs={{0,1},{1,2},{2,3},{3,0},{4,5},{5,6},{6,7},{7,4},{8,9},{9,10},{10,1... | collective-permute-start | bytes 737288 | tf_op jit(solution)/shard_map/ppermute | solution.py:165
  135.4 16.2 %collective-permute-start.21 = (bf16[32,6,640]{2,0,1:T(8,128)(2,1)}, bf16[32,6,640]{2,0,1:T(8,128)(2,1)S(1)}, u32[]{:S(2)}, u32[]{:S(2)}) collective-permute-start(bf16[32,6,640]{2,0,1:T(8,128)(2,1)} %collective-permute-done.20), channel_id=1, source_target_pairs={{0,3},{1,0},{2,1},{3,2},{4,7},{5,4},{6,5},{7,6},{8,11},{9,8},{10,9... | collective-permute-start | bytes 737288 | tf_op jit(solution)/shard_map/ppermute | solution.py:165
  138.6 24.9 %all-to-all-start.1 = ((bf16[64,15,128]{2,1,0:T(8,128)(2,1)}), bf16[64,15,128]{2,1,0:T(8,128)(2,1)S(1)}, u32[]{:S(2)}, u32[]{:S(2)}) async-start(bf16[64,15,128]{2,1,0:T(8,128)(2,1)} %reshape.58), calls=%async_computation.1 | async-start | bytes 524288 | tf_op jit(solution)/shard_map/all_to_all | solution.py:183
  153.1 16.4 %copy-start.5 = (f32[64,6]{0,1:T(8,128)S(1)}, f32[64,6]{0,1:T(8,128)}, u32[]{:S(2)}) copy-start(f32[64,6]{0,1:T(8,128)} %param.21) | copy-start | bytes 4612
  163.5 23.3 %all-to-all-start.2 = ((bf16[64,30,128]{2,1,0:T(8,128)(2,1)}), bf16[64,30,128]{2,1,0:T(8,128)(2,1)S(1)}, u32[]{:S(2)}, u32[]{:S(2)}) async-start(bf16[64,30,128]{2,1,0:T(8,128)(2,1)} %reshape.60), calls=%async_computation.2 | async-start | bytes 1048576 | tf_op jit(solution)/shard_map/all_to_all | solution.py:183

commit v4 on v2

--- a/solution.py
+++ b/solution.py
@@ -12,11 +12,11 @@
 
 
 def attention_kernel(
-    table_ref, len_ref, base_ref, q_ref, new_k_ref, new_v_ref, kv_hbm, o_ref,
+    table_ref, len_ref, base_ref, q_ref, new_kv_ref, kv_hbm, o_ref,
     short_k, short_v, long_k, long_v, sem,
 ):
     rows = q_ref.shape[0]
-    head_dim = new_k_ref.shape[1]
+    head_dim = new_kv_ref.shape[2]
     groups = q_ref.shape[1] // head_dim
     table_width = table_ref.shape[1]
     pool_pages = kv_hbm.shape[1]
@@ -59,11 +59,6 @@
     def _(j):
         long_copy(j, 0, long_k).start()
         long_copy(j, 1, long_v).start()
-
-    @pl.loop(0, rows)
-    def _(r):
-        short_copy(r, 0, short_k).wait()
-        short_copy(r, 1, short_v).wait()
 
     def attend(qh, keys, values, valid, new_k, new_v):
         scores = lax.dot_general(
@@ -93,14 +88,20 @@
     def _(c):
         r0 = pl.multiple_of(c * chunk, chunk)
         k0 = pl.multiple_of(c * width, width)
+
+        @pl.loop(0, chunk)
+        def _(i):
+            short_copy(r0 + i, 0, short_k).wait()
+            short_copy(r0 + i, 1, short_v).wait()
+
         keys = short_k[pl.ds(k0, width), :]
         values = short_v[pl.ds(k0, width), :]
         lengths = jnp.zeros((chunk, 1), jnp.int32)
         for i in range(chunk):
             lengths = jnp.where(row[:, :1] == i, jnp.minimum(len_ref[r0 + i], SHORT), lengths)
         valid = (col >= row * SHORT) & (col < row * SHORT + lengths)
-        new_k = new_k_ref[pl.ds(r0, chunk), :]
-        new_v = new_v_ref[pl.ds(r0, chunk), :]
+        new_k = new_kv_ref[0, pl.ds(r0, chunk), :]
+        new_v = new_kv_ref[1, pl.ds(r0, chunk), :]
         for h in range(groups):
             qh = q_ref[pl.ds(r0, chunk), h * head_dim:(h + 1) * head_dim]
             o_ref[pl.ds(r0, chunk), h * head_dim:(h + 1) * head_dim] = attend(
@@ -119,8 +120,8 @@
     @pl.when(long_len >= SHORT)
     def _():
         r0 = pl.multiple_of((long_row // chunk) * chunk, chunk)
-        new_k = new_k_ref[pl.ds(r0, chunk), :]
-        new_v = new_v_ref[pl.ds(r0, chunk), :]
+        new_k = new_kv_ref[0, pl.ds(r0, chunk), :]
+        new_v = new_kv_ref[1, pl.ds(r0, chunk), :]
         chosen = (own_row + r0) == long_row
         for h in range(groups):
             qh = q_ref[pl.ds(r0, chunk), h * head_dim:(h + 1) * head_dim]
@@ -144,7 +145,7 @@
     return pl.pallas_call(
         attention_kernel,
         out_shape=jax.ShapeDtypeStruct(query.shape, jnp.bfloat16),
-        in_specs=[smem, smem, smem, vmem, vmem, vmem, pl.BlockSpec(memory_space=pl.ANY)],
+        in_specs=[smem, smem, smem, vmem, vmem, pl.BlockSpec(memory_space=pl.ANY)],
         out_specs=vmem,
         scratch_shapes=[
             pltpu.VMEM((row_count * SHORT, head_dim), key_value_pages.dtype),
@@ -158,7 +159,7 @@
             transcendentals=16 * query.shape[1] // head_dim * rows,
             bytes_accessed=2 * 2 * head_dim * rows,
         ),
-    )(page_table, cache_len, base, query, new_kv[0], new_kv[1], key_value_pages)
+    )(page_table, cache_len, base, query, new_kv, key_value_pages)
 
 
 def ring_shift(x, shift, axis_name, size):

time: 185 us -> 183 us (0.989)
  waiting for transfers between devices: 64 us -> 66.9 us
  blocking collectives: 40.1 us -> 37.9 us
    ppermute x16, waiting for transfers between devices: 41.3 us -> 44.1 us  [ring_shift(): lax.ppermute(x, axis_name, [(i, (i + shift) % size) for i in range(size)])]
    all_to_all x1, blocking collectives: 40.1 us -> 37.9 us  [dense_all_to_all(): lax.all_to_all(flat, axis_name, split_axis=0, concat_axis=0, tiled=True)]
  transfers between devices with their start and end apart: 17 -> 17, of which waited for: 7 -> 8; matrix products, arithmetic and copies ran while one was open for 7% -> 7% of each run, Pallas kernels for 0% -> 0%
where the time goes in v4:
time: 183 us; the launch traced here: 182 us
  waiting for transfers between devices  66.9 us (37%)
  blocking collectives  37.9 us (21%)
  starting transfers between devices  33.9 us (19%)
  local copies, waits for them, and re-layouts  16.7 us (9%)
  Pallas kernels  13.2 us (7%)
  matrix products  10.9 us (6%)
  other arithmetic  1.93 us (1%)
    ppermute x16, waiting for transfers between devices, ring_shift(): lax.ppermute(x, axis_name, [(i, (i + shift) % size) for i in range(size)])  44.1 us
    all_to_all x1, blocking collectives, dense_all_to_all(): lax.all_to_all(flat, axis_name, split_axis=0, concat_axis=0, tiled=True)  37.9 us
    ppermute x16, starting transfers between devices, ring_shift(): lax.ppermute(x, axis_name, [(i, (i + shift) % size) for i in range(size)])  24.4 us
    all_to_all x1, waiting for transfers between devices, dense_all_to_all(): lax.all_to_all(flat, axis_name, split_axis=0, concat_axis=0, tiled=True)  22.7 us
    pallas_call x1, Pallas kernels, local_attention(): pl.pallas_call(attention_kernel, out_shape=jax.ShapeDtypeStruct(query.sha...  13.2 us
    all_to_all x1, starting transfers between devices, dense_all_to_all(): lax.all_to_all(flat, axis_name, split_axis=0, concat_axis=0, tiled=True)  9.55 us
    dot_general x4, matrix products, per_device(): jnp.einsum('snc,cgf->sngf', piece, weight, preferred_element_type=jnp.flo...  5.84 us
    dynamic_slice x1, local copies, waits for them, and re-layouts, per_device(): lax.dynamic_index_in_dim(split_w1, (tensor_index - shift) % tensor_size,...  4.22 us
  transfers between devices with their start and end apart: 17, of which 8 were waited for; matrix products, arithmetic and copies ran while one was open for 7% of the time, Pallas kernels for 0%

profile of v4, /device:TPU:1, one launch (start us, length us, event | category | flops | bytes accessed | tf_op | source)
XLA Modules:
  0.0 181.8 jit_solution(7931819558623450254)
XLA Ops:
  0.0 1.4 copy.52.table_ref
  1.4 13.2 %shard_map.118 = bf16[64,640]{1,0:T(8,128)(2,1)} custom-call(s32[64,32]{1,0:T(8,128)} %copy.52.table_ref, s32[64]{0:T(128)} %len_ref.1, s32[1]{0:T(128)} %bitcast.base_ref, bf16[64,640]{1,0:T(8,128)(2,1)} %q_ref.1, bf16[2,64,128]{2,1,0:T(8,128)(2,1)} %new_kv_ref.1, bf16[2,95,128,128]{3,2,1,0:T(8,128)(2,1)} %kv_hbm.1), custom_call_target="tpu_custom_call" | custom-call | flops 335544320 | bytes 4194304 | tf_op jit(solution)/shard_map/pallas_call | solution.py:145
  14.7 1.6 fusion
  17.1 2.1 %collective-permute-start = (f32[64,640]{1,0:T(8,128)S(1)}, f32[64,640]{1,0:T(8,128)S(1)}, u32[]{:S(2)}, u32[]{:S(2)}) collective-permute-start(f32[64,640]{1,0:T(8,128)S(1)} %get-tuple-element.16), channel_id=1, source_target_pairs={{0,1},{1,2},{2,3},{3,0},{4,5},{5,6},{6,7},{7,4},{8,9},{9,10},{10,1... | collective-permute-start | bytes 491528 | tf_op jit(solution)/shard_map/ppermute | solution.py:166
  19.2 2.5 %collective-permute-start.1 = (f32[64,640]{1,0:T(8,128)S(1)}, f32[64,640]{1,0:T(8,128)S(1)}, u32[]{:S(2)}, u32[]{:S(2)}) collective-permute-start(f32[64,640]{1,0:T(8,128)S(1)} %get-tuple-element.18), channel_id=1, source_target_pairs={{0,2},{1,3},{2,0},{3,1},{4,6},{5,7},{6,4},{7,5},{8,10},{9,11},{10,... | collective-permute-start | bytes 491528 | tf_op jit(solution)/shard_map/ppermute | solution.py:166
  21.7 1.1 collective-permute-start.2
  23.5 5.3 %collective-permute-done.1 = f32[64,640]{1,0:T(8,128)S(1)} collective-permute-done((f32[64,640]{1,0:T(8,128)S(1)}, f32[64,640]{1,0:T(8,128)S(1)}, u32[]{:S(2)}, u32[]{:S(2)}) %collective-permute-start.1) | collective-permute-done | bytes 163872 | tf_op jit(solution)/shard_map/ppermute | solution.py:166
  28.9 1.1 multiply_reduce_fusion
  30.0 1.0 collective-permute-start.3
  31.0 1.9 %collective-permute-start.4 = (f32[64,1]{0,1:T(1,128)S(1)}, f32[64,1]{0,1:T(1,128)S(1)}, u32[]{:S(2)}, u32[]{:S(2)}) collective-permute-start(f32[64,1]{0,1:T(1,128)S(1)} %bitcast.91), channel_id=1, source_target_pairs={{0,2},{1,3},{2,0},{3,1},{4,6},{5,7},{6,4},{7,5},{8,10},{9,11},{10,... | collective-permute-start | bytes 776 | tf_op jit(solution)/shard_map/ppermute | solution.py:166
  32.9 1.3 collective-permute-start.5
  36.4 37.9 %all_to_all.10 = bf16[64,45,128]{2,1,0:T(8,128)(2,1)S(1)} all-to-all(bf16[64,45,128]{2,1,0:T(8,128)(2,1)S(1)} %reshape_reshape.6), channel_id=1, replica_groups=mesh['dp'=64,'tensor'=4] {'dp'}, dimensions={0} | all-to-all | bytes 1474560 | tf_op jit(solution)/shard_map/all_to_all | solution.py:184
  76.1 2.6 %collective-permute-start.8 = (bf16[64,9,640]{2,0,1:T(8,128)(2,1)}, bf16[64,9,640]{2,0,1:T(8,128)(2,1)}, u32[]{:S(2)}, u32[]{:S(2)}) collective-permute-start(bf16[64,9,640]{2,0,1:T(8,128)(2,1)} %copy.58), channel_id=1, source_target_pairs={{0,3},{1,0},{2,1},{3,2},{4,7},{5,4},{6,5},{7,6},{8,11},{9,8},{10,9... | collective-permute-start | bytes 2211848 | tf_op jit(solution)/shard_map/ppermute | solution.py:166
  78.6 2.0 %reshape_squeeze.3 = bf16[384,4,640]{2,1,0:T(4,128)(2,1)} reshape(bf16[1,384,2560]{2,1,0:T(8,128)(2,1)S(1)} %copy-done.2) | data formatting | bytes 3932160 | tf_op jit(solution)/shard_map/reshape;squeeze | solution.py:276
  80.6 4.2 %constant_dynamic-slice_fusion = (bf16[1,640,2,384]{3,2,1,0:T(2,128)(2,1)S(1)}, bf16[1,640,2,384]{3,2,1,0:T(2,128)(2,1)S(1)}, bf16[1,640,2,384]{3,2,1,0:T(2,128)(2,1)S(1)}, bf16[1,640,2,384]{3,2,1,0:T(2,128)(2,1)S(1)}) fusion(bf16[4,640,2,384]{3,2,1,0:T(2,128)(2,1)} %bitcast.88, s32[]{:T(128)S(6)} %select_n.94, s32[]{:T(128)S(6)} %select_n.92, ...), kind=kLoop, calls=%fused_computation.58 | loop fusion | bytes 7864336 | tf_op jit(solution)/shard_map/jit(dynamic_index_in_dim)/dynamic_slice | solution.py:287
  84.8 10.3 %collective-permute-done.6 = bf16[64,9,640]{2,0,1:T(8,128)(2,1)} collective-permute-done((bf16[64,9,640]{2,0,1:T(8,128)(2,1)}, bf16[64,9,640]{2,0,1:T(8,128)(2,1)}, u32[]{:S(2)}, u32[]{:S(2)}) %collective-permute-start.6) | collective-permute-done | bytes 737312 | tf_op jit(solution)/shard_map/ppermute | solution.py:166
  95.1 1.0 slice.32
  96.2 1.0 slice.33
  97.3 2.7 %collective-permute-start.9 = (bf16[32,9,640]{2,0,1:T(8,128)(2,1)S(1)}, bf16[32,9,640]{2,0,1:T(8,128)(2,1)S(1)}, u32[]{:S(2)}, u32[]{:S(2)}) collective-permute-start(bf16[32,9,640]{2,0,1:T(8,128)(2,1)S(1)} %slice.33), channel_id=1, source_target_pairs={{0,3},{1,0},{2,1},{3,2},{4,7},{5,4},{6,5},{7,6},{8,11},{9,8},{10,9... | collective-permute-start | bytes 1105928 | tf_op jit(solution)/shard_map/ppermute | solution.py:166
  100.9 2.0 %fusion.12 = f32[64,9,2,384]{3,0,2,1:T(8,128)S(1)} fusion(bf16[1,640,2,384]{3,2,1,0:T(2,128)(2,1)S(1)} %get-tuple-element.9, bf16[64,9,640]{2,0,1:T(8,128)(2,1)} %collective-permute-done.6), kind=kOutput, calls=%fused_computation.21 | convolution fusion | flops 566231040 | bytes 3489792 | tf_op jit(solution)/shard_map/snc,cgf->sngf/dot_general | solution.py:290
  102.8 3.5 %collective-permute-done.7 = bf16[32,9,640]{2,0,1:T(8,128)(2,1)S(1)} collective-permute-done((bf16[32,9,640]{2,0,1:T(8,128)(2,1)S(1)}, bf16[32,9,640]{2,0,1:T(8,128)(2,1)S(1)}, u32[]{:S(2)}, u32[]{:S(2)}) %collective-permute-start.7) | collective-permute-done | bytes 368672 | tf_op jit(solution)/shard_map/ppermute | solution.py:166
  107.3 2.1 %add_add_fusion = f32[64,9,2,384]{3,0,2,1:T(8,128)S(1)} fusion(f32[64,9,2,384]{3,0,2,1:T(8,128)S(1)} %fusion.11, f32[64,9,2,384]{3,0,2,1:T(8,128)S(1)} %fusion.13, f32[64,9,2,384]{3,0,2,1:T(8,128)S(1)} %fusion.12, bf16[1,640,2,384]{3,2,1,0:T(2,128)(2,1)S(1)} %get-tuple-element.7, bf16[64,9,640]{2,0,1:T(8,128)(2,1)} %collective-permute-done.8), kind=kOutput, calls=%fused_computation.6 | convolution fusion | flops 567558144 | bytes 8798208 | tf_op jit(solution)/shard_map/snc,cgf->sngf/dot_general | solution.py:290
  109.4 1.7 convolution_convert_fusion
  112.1 3.0 %collective-permute-start.14 = (bf16[32,9,640]{2,0,1:T(8,128)(2,1)S(1)}, bf16[32,9,640]{2,0,1:T(8,128)(2,1)S(1)}, u32[]{:S(2)}, u32[]{:S(2)}) collective-permute-start(bf16[32,9,640]{2,0,1:T(8,128)(2,1)S(1)} %get-tuple-element.15), channel_id=1, source_target_pairs={{0,3},{1,0},{2,1},{3,2},{4,7},{5,4},{6,5},{7,6},{8,11},{9,8},{10,9... | collective-permute-start | bytes 1105928 | tf_op jit(solution)/shard_map/ppermute | solution.py:166
  115.1 2.7 %collective-permute-start.11 = (bf16[64,9,640]{2,0,1:T(8,128)(2,1)S(1)}, bf16[64,9,640]{2,0,1:T(8,128)(2,1)S(1)}, u32[]{:S(2)}, u32[]{:S(2)}) collective-permute-start(bf16[64,9,640]{2,0,1:T(8,128)(2,1)S(1)} %get-tuple-element.12), channel_id=1, source_target_pairs={{0,3},{1,0},{2,1},{3,2},{4,7},{5,4},{6,5},{7,6},{8,11},{9,8},{10,9... | collective-permute-start | bytes 2211848 | tf_op jit(solution)/shard_map/ppermute | solution.py:166
  117.7 3.8 %collective-permute-done.12 = bf16[32,9,640]{2,0,1:T(8,128)(2,1)S(1)} collective-permute-done((bf16[32,9,640]{2,0,1:T(8,128)(2,1)S(1)}, bf16[32,9,640]{2,0,1:T(8,128)(2,1)S(1)}, u32[]{:S(2)}, u32[]{:S(2)}) %collective-permute-start.12) | collective-permute-done | bytes 368672 | tf_op jit(solution)/shard_map/ppermute | solution.py:166
  121.6 2.7 %collective-permute-start.15 = (bf16[32,9,640]{2,0,1:T(8,128)(2,1)S(1)}, bf16[32,9,640]{2,0,1:T(8,128)(2,1)S(1)}, u32[]{:S(2)}, u32[]{:S(2)}) collective-permute-start(bf16[32,9,640]{2,0,1:T(8,128)(2,1)S(1)} %collective-permute-done.14), channel_id=1, source_target_pairs={{0,3},{1,0},{2,1},{3,2},{4,7},{5,4},{6,5},{7,6},{8,11},{9,8},{10,9... | collective-permute-start | bytes 1105928 | tf_op jit(solution)/shard_map/ppermute | solution.py:166
  124.2 21.0 %collective-permute-done.13 = bf16[32,9,640]{2,0,1:T(8,128)(2,1)S(1)} collective-permute-done((bf16[32,9,640]{2,0,1:T(8,128)(2,1)S(1)}, bf16[32,9,640]{2,0,1:T(8,128)(2,1)S(1)}, u32[]{:S(2)}, u32[]{:S(2)}) %collective-permute-start.13) | collective-permute-done | bytes 368672 | tf_op jit(solution)/shard_map/ppermute | solution.py:166
  146.2 1.4 reshape.48
  147.6 9.5 %all-to-all-start.1 = ((bf16[64,45,128]{2,1,0:T(8,128)(2,1)}), bf16[64,45,128]{2,1,0:T(8,128)(2,1)S(1)}, u32[]{:S(2)}, u32[]{:S(2)}) async-start(bf16[64,45,128]{2,1,0:T(8,128)(2,1)} %reshape.48), calls=%async_computation.1 | async-start | bytes 1572864 | tf_op jit(solution)/shard_map/all_to_all | solution.py:184
  157.3 22.7 %all-to-all-done.1 = bf16[64,45,128]{2,1,0:T(8,128)(2,1)S(1)} async-done(((bf16[64,45,128]{2,1,0:T(8,128)(2,1)}), bf16[64,45,128]{2,1,0:T(8,128)(2,1)S(1)}, u32[]{:S(2)}, u32[]{:S(2)}) %all-to-all-start.1) | async-done | bytes 737312 | tf_op jit(solution)/shard_map/all_to_all | solution.py:184
  180.7 1.1 fusion.8
  (51 shorter events, 9.9 us)
Async XLA Ops:
  1.4 13.2 %copy-start = (bf16[640,2560]{1,0:T(8,128)(2,1)S(1)}, bf16[640,2560]{1,0:T(8,128)(2,1)}, u32[]{:S(2)}) copy-start(bf16[640,2560]{1,0:T(8,128)(2,1)} %param.18) | copy-start | bytes 9830404
  14.6 8.2 %copy-start.4 = (s32[64,6]{0,1:T(8,128)S(1)}, s32[64,6]{0,1:T(8,128)}, u32[]{:S(2)}) copy-start(s32[64,6]{0,1:T(8,128)} %param.20) | copy-start | bytes 4612
  16.2 0.8 copy-start.1
  17.1 6.4 %collective-permute-start = (f32[64,640]{1,0:T(8,128)S(1)}, f32[64,640]{1,0:T(8,128)S(1)}, u32[]{:S(2)}, u32[]{:S(2)}) collective-permute-start(f32[64,640]{1,0:T(8,128)S(1)} %get-tuple-element.16), channel_id=1, source_target_pairs={{0,1},{1,2},{2,3},{3,0},{4,5},{5,6},{6,7},{7,4},{8,9},{9,10},{10,1... | collective-permute-start | bytes 491528 | tf_op jit(solution)/shard_map/ppermute | solution.py:166
  19.2 9.6 %collective-permute-start.1 = (f32[64,640]{1,0:T(8,128)S(1)}, f32[64,640]{1,0:T(8,128)S(1)}, u32[]{:S(2)}, u32[]{:S(2)}) collective-permute-start(f32[64,640]{1,0:T(8,128)S(1)} %get-tuple-element.18), channel_id=1, source_target_pairs={{0,2},{1,3},{2,0},{3,1},{4,6},{5,7},{6,4},{7,5},{8,10},{9,11},{10,... | collective-permute-start | bytes 491528 | tf_op jit(solution)/shard_map/ppermute | solution.py:166
  21.7 7.2 %collective-permute-start.2 = (f32[64,640]{1,0:T(8,128)S(1)}, f32[64,640]{1,0:T(8,128)S(1)}, u32[]{:S(2)}, u32[]{:S(2)}) collective-permute-start(f32[64,640]{1,0:T(8,128)S(1)} %get-tuple-element.17), channel_id=1, source_target_pairs={{0,3},{1,0},{2,1},{3,2},{4,7},{5,4},{6,5},{7,6},{8,11},{9,8},{10,9... | collective-permute-start | bytes 491528 | tf_op jit(solution)/shard_map/ppermute | solution.py:166
  30.0 5.2 %collective-permute-start.3 = (f32[64,1]{0,1:T(1,128)S(1)}, f32[64,1]{0,1:T(1,128)S(1)}, u32[]{:S(2)}, u32[]{:S(2)}) collective-permute-start(f32[64,1]{0,1:T(1,128)S(1)} %bitcast.90), channel_id=1, source_target_pairs={{0,1},{1,2},{2,3},{3,0},{4,5},{5,6},{6,7},{7,4},{8,9},{9,10},{10,1... | collective-permute-start | bytes 776 | tf_op jit(solution)/shard_map/ppermute | solution.py:166
  31.0 4.2 %collective-permute-start.4 = (f32[64,1]{0,1:T(1,128)S(1)}, f32[64,1]{0,1:T(1,128)S(1)}, u32[]{:S(2)}, u32[]{:S(2)}) collective-permute-start(f32[64,1]{0,1:T(1,128)S(1)} %bitcast.91), channel_id=1, source_target_pairs={{0,2},{1,3},{2,0},{3,1},{4,6},{5,7},{6,4},{7,5},{8,10},{9,11},{10,... | collective-permute-start | bytes 776 | tf_op jit(solution)/shard_map/ppermute | solution.py:166
  32.9 2.4 %collective-permute-start.5 = (f32[64,1]{0,1:T(1,128)S(1)}, f32[64,1]{0,1:T(1,128)S(1)}, u32[]{:S(2)}, u32[]{:S(2)}) collective-permute-start(f32[64,1]{0,1:T(1,128)S(1)} %bitcast.92), channel_id=1, source_target_pairs={{0,3},{1,0},{2,1},{3,2},{4,7},{5,4},{6,5},{7,6},{8,11},{9,8},{10,9... | collective-permute-start | bytes 776 | tf_op jit(solution)/shard_map/ppermute | solution.py:166
  74.9 3.7 %copy-start.2 = (bf16[1,384,2560]{2,1,0:T(8,128)(2,1)S(1)}, bf16[1,384,2560]{2,1,0:T(8,128)(2,1)}, u32[]{:S(2)}) copy-start(bf16[1,384,2560]{2,1,0:T(8,128)(2,1)} %param.23) | copy-start | bytes 5898244
  75.9 19.2 %collective-permute-start.6 = (bf16[64,9,640]{2,0,1:T(8,128)(2,1)}, bf16[64,9,640]{2,0,1:T(8,128)(2,1)}, u32[]{:S(2)}, u32[]{:S(2)}) collective-permute-start(bf16[64,9,640]{2,0,1:T(8,128)(2,1)} %copy.58), channel_id=1, source_target_pairs={{0,1},{1,2},{2,3},{3,0},{4,5},{5,6},{6,7},{7,4},{8,9},{9,10},{10,1... | collective-permute-start | bytes 2211848 | tf_op jit(solution)/shard_map/ppermute | solution.py:166
  76.1 20.2 %collective-permute-start.8 = (bf16[64,9,640]{2,0,1:T(8,128)(2,1)}, bf16[64,9,640]{2,0,1:T(8,128)(2,1)}, u32[]{:S(2)}, u32[]{:S(2)}) collective-permute-start(bf16[64,9,640]{2,0,1:T(8,128)(2,1)} %copy.58), channel_id=1, source_target_pairs={{0,3},{1,0},{2,1},{3,2},{4,7},{5,4},{6,5},{7,6},{8,11},{9,8},{10,9... | collective-permute-start | bytes 2211848 | tf_op jit(solution)/shard_map/ppermute | solution.py:166
  96.1 10.2 %collective-permute-start.7 = (bf16[32,9,640]{2,0,1:T(8,128)(2,1)S(1)}, bf16[32,9,640]{2,0,1:T(8,128)(2,1)S(1)}, u32[]{:S(2)}, u32[]{:S(2)}) collective-permute-start(bf16[32,9,640]{2,0,1:T(8,128)(2,1)S(1)} %slice.32), channel_id=1, source_target_pairs={{0,1},{1,2},{2,3},{3,0},{4,5},{5,6},{6,7},{7,4},{8,9},{9,10},{10,1... | collective-permute-start | bytes 1105928 | tf_op jit(solution)/shard_map/ppermute | solution.py:166
  97.3 9.1 %collective-permute-start.9 = (bf16[32,9,640]{2,0,1:T(8,128)(2,1)S(1)}, bf16[32,9,640]{2,0,1:T(8,128)(2,1)S(1)}, u32[]{:S(2)}, u32[]{:S(2)}) collective-permute-start(bf16[32,9,640]{2,0,1:T(8,128)(2,1)S(1)} %slice.33), channel_id=1, source_target_pairs={{0,3},{1,0},{2,1},{3,2},{4,7},{5,4},{6,5},{7,6},{8,11},{9,8},{10,9... | collective-permute-start | bytes 1105928 | tf_op jit(solution)/shard_map/ppermute | solution.py:166
  107.3 2.2 %copy-start.3 = (bf16[384,4,640]{2,1,0:T(4,128)(2,1)S(1)}, bf16[384,4,640]{2,1,0:T(4,128)(2,1)}, u32[]{:S(2)}) copy-start(bf16[384,4,640]{2,1,0:T(4,128)(2,1)} %reshape_squeeze.3) | copy-start | bytes 5898244
  111.5 10.1 %collective-permute-start.12 = (bf16[32,9,640]{2,0,1:T(8,128)(2,1)S(1)}, bf16[32,9,640]{2,0,1:T(8,128)(2,1)S(1)}, u32[]{:S(2)}, u32[]{:S(2)}) collective-permute-start(bf16[32,9,640]{2,0,1:T(8,128)(2,1)S(1)} %get-tuple-element.14), channel_id=1, source_target_pairs={{0,1},{1,2},{2,3},{3,0},{4,5},{5,6},{6,7},{7,4},{8,9},{9,10},{10,1... | collective-permute-start | bytes 1105928 | tf_op jit(solution)/shard_map/ppermute | solution.py:166
  112.1 9.5 %collective-permute-start.14 = (bf16[32,9,640]{2,0,1:T(8,128)(2,1)S(1)}, bf16[32,9,640]{2,0,1:T(8,128)(2,1)S(1)}, u32[]{:S(2)}, u32[]{:S(2)}) collective-permute-start(bf16[32,9,640]{2,0,1:T(8,128)(2,1)S(1)} %get-tuple-element.15), channel_id=1, source_target_pairs={{0,3},{1,0},{2,1},{3,2},{4,7},{5,4},{6,5},{7,6},{8,11},{9,8},{10,9... | collective-permute-start | bytes 1105928 | tf_op jit(solution)/shard_map/ppermute | solution.py:166
  115.1 30.2 %collective-permute-start.10 = (bf16[64,9,640]{2,0,1:T(8,128)(2,1)S(1)}, bf16[64,9,640]{2,0,1:T(8,128)(2,1)S(1)}, u32[]{:S(2)}, u32[]{:S(2)}) collective-permute-start(bf16[64,9,640]{2,0,1:T(8,128)(2,1)S(1)} %get-tuple-element.13), channel_id=1, source_target_pairs={{0,1},{1,2},{2,3},{3,0},{4,5},{5,6},{6,7},{7,4},{8,9},{9,10},{10,1... | collective-permute-start | bytes 2211848 | tf_op jit(solution)/shard_map/ppermute | solution.py:166
  115.1 30.2 %collective-permute-start.11 = (bf16[64,9,640]{2,0,1:T(8,128)(2,1)S(1)}, bf16[64,9,640]{2,0,1:T(8,128)(2,1)S(1)}, u32[]{:S(2)}, u32[]{:S(2)}) collective-permute-start(bf16[64,9,640]{2,0,1:T(8,128)(2,1)S(1)} %get-tuple-element.12), channel_id=1, source_target_pairs={{0,3},{1,0},{2,1},{3,2},{4,7},{5,4},{6,5},{7,6},{8,11},{9,8},{10,9... | collective-permute-start | bytes 2211848 | tf_op jit(solution)/shard_map/ppermute | solution.py:166
  121.6 23.7 %collective-permute-start.13 = (bf16[32,9,640]{2,0,1:T(8,128)(2,1)S(1)}, bf16[32,9,640]{2,0,1:T(8,128)(2,1)S(1)}, u32[]{:S(2)}, u32[]{:S(2)}) collective-permute-start(bf16[32,9,640]{2,0,1:T(8,128)(2,1)S(1)} %collective-permute-done.12), channel_id=1, source_target_pairs={{0,1},{1,2},{2,3},{3,0},{4,5},{5,6},{6,7},{7,4},{8,9},{9,10},{10,1... | collective-permute-start | bytes 1105928 | tf_op jit(solution)/shard_map/ppermute | solution.py:166
  121.6 23.7 %collective-permute-start.15 = (bf16[32,9,640]{2,0,1:T(8,128)(2,1)S(1)}, bf16[32,9,640]{2,0,1:T(8,128)(2,1)S(1)}, u32[]{:S(2)}, u32[]{:S(2)}) collective-permute-start(bf16[32,9,640]{2,0,1:T(8,128)(2,1)S(1)} %collective-permute-done.14), channel_id=1, source_target_pairs={{0,3},{1,0},{2,1},{3,2},{4,7},{5,4},{6,5},{7,6},{8,11},{9,8},{10,9... | collective-permute-start | bytes 1105928 | tf_op jit(solution)/shard_map/ppermute | solution.py:166
  146.2 11.0 %copy-start.5 = (f32[64,6]{0,1:T(8,128)S(1)}, f32[64,6]{0,1:T(8,128)}, u32[]{:S(2)}) copy-start(f32[64,6]{0,1:T(8,128)} %param.21) | copy-start | bytes 4612
  147.6 32.5 %all-to-all-start.1 = ((bf16[64,45,128]{2,1,0:T(8,128)(2,1)}), bf16[64,45,128]{2,1,0:T(8,128)(2,1)S(1)}, u32[]{:S(2)}, u32[]{:S(2)}) async-start(bf16[64,45,128]{2,1,0:T(8,128)(2,1)} %reshape.48), calls=%async_computation.1 | async-start | bytes 1572864 | tf_op jit(solution)/shard_map/all_to_all | solution.py:184

commit v5 on v4

--- a/solution.py
+++ b/solution.py
@@ -243,7 +243,11 @@
     summed = ring_reduce_scatter(partial_proj, "tensor", tensor_size, tensor_index)
     residual_share = lax.dynamic_slice_in_dim(residual, share_start, share_width, 1)
     state = residual_share.astype(jnp.float32) + summed
-    square_sum = sum(ring_all_gather(jnp.sum(state * state, axis=1, keepdims=True), "tensor", tensor_size))
+    own_square = jnp.sum(state * state, axis=1, keepdims=True)
+    square_from_left = ring_shift(own_square, 1, "tensor", tensor_size)
+    square_from_right = ring_shift(own_square, tensor_size - 1, "tensor", tensor_size)
+    square_far = ring_shift(square_from_left, 1, "tensor", tensor_size)
+    square_sum = own_square + square_from_left + square_far + square_from_right
     mean_square = square_sum / model_width
     gain_share = lax.dynamic_slice_in_dim(norm_gain, share_start, share_width, 0)
     normed = (state * lax.rsqrt(mean_square + 1e-05) * gain_share).astype(jnp.bfloat16)

time: 183 us -> 185 us (1.011)
  waiting for transfers between devices: 66.9 us -> 70.3 us
    ppermute x16, waiting for transfers between devices: 44.1 us -> 47.6 us  [ring_shift(): lax.ppermute(x, axis_name, [(i, (i + shift) % size) for i in range(size)])]
  transfers between devices with their start and end apart: 17 -> 17, of which waited for: 8 -> 9; matrix products, arithmetic and copies ran while one was open for 7% -> 7% of each run, Pallas kernels for 0% -> 0%
where the time goes in v5:
time: 185 us; the launch traced here: 184 us
  waiting for transfers between devices  70.3 us (38%)
  blocking collectives  38.2 us (21%)
  starting transfers between devices  32.4 us (18%)
  local copies, waits for them, and re-layouts  16.7 us (9%)
  Pallas kernels  13.2 us (7%)
  matrix products  10.9 us (6%)
  other arithmetic  1.93 us (1%)
    ppermute x16, waiting for transfers between devices, ring_shift(): lax.ppermute(x, axis_name, [(i, (i + shift) % size) for i in range(size)])  47.6 us
    all_to_all x1, blocking collectives, dense_all_to_all(): lax.all_to_all(flat, axis_name, split_axis=0, concat_axis=0, tiled=True)  38.2 us
    ppermute x16, starting transfers between devices, ring_shift(): lax.ppermute(x, axis_name, [(i, (i + shift) % size) for i in range(size)])  22.9 us
    all_to_all x1, waiting for transfers between devices, dense_all_to_all(): lax.all_to_all(flat, axis_name, split_axis=0, concat_axis=0, tiled=True)  22.7 us
    pallas_call x1, Pallas kernels, local_attention(): pl.pallas_call(attention_kernel, out_shape=jax.ShapeDtypeStruct(query.sha...  13.2 us
    all_to_all x1, starting transfers between devices, dense_all_to_all(): lax.all_to_all(flat, axis_name, split_axis=0, concat_axis=0, tiled=True)  9.55 us
    dot_general x4, matrix products, per_device(): jnp.einsum('snc,cgf->sngf', piece, weight, preferred_element_type=jnp.flo...  5.85 us
    dynamic_slice x1, local copies, waits for them, and re-layouts, per_device(): lax.dynamic_index_in_dim(split_w1, (tensor_index - shift) % tensor_size,...  4.22 us
  transfers between devices with their start and end apart: 17, of which 9 were waited for; matrix products, arithmetic and copies ran while one was open for 7% of the time, Pallas kernels for 0%

profile of v5, /device:TPU:1, one launch (start us, length us, event | category | flops | bytes accessed | tf_op | source)
XLA Modules:
  0.0 184.0 jit_solution(5160495254009219778)
XLA Ops:
  0.0 1.4 copy.52.table_ref
  1.4 13.2 %shard_map.118 = bf16[64,640]{1,0:T(8,128)(2,1)} custom-call(s32[64,32]{1,0:T(8,128)} %copy.52.table_ref, s32[64]{0:T(128)} %len_ref.1, s32[1]{0:T(128)} %bitcast.base_ref, bf16[64,640]{1,0:T(8,128)(2,1)} %q_ref.1, bf16[2,64,128]{2,1,0:T(8,128)(2,1)} %new_kv_ref.1, bf16[2,95,128,128]{3,2,1,0:T(8,128)(2,1)} %kv_hbm.1), custom_call_target="tpu_custom_call" | custom-call | flops 335544320 | bytes 4194304 | tf_op jit(solution)/shard_map/pallas_call | solution.py:145
  14.7 1.6 fusion
  17.1 2.1 %collective-permute-start = (f32[64,640]{1,0:T(8,128)S(1)}, f32[64,640]{1,0:T(8,128)S(1)}, u32[]{:S(2)}, u32[]{:S(2)}) collective-permute-start(f32[64,640]{1,0:T(8,128)S(1)} %get-tuple-element.16), channel_id=1, source_target_pairs={{0,1},{1,2},{2,3},{3,0},{4,5},{5,6},{6,7},{7,4},{8,9},{9,10},{10,1... | collective-permute-start | bytes 491528 | tf_op jit(solution)/shard_map/ppermute | solution.py:166
  19.2 2.5 %collective-permute-start.1 = (f32[64,640]{1,0:T(8,128)S(1)}, f32[64,640]{1,0:T(8,128)S(1)}, u32[]{:S(2)}, u32[]{:S(2)}) collective-permute-start(f32[64,640]{1,0:T(8,128)S(1)} %get-tuple-element.18), channel_id=1, source_target_pairs={{0,2},{1,3},{2,0},{3,1},{4,6},{5,7},{6,4},{7,5},{8,10},{9,11},{10,... | collective-permute-start | bytes 491528 | tf_op jit(solution)/shard_map/ppermute | solution.py:166
  21.7 1.1 collective-permute-start.2
  23.5 5.3 %collective-permute-done.1 = f32[64,640]{1,0:T(8,128)S(1)} collective-permute-done((f32[64,640]{1,0:T(8,128)S(1)}, f32[64,640]{1,0:T(8,128)S(1)}, u32[]{:S(2)}, u32[]{:S(2)}) %collective-permute-start.1) | collective-permute-done | bytes 163872 | tf_op jit(solution)/shard_map/ppermute | solution.py:166
  28.9 1.1 multiply_reduce_fusion
  30.0 1.0 collective-permute-start.3
  31.0 1.7 collective-permute-start.5
  34.7 2.6 %collective-permute-done.4 = f32[64,1]{0,1:T(1,128)S(1)} collective-permute-done((f32[64,1]{0,1:T(1,128)S(1)}, f32[64,1]{0,1:T(1,128)S(1)}, u32[]{:S(2)}, u32[]{:S(2)}) %collective-permute-start.4) | collective-permute-done | bytes 288 | tf_op jit(solution)/shard_map/ppermute | solution.py:166
  38.4 38.2 %all_to_all.10 = bf16[64,45,128]{2,1,0:T(8,128)(2,1)S(1)} all-to-all(bf16[64,45,128]{2,1,0:T(8,128)(2,1)S(1)} %reshape_reshape.6), channel_id=1, replica_groups=mesh['dp'=64,'tensor'=4] {'dp'}, dimensions={0} | all-to-all | bytes 1474560 | tf_op jit(solution)/shard_map/all_to_all | solution.py:184
  78.2 2.7 %collective-permute-start.8 = (bf16[64,9,640]{2,0,1:T(8,128)(2,1)}, bf16[64,9,640]{2,0,1:T(8,128)(2,1)}, u32[]{:S(2)}, u32[]{:S(2)}) collective-permute-start(bf16[64,9,640]{2,0,1:T(8,128)(2,1)} %copy.58), channel_id=1, source_target_pairs={{0,3},{1,0},{2,1},{3,2},{4,7},{5,4},{6,5},{7,6},{8,11},{9,8},{10,9... | collective-permute-start | bytes 2211848 | tf_op jit(solution)/shard_map/ppermute | solution.py:166
  80.9 2.0 %reshape_squeeze.3 = bf16[384,4,640]{2,1,0:T(4,128)(2,1)} reshape(bf16[1,384,2560]{2,1,0:T(8,128)(2,1)S(1)} %copy-done.2) | data formatting | bytes 3932160 | tf_op jit(solution)/shard_map/reshape;squeeze | solution.py:280
  82.9 4.2 %constant_dynamic-slice_fusion = (bf16[1,640,2,384]{3,2,1,0:T(2,128)(2,1)S(1)}, bf16[1,640,2,384]{3,2,1,0:T(2,128)(2,1)S(1)}, bf16[1,640,2,384]{3,2,1,0:T(2,128)(2,1)S(1)}, bf16[1,640,2,384]{3,2,1,0:T(2,128)(2,1)S(1)}) fusion(bf16[4,640,2,384]{3,2,1,0:T(2,128)(2,1)} %bitcast.88, s32[]{:T(128)S(6)} %select_n.94, s32[]{:T(128)S(6)} %select_n.92, ...), kind=kLoop, calls=%fused_computation.58 | loop fusion | bytes 7864336 | tf_op jit(solution)/shard_map/jit(dynamic_index_in_dim)/dynamic_slice | solution.py:291
  87.1 10.3 %collective-permute-done.6 = bf16[64,9,640]{2,0,1:T(8,128)(2,1)} collective-permute-done((bf16[64,9,640]{2,0,1:T(8,128)(2,1)}, bf16[64,9,640]{2,0,1:T(8,128)(2,1)}, u32[]{:S(2)}, u32[]{:S(2)}) %collective-permute-start.6) | collective-permute-done | bytes 737312 | tf_op jit(solution)/shard_map/ppermute | solution.py:166
  97.4 1.0 slice.32
  98.5 1.0 slice.33
  99.5 2.7 %collective-permute-start.9 = (bf16[32,9,640]{2,0,1:T(8,128)(2,1)S(1)}, bf16[32,9,640]{2,0,1:T(8,128)(2,1)S(1)}, u32[]{:S(2)}, u32[]{:S(2)}) collective-permute-start(bf16[32,9,640]{2,0,1:T(8,128)(2,1)S(1)} %slice.33), channel_id=1, source_target_pairs={{0,3},{1,0},{2,1},{3,2},{4,7},{5,4},{6,5},{7,6},{8,11},{9,8},{10,9... | collective-permute-start | bytes 1105928 | tf_op jit(solution)/shard_map/ppermute | solution.py:166
  103.1 2.0 %fusion.12 = f32[64,9,2,384]{3,0,2,1:T(8,128)S(1)} fusion(bf16[1,640,2,384]{3,2,1,0:T(2,128)(2,1)S(1)} %get-tuple-element.9, bf16[64,9,640]{2,0,1:T(8,128)(2,1)} %collective-permute-done.6), kind=kOutput, calls=%fused_computation.21 | convolution fusion | flops 566231040 | bytes 3489792 | tf_op jit(solution)/shard_map/snc,cgf->sngf/dot_general | solution.py:294
  105.1 3.5 %collective-permute-done.7 = bf16[32,9,640]{2,0,1:T(8,128)(2,1)S(1)} collective-permute-done((bf16[32,9,640]{2,0,1:T(8,128)(2,1)S(1)}, bf16[32,9,640]{2,0,1:T(8,128)(2,1)S(1)}, u32[]{:S(2)}, u32[]{:S(2)}) %collective-permute-start.7) | collective-permute-done | bytes 368672 | tf_op jit(solution)/shard_map/ppermute | solution.py:166
  109.5 2.1 %add_add_fusion = f32[64,9,2,384]{3,0,2,1:T(8,128)S(1)} fusion(f32[64,9,2,384]{3,0,2,1:T(8,128)S(1)} %fusion.11, f32[64,9,2,384]{3,0,2,1:T(8,128)S(1)} %fusion.13, f32[64,9,2,384]{3,0,2,1:T(8,128)S(1)} %fusion.12, bf16[1,640,2,384]{3,2,1,0:T(2,128)(2,1)S(1)} %get-tuple-element.7, bf16[64,9,640]{2,0,1:T(8,128)(2,1)} %collective-permute-done.8), kind=kOutput, calls=%fused_computation.6 | convolution fusion | flops 567558144 | bytes 8798208 | tf_op jit(solution)/shard_map/snc,cgf->sngf/dot_general | solution.py:294
  111.7 1.7 convolution_convert_fusion
  113.8 3.5 %collective-permute-start.14 = (bf16[32,9,640]{2,0,1:T(8,128)(2,1)S(1)}, bf16[32,9,640]{2,0,1:T(8,128)(2,1)S(1)}, u32[]{:S(2)}, u32[]{:S(2)}) collective-permute-start(bf16[32,9,640]{2,0,1:T(8,128)(2,1)S(1)} %get-tuple-element.15), channel_id=1, source_target_pairs={{0,3},{1,0},{2,1},{3,2},{4,7},{5,4},{6,5},{7,6},{8,11},{9,8},{10,9... | collective-permute-start | bytes 1105928 | tf_op jit(solution)/shard_map/ppermute | solution.py:166
  117.3 2.7 %collective-permute-start.11 = (bf16[64,9,640]{2,0,1:T(8,128)(2,1)S(1)}, bf16[64,9,640]{2,0,1:T(8,128)(2,1)S(1)}, u32[]{:S(2)}, u32[]{:S(2)}) collective-permute-start(bf16[64,9,640]{2,0,1:T(8,128)(2,1)S(1)} %get-tuple-element.12), channel_id=1, source_target_pairs={{0,3},{1,0},{2,1},{3,2},{4,7},{5,4},{6,5},{7,6},{8,11},{9,8},{10,9... | collective-permute-start | bytes 2211848 | tf_op jit(solution)/shard_map/ppermute | solution.py:166
  120.0 3.8 %collective-permute-done.12 = bf16[32,9,640]{2,0,1:T(8,128)(2,1)S(1)} collective-permute-done((bf16[32,9,640]{2,0,1:T(8,128)(2,1)S(1)}, bf16[32,9,640]{2,0,1:T(8,128)(2,1)S(1)}, u32[]{:S(2)}, u32[]{:S(2)}) %collective-permute-start.12) | collective-permute-done | bytes 368672 | tf_op jit(solution)/shard_map/ppermute | solution.py:166
  123.8 2.7 %collective-permute-start.15 = (bf16[32,9,640]{2,0,1:T(8,128)(2,1)S(1)}, bf16[32,9,640]{2,0,1:T(8,128)(2,1)S(1)}, u32[]{:S(2)}, u32[]{:S(2)}) collective-permute-start(bf16[32,9,640]{2,0,1:T(8,128)(2,1)S(1)} %collective-permute-done.14), channel_id=1, source_target_pairs={{0,3},{1,0},{2,1},{3,2},{4,7},{5,4},{6,5},{7,6},{8,11},{9,8},{10,9... | collective-permute-start | bytes 1105928 | tf_op jit(solution)/shard_map/ppermute | solution.py:166
  126.5 21.0 %collective-permute-done.13 = bf16[32,9,640]{2,0,1:T(8,128)(2,1)S(1)} collective-permute-done((bf16[32,9,640]{2,0,1:T(8,128)(2,1)S(1)}, bf16[32,9,640]{2,0,1:T(8,128)(2,1)S(1)}, u32[]{:S(2)}, u32[]{:S(2)}) %collective-permute-start.13) | collective-permute-done | bytes 368672 | tf_op jit(solution)/shard_map/ppermute | solution.py:166
  148.4 1.4 reshape.48
  149.8 9.6 %all-to-all-start.1 = ((bf16[64,45,128]{2,1,0:T(8,128)(2,1)}), bf16[64,45,128]{2,1,0:T(8,128)(2,1)S(1)}, u32[]{:S(2)}, u32[]{:S(2)}) async-start(bf16[64,45,128]{2,1,0:T(8,128)(2,1)} %reshape.48), calls=%async_computation.1 | async-start | bytes 1572864 | tf_op jit(solution)/shard_map/all_to_all | solution.py:184
  159.6 22.7 %all-to-all-done.1 = bf16[64,45,128]{2,1,0:T(8,128)(2,1)S(1)} async-done(((bf16[64,45,128]{2,1,0:T(8,128)(2,1)}), bf16[64,45,128]{2,1,0:T(8,128)(2,1)S(1)}, u32[]{:S(2)}, u32[]{:S(2)}) %all-to-all-start.1) | async-done | bytes 737312 | tf_op jit(solution)/shard_map/all_to_all | solution.py:184
  182.9 1.1 fusion.8
  (51 shorter events, 10.2 us)
Async XLA Ops:
  1.4 13.2 %copy-start = (bf16[640,2560]{1,0:T(8,128)(2,1)S(1)}, bf16[640,2560]{1,0:T(8,128)(2,1)}, u32[]{:S(2)}) copy-start(bf16[640,2560]{1,0:T(8,128)(2,1)} %param.18) | copy-start | bytes 9830404
  14.6 8.2 %copy-start.4 = (s32[64,6]{0,1:T(8,128)S(1)}, s32[64,6]{0,1:T(8,128)}, u32[]{:S(2)}) copy-start(s32[64,6]{0,1:T(8,128)} %param.20) | copy-start | bytes 4612
  16.2 0.8 copy-start.1
  17.1 6.4 %collective-permute-start = (f32[64,640]{1,0:T(8,128)S(1)}, f32[64,640]{1,0:T(8,128)S(1)}, u32[]{:S(2)}, u32[]{:S(2)}) collective-permute-start(f32[64,640]{1,0:T(8,128)S(1)} %get-tuple-element.16), channel_id=1, source_target_pairs={{0,1},{1,2},{2,3},{3,0},{4,5},{5,6},{6,7},{7,4},{8,9},{9,10},{10,1... | collective-permute-start | bytes 491528 | tf_op jit(solution)/shard_map/ppermute | solution.py:166
  19.2 9.6 %collective-permute-start.1 = (f32[64,640]{1,0:T(8,128)S(1)}, f32[64,640]{1,0:T(8,128)S(1)}, u32[]{:S(2)}, u32[]{:S(2)}) collective-permute-start(f32[64,640]{1,0:T(8,128)S(1)} %get-tuple-element.18), channel_id=1, source_target_pairs={{0,2},{1,3},{2,0},{3,1},{4,6},{5,7},{6,4},{7,5},{8,10},{9,11},{10,... | collective-permute-start | bytes 491528 | tf_op jit(solution)/shard_map/ppermute | solution.py:166
  21.7 7.2 %collective-permute-start.2 = (f32[64,640]{1,0:T(8,128)S(1)}, f32[64,640]{1,0:T(8,128)S(1)}, u32[]{:S(2)}, u32[]{:S(2)}) collective-permute-start(f32[64,640]{1,0:T(8,128)S(1)} %get-tuple-element.17), channel_id=1, source_target_pairs={{0,3},{1,0},{2,1},{3,2},{4,7},{5,4},{6,5},{7,6},{8,11},{9,8},{10,9... | collective-permute-start | bytes 491528 | tf_op jit(solution)/shard_map/ppermute | solution.py:166
  30.0 3.7 %collective-permute-start.3 = (f32[64,1]{0,1:T(1,128)S(1)}, f32[64,1]{0,1:T(1,128)S(1)}, u32[]{:S(2)}, u32[]{:S(2)}) collective-permute-start(f32[64,1]{0,1:T(1,128)S(1)} %bitcast.90), channel_id=1, source_target_pairs={{0,1},{1,2},{2,3},{3,0},{4,5},{5,6},{6,7},{7,4},{8,9},{9,10},{10,1... | collective-permute-start | bytes 776 | tf_op jit(solution)/shard_map/ppermute | solution.py:166
  31.0 3.7 %collective-permute-start.5 = (f32[64,1]{0,1:T(1,128)S(1)}, f32[64,1]{0,1:T(1,128)S(1)}, u32[]{:S(2)}, u32[]{:S(2)}) collective-permute-start(f32[64,1]{0,1:T(1,128)S(1)} %bitcast.91), channel_id=1, source_target_pairs={{0,3},{1,0},{2,1},{3,2},{4,7},{5,4},{6,5},{7,6},{8,11},{9,8},{10,9... | collective-permute-start | bytes 776 | tf_op jit(solution)/shard_map/ppermute | solution.py:166
  33.7 3.6 %collective-permute-start.4 = (f32[64,1]{0,1:T(1,128)S(1)}, f32[64,1]{0,1:T(1,128)S(1)}, u32[]{:S(2)}, u32[]{:S(2)}) collective-permute-start(f32[64,1]{0,1:T(1,128)S(1)} %collective-permute-done.3), channel_id=1, source_target_pairs={{0,1},{1,2},{2,3},{3,0},{4,5},{5,6},{6,7},{7,4},{8,9},{9,10},{10,1... | collective-permute-start | bytes 776 | tf_op jit(solution)/shard_map/ppermute | solution.py:166
  77.2 3.7 %copy-start.2 = (bf16[1,384,2560]{2,1,0:T(8,128)(2,1)S(1)}, bf16[1,384,2560]{2,1,0:T(8,128)(2,1)}, u32[]{:S(2)}) copy-start(bf16[1,384,2560]{2,1,0:T(8,128)(2,1)} %param.23) | copy-start | bytes 5898244
  78.2 19.2 %collective-permute-start.6 = (bf16[64,9,640]{2,0,1:T(8,128)(2,1)}, bf16[64,9,640]{2,0,1:T(8,128)(2,1)}, u32[]{:S(2)}, u32[]{:S(2)}) collective-permute-start(bf16[64,9,640]{2,0,1:T(8,128)(2,1)} %copy.58), channel_id=1, source_target_pairs={{0,1},{1,2},{2,3},{3,0},{4,5},{5,6},{6,7},{7,4},{8,9},{9,10},{10,1... | collective-permute-start | bytes 2211848 | tf_op jit(solution)/shard_map/ppermute | solution.py:166
  78.2 20.3 %collective-permute-start.8 = (bf16[64,9,640]{2,0,1:T(8,128)(2,1)}, bf16[64,9,640]{2,0,1:T(8,128)(2,1)}, u32[]{:S(2)}, u32[]{:S(2)}) collective-permute-start(bf16[64,9,640]{2,0,1:T(8,128)(2,1)} %copy.58), channel_id=1, source_target_pairs={{0,3},{1,0},{2,1},{3,2},{4,7},{5,4},{6,5},{7,6},{8,11},{9,8},{10,9... | collective-permute-start | bytes 2211848 | tf_op jit(solution)/shard_map/ppermute | solution.py:166
  98.4 10.2 %collective-permute-start.7 = (bf16[32,9,640]{2,0,1:T(8,128)(2,1)S(1)}, bf16[32,9,640]{2,0,1:T(8,128)(2,1)S(1)}, u32[]{:S(2)}, u32[]{:S(2)}) collective-permute-start(bf16[32,9,640]{2,0,1:T(8,128)(2,1)S(1)} %slice.32), channel_id=1, source_target_pairs={{0,1},{1,2},{2,3},{3,0},{4,5},{5,6},{6,7},{7,4},{8,9},{9,10},{10,1... | collective-permute-start | bytes 1105928 | tf_op jit(solution)/shard_map/ppermute | solution.py:166
  99.5 9.1 %collective-permute-start.9 = (bf16[32,9,640]{2,0,1:T(8,128)(2,1)S(1)}, bf16[32,9,640]{2,0,1:T(8,128)(2,1)S(1)}, u32[]{:S(2)}, u32[]{:S(2)}) collective-permute-start(bf16[32,9,640]{2,0,1:T(8,128)(2,1)S(1)} %slice.33), channel_id=1, source_target_pairs={{0,3},{1,0},{2,1},{3,2},{4,7},{5,4},{6,5},{7,6},{8,11},{9,8},{10,9... | collective-permute-start | bytes 1105928 | tf_op jit(solution)/shard_map/ppermute | solution.py:166
  109.5 2.2 %copy-start.3 = (bf16[384,4,640]{2,1,0:T(4,128)(2,1)S(1)}, bf16[384,4,640]{2,1,0:T(4,128)(2,1)}, u32[]{:S(2)}) copy-start(bf16[384,4,640]{2,1,0:T(4,128)(2,1)} %reshape_squeeze.3) | copy-start | bytes 5898244
  113.7 10.1 %collective-permute-start.12 = (bf16[32,9,640]{2,0,1:T(8,128)(2,1)S(1)}, bf16[32,9,640]{2,0,1:T(8,128)(2,1)S(1)}, u32[]{:S(2)}, u32[]{:S(2)}) collective-permute-start(bf16[32,9,640]{2,0,1:T(8,128)(2,1)S(1)} %get-tuple-element.14), channel_id=1, source_target_pairs={{0,1},{1,2},{2,3},{3,0},{4,5},{5,6},{6,7},{7,4},{8,9},{9,10},{10,1... | collective-permute-start | bytes 1105928 | tf_op jit(solution)/shard_map/ppermute | solution.py:166
  113.8 10.0 %collective-permute-start.14 = (bf16[32,9,640]{2,0,1:T(8,128)(2,1)S(1)}, bf16[32,9,640]{2,0,1:T(8,128)(2,1)S(1)}, u32[]{:S(2)}, u32[]{:S(2)}) collective-permute-start(bf16[32,9,640]{2,0,1:T(8,128)(2,1)S(1)} %get-tuple-element.15), channel_id=1, source_target_pairs={{0,3},{1,0},{2,1},{3,2},{4,7},{5,4},{6,5},{7,6},{8,11},{9,8},{10,9... | collective-permute-start | bytes 1105928 | tf_op jit(solution)/shard_map/ppermute | solution.py:166
  117.3 30.2 %collective-permute-start.10 = (bf16[64,9,640]{2,0,1:T(8,128)(2,1)S(1)}, bf16[64,9,640]{2,0,1:T(8,128)(2,1)S(1)}, u32[]{:S(2)}, u32[]{:S(2)}) collective-permute-start(bf16[64,9,640]{2,0,1:T(8,128)(2,1)S(1)} %get-tuple-element.13), channel_id=1, source_target_pairs={{0,1},{1,2},{2,3},{3,0},{4,5},{5,6},{6,7},{7,4},{8,9},{9,10},{10,1... | collective-permute-start | bytes 2211848 | tf_op jit(solution)/shard_map/ppermute | solution.py:166
  117.3 30.2 %collective-permute-start.11 = (bf16[64,9,640]{2,0,1:T(8,128)(2,1)S(1)}, bf16[64,9,640]{2,0,1:T(8,128)(2,1)S(1)}, u32[]{:S(2)}, u32[]{:S(2)}) collective-permute-start(bf16[64,9,640]{2,0,1:T(8,128)(2,1)S(1)} %get-tuple-element.12), channel_id=1, source_target_pairs={{0,3},{1,0},{2,1},{3,2},{4,7},{5,4},{6,5},{7,6},{8,11},{9,8},{10,9... | collective-permute-start | bytes 2211848 | tf_op jit(solution)/shard_map/ppermute | solution.py:166
  123.8 23.7 %collective-permute-start.13 = (bf16[32,9,640]{2,0,1:T(8,128)(2,1)S(1)}, bf16[32,9,640]{2,0,1:T(8,128)(2,1)S(1)}, u32[]{:S(2)}, u32[]{:S(2)}) collective-permute-start(bf16[32,9,640]{2,0,1:T(8,128)(2,1)S(1)} %collective-permute-done.12), channel_id=1, source_target_pairs={{0,1},{1,2},{2,3},{3,0},{4,5},{5,6},{6,7},{7,4},{8,9},{9,10},{10,1... | collective-permute-start | bytes 1105928 | tf_op jit(solution)/shard_map/ppermute | solution.py:166
  123.8 23.7 %collective-permute-start.15 = (bf16[32,9,640]{2,0,1:T(8,128)(2,1)S(1)}, bf16[32,9,640]{2,0,1:T(8,128)(2,1)S(1)}, u32[]{:S(2)}, u32[]{:S(2)}) collective-permute-start(bf16[32,9,640]{2,0,1:T(8,128)(2,1)S(1)} %collective-permute-done.14), channel_id=1, source_target_pairs={{0,3},{1,0},{2,1},{3,2},{4,7},{5,4},{6,5},{7,6},{8,11},{9,8},{10,9... | collective-permute-start | bytes 1105928 | tf_op jit(solution)/shard_map/ppermute | solution.py:166
  148.4 11.0 %copy-start.5 = (f32[64,6]{0,1:T(8,128)S(1)}, f32[64,6]{0,1:T(8,128)}, u32[]{:S(2)}) copy-start(f32[64,6]{0,1:T(8,128)} %param.21) | copy-start | bytes 4612
  149.8 32.5 %all-to-all-start.1 = ((bf16[64,45,128]{2,1,0:T(8,128)(2,1)}), bf16[64,45,128]{2,1,0:T(8,128)(2,1)S(1)}, u32[]{:S(2)}, u32[]{:S(2)}) async-start(bf16[64,45,128]{2,1,0:T(8,128)(2,1)} %reshape.48), calls=%async_computation.1 | async-start | bytes 1572864 | tf_op jit(solution)/shard_map/all_to_all | solution.py:184

commit v6 on v4

--- a/solution.py
+++ b/solution.py
@@ -240,7 +240,7 @@
     partial_proj = jnp.einsum(
         "rk,kuc->urc", attn, split_weight, preferred_element_type=jnp.float32
     )
-    summed = ring_reduce_scatter(partial_proj, "tensor", tensor_size, tensor_index)
+    summed = ring_reduce_scatter_two_step(partial_proj, "tensor", tensor_size, tensor_index)
     residual_share = lax.dynamic_slice_in_dim(residual, share_start, share_width, 1)
     state = residual_share.astype(jnp.float32) + summed
     square_sum = sum(ring_all_gather(jnp.sum(state * state, axis=1, keepdims=True), "tensor", tensor_size))

time: 183 us -> 185 us (1.011)
  starting transfers between devices: 33.9 us -> 36.5 us
    ppermute x16 -> x19, starting transfers between devices: 24.4 us -> 26.9 us  [ring_shift(): lax.ppermute(x, axis_name, [(i, (i + shift) % size) for i in range(size)])]
    ppermute x16 -> x19, waiting for transfers between devices: 44.1 us -> 43 us  [ring_shift(): lax.ppermute(x, axis_name, [(i, (i + shift) % size) for i in range(size)])]
  transfers between devices with their start and end apart: 17 -> 20, of which waited for: 8 -> 8; matrix products, arithmetic and copies ran while one was open for 7% -> 7% of each run, Pallas kernels for 0% -> 0%
where the time goes in v6:
time: 185 us; the launch traced here: 184 us
  waiting for transfers between devices  65.7 us (36%)
  blocking collectives  38.8 us (21%)
  starting transfers between devices  36.5 us (20%)
  local copies, waits for them, and re-layouts  16.8 us (9%)
  Pallas kernels  13.2 us (7%)
  matrix products  10.9 us (6%)
  other arithmetic  1.91 us (1%)
    ppermute x19, waiting for transfers between devices, ring_shift(): lax.ppermute(x, axis_name, [(i, (i + shift) % size) for i in range(size)])  43 us
    all_to_all x1, blocking collectives, dense_all_to_all(): lax.all_to_all(flat, axis_name, split_axis=0, concat_axis=0, tiled=True)  38.8 us
    ppermute x19, starting transfers between devices, ring_shift(): lax.ppermute(x, axis_name, [(i, (i + shift) % size) for i in range(size)])  26.9 us
    all_to_all x1, waiting for transfers between devices, dense_all_to_all(): lax.all_to_all(flat, axis_name, split_axis=0, concat_axis=0, tiled=True)  22.7 us
    pallas_call x1, Pallas kernels, local_attention(): pl.pallas_call(attention_kernel, out_shape=jax.ShapeDtypeStruct(query.sha...  13.2 us
    all_to_all x1, starting transfers between devices, dense_all_to_all(): lax.all_to_all(flat, axis_name, split_axis=0, concat_axis=0, tiled=True)  9.55 us
    dot_general x4, matrix products, per_device(): jnp.einsum('snc,cgf->sngf', piece, weight, preferred_element_type=jnp.flo...  5.84 us
    dynamic_slice x1, local copies, waits for them, and re-layouts, per_device(): lax.dynamic_index_in_dim(split_w1, (tensor_index - shift) % tensor_size,...  4.22 us
  transfers between devices with their start and end apart: 20, of which 8 were waited for; matrix products, arithmetic and copies ran while one was open for 7% of the time, Pallas kernels for 0%

profile of v6, /device:TPU:1, one launch (start us, length us, event | category | flops | bytes accessed | tf_op | source)
XLA Modules:
  0.0 184.1 jit_solution(3605408832797192837)
XLA Ops:
  0.0 1.4 copy.52.table_ref
  1.4 13.2 %shard_map.118 = bf16[64,640]{1,0:T(8,128)(2,1)} custom-call(s32[64,32]{1,0:T(8,128)} %copy.52.table_ref, s32[64]{0:T(128)} %len_ref.1, s32[1]{0:T(128)} %bitcast.base_ref, bf16[64,640]{1,0:T(8,128)(2,1)} %q_ref.1, bf16[2,64,128]{2,1,0:T(8,128)(2,1)} %new_kv_ref.1, bf16[2,95,128,128]{3,2,1,0:T(8,128)(2,1)} %kv_hbm.1), custom_call_target="tpu_custom_call" | custom-call | flops 335544320 | bytes 4194304 | tf_op jit(solution)/shard_map/pallas_call | solution.py:145
  14.7 1.6 fusion
  17.2 2.1 %collective-permute-start.2 = (f32[32,640]{1,0:T(8,128)S(1)}, f32[32,640]{1,0:T(8,128)S(1)}, u32[]{:S(2)}, u32[]{:S(2)}) collective-permute-start(f32[32,640]{1,0:T(8,128)S(1)} %get-tuple-element.19), channel_id=1, source_target_pairs={{0,1},{1,2},{2,3},{3,0},{4,5},{5,6},{6,7},{7,4},{8,9},{9,10},{10,1... | collective-permute-start | bytes 245768 | tf_op jit(solution)/shard_map/ppermute | solution.py:166
  19.3 1.4 collective-permute-start.4
  20.7 2.6 %collective-permute-start.1 = (f32[64,640]{1,0:T(8,128)S(1)}, f32[64,640]{1,0:T(8,128)S(1)}, u32[]{:S(2)}, u32[]{:S(2)}) collective-permute-start(f32[64,640]{1,0:T(8,128)S(1)} %get-tuple-element.18), channel_id=1, source_target_pairs={{0,3},{1,0},{2,1},{3,2},{4,7},{5,4},{6,5},{7,6},{8,11},{9,8},{10,9... | collective-permute-start | bytes 491528 | tf_op jit(solution)/shard_map/ppermute | solution.py:166
  24.1 2.7 %collective-permute-start.5 = (f32[32,640]{1,0:T(8,128)S(1)}, f32[32,640]{1,0:T(8,128)S(1)}, u32[]{:S(2)}, u32[]{:S(2)}) collective-permute-start(f32[32,640]{1,0:T(8,128)S(1)} %collective-permute-done.4), channel_id=1, source_target_pairs={{0,3},{1,0},{2,1},{3,2},{4,7},{5,4},{6,5},{7,6},{8,11},{9,8},{10,9... | collective-permute-start | bytes 245768 | tf_op jit(solution)/shard_map/ppermute | solution.py:166
  26.7 2.9 %collective-permute-done.3 = f32[32,640]{1,0:T(8,128)S(1)} collective-permute-done((f32[32,640]{1,0:T(8,128)S(1)}, f32[32,640]{1,0:T(8,128)S(1)}, u32[]{:S(2)}, u32[]{:S(2)}) %collective-permute-start.3) | collective-permute-done | bytes 81952 | tf_op jit(solution)/shard_map/ppermute | solution.py:166
  29.6 1.1 multiply_reduce_fusion
  30.8 3.6 %collective-permute-start.7 = (f32[64,1]{0,1:T(1,128)S(1)}, f32[64,1]{0,1:T(1,128)S(1)}, u32[]{:S(2)}, u32[]{:S(2)}) collective-permute-start(f32[64,1]{0,1:T(1,128)S(1)} %bitcast.93), channel_id=1, source_target_pairs={{0,2},{1,3},{2,0},{3,1},{4,6},{5,7},{6,4},{7,5},{8,10},{9,11},{10,... | collective-permute-start | bytes 776 | tf_op jit(solution)/shard_map/ppermute | solution.py:166
  35.4 1.4 collective-permute-done.8
  37.9 38.8 %all_to_all.10 = bf16[64,45,128]{2,1,0:T(8,128)(2,1)S(1)} all-to-all(bf16[64,45,128]{2,1,0:T(8,128)(2,1)S(1)} %reshape_reshape.6), channel_id=1, replica_groups=mesh['dp'=64,'tensor'=4] {'dp'}, dimensions={0} | all-to-all | bytes 1474560 | tf_op jit(solution)/shard_map/all_to_all | solution.py:184
  78.3 2.7 %collective-permute-start.11 = (bf16[64,9,640]{2,0,1:T(8,128)(2,1)}, bf16[64,9,640]{2,0,1:T(8,128)(2,1)}, u32[]{:S(2)}, u32[]{:S(2)}) collective-permute-start(bf16[64,9,640]{2,0,1:T(8,128)(2,1)} %copy.58), channel_id=1, source_target_pairs={{0,3},{1,0},{2,1},{3,2},{4,7},{5,4},{6,5},{7,6},{8,11},{9,8},{10,9... | collective-permute-start | bytes 2211848 | tf_op jit(solution)/shard_map/ppermute | solution.py:166
  81.0 2.0 %reshape_squeeze.3 = bf16[384,4,640]{2,1,0:T(4,128)(2,1)} reshape(bf16[1,384,2560]{2,1,0:T(8,128)(2,1)S(1)} %copy-done.2) | data formatting | bytes 3932160 | tf_op jit(solution)/shard_map/reshape;squeeze | solution.py:276
  83.0 4.2 %constant_dynamic-slice_fusion = (bf16[1,640,2,384]{3,2,1,0:T(2,128)(2,1)S(1)}, bf16[1,640,2,384]{3,2,1,0:T(2,128)(2,1)S(1)}, bf16[1,640,2,384]{3,2,1,0:T(2,128)(2,1)S(1)}, bf16[1,640,2,384]{3,2,1,0:T(2,128)(2,1)S(1)}) fusion(bf16[4,640,2,384]{3,2,1,0:T(2,128)(2,1)} %bitcast.90, s32[]{:T(128)S(6)} %select_n.93, s32[]{:T(128)S(6)} %select_n.91, ...), kind=kLoop, calls=%fused_computation.60 | loop fusion | bytes 7864336 | tf_op jit(solution)/shard_map/jit(dynamic_index_in_dim)/dynamic_slice | solution.py:287
  87.2 10.3 %collective-permute-done.9 = bf16[64,9,640]{2,0,1:T(8,128)(2,1)} collective-permute-done((bf16[64,9,640]{2,0,1:T(8,128)(2,1)}, bf16[64,9,640]{2,0,1:T(8,128)(2,1)}, u32[]{:S(2)}, u32[]{:S(2)}) %collective-permute-start.9) | collective-permute-done | bytes 737312 | tf_op jit(solution)/shard_map/ppermute | solution.py:166
  97.5 1.0 slice.50
  98.6 1.0 slice.51
  99.7 2.7 %collective-permute-start.12 = (bf16[32,9,640]{2,0,1:T(8,128)(2,1)S(1)}, bf16[32,9,640]{2,0,1:T(8,128)(2,1)S(1)}, u32[]{:S(2)}, u32[]{:S(2)}) collective-permute-start(bf16[32,9,640]{2,0,1:T(8,128)(2,1)S(1)} %slice.51), channel_id=1, source_target_pairs={{0,3},{1,0},{2,1},{3,2},{4,7},{5,4},{6,5},{7,6},{8,11},{9,8},{10,9... | collective-permute-start | bytes 1105928 | tf_op jit(solution)/shard_map/ppermute | solution.py:166
  103.3 2.0 %fusion.12 = f32[64,9,2,384]{3,0,2,1:T(8,128)S(1)} fusion(bf16[1,640,2,384]{3,2,1,0:T(2,128)(2,1)S(1)} %get-tuple-element.9, bf16[64,9,640]{2,0,1:T(8,128)(2,1)} %collective-permute-done.9), kind=kOutput, calls=%fused_computation.21 | convolution fusion | flops 566231040 | bytes 3489792 | tf_op jit(solution)/shard_map/snc,cgf->sngf/dot_general | solution.py:290
  105.2 3.5 %collective-permute-done.10 = bf16[32,9,640]{2,0,1:T(8,128)(2,1)S(1)} collective-permute-done((bf16[32,9,640]{2,0,1:T(8,128)(2,1)S(1)}, bf16[32,9,640]{2,0,1:T(8,128)(2,1)S(1)}, u32[]{:S(2)}, u32[]{:S(2)}) %collective-permute-start.10) | collective-permute-done | bytes 368672 | tf_op jit(solution)/shard_map/ppermute | solution.py:166
  109.7 2.1 %add_add_fusion = f32[64,9,2,384]{3,0,2,1:T(8,128)S(1)} fusion(f32[64,9,2,384]{3,0,2,1:T(8,128)S(1)} %fusion.11, f32[64,9,2,384]{3,0,2,1:T(8,128)S(1)} %fusion.13, f32[64,9,2,384]{3,0,2,1:T(8,128)S(1)} %fusion.12, bf16[1,640,2,384]{3,2,1,0:T(2,128)(2,1)S(1)} %get-tuple-element.7, bf16[64,9,640]{2,0,1:T(8,128)(2,1)} %collective-permute-done.11), kind=kOutput, calls=%fused_computation.6 | convolution fusion | flops 567558144 | bytes 8798208 | tf_op jit(solution)/shard_map/snc,cgf->sngf/dot_general | solution.py:290
  111.8 1.7 convolution_convert_fusion
  113.9 3.5 %collective-permute-start.17 = (bf16[32,9,640]{2,0,1:T(8,128)(2,1)S(1)}, bf16[32,9,640]{2,0,1:T(8,128)(2,1)S(1)}, u32[]{:S(2)}, u32[]{:S(2)}) collective-permute-start(bf16[32,9,640]{2,0,1:T(8,128)(2,1)S(1)} %get-tuple-element.15), channel_id=1, source_target_pairs={{0,3},{1,0},{2,1},{3,2},{4,7},{5,4},{6,5},{7,6},{8,11},{9,8},{10,9... | collective-permute-start | bytes 1105928 | tf_op jit(solution)/shard_map/ppermute | solution.py:166
  117.4 2.7 %collective-permute-start.14 = (bf16[64,9,640]{2,0,1:T(8,128)(2,1)S(1)}, bf16[64,9,640]{2,0,1:T(8,128)(2,1)S(1)}, u32[]{:S(2)}, u32[]{:S(2)}) collective-permute-start(bf16[64,9,640]{2,0,1:T(8,128)(2,1)S(1)} %get-tuple-element.12), channel_id=1, source_target_pairs={{0,3},{1,0},{2,1},{3,2},{4,7},{5,4},{6,5},{7,6},{8,11},{9,8},{10,9... | collective-permute-start | bytes 2211848 | tf_op jit(solution)/shard_map/ppermute | solution.py:166
  120.1 3.8 %collective-permute-done.15 = bf16[32,9,640]{2,0,1:T(8,128)(2,1)S(1)} collective-permute-done((bf16[32,9,640]{2,0,1:T(8,128)(2,1)S(1)}, bf16[32,9,640]{2,0,1:T(8,128)(2,1)S(1)}, u32[]{:S(2)}, u32[]{:S(2)}) %collective-permute-start.15) | collective-permute-done | bytes 368672 | tf_op jit(solution)/shard_map/ppermute | solution.py:166
  123.9 2.7 %collective-permute-start.18 = (bf16[32,9,640]{2,0,1:T(8,128)(2,1)S(1)}, bf16[32,9,640]{2,0,1:T(8,128)(2,1)S(1)}, u32[]{:S(2)}, u32[]{:S(2)}) collective-permute-start(bf16[32,9,640]{2,0,1:T(8,128)(2,1)S(1)} %collective-permute-done.17), channel_id=1, source_target_pairs={{0,3},{1,0},{2,1},{3,2},{4,7},{5,4},{6,5},{7,6},{8,11},{9,8},{10,9... | collective-permute-start | bytes 1105928 | tf_op jit(solution)/shard_map/ppermute | solution.py:166
  126.6 21.0 %collective-permute-done.16 = bf16[32,9,640]{2,0,1:T(8,128)(2,1)S(1)} collective-permute-done((bf16[32,9,640]{2,0,1:T(8,128)(2,1)S(1)}, bf16[32,9,640]{2,0,1:T(8,128)(2,1)S(1)}, u32[]{:S(2)}, u32[]{:S(2)}) %collective-permute-start.16) | collective-permute-done | bytes 368672 | tf_op jit(solution)/shard_map/ppermute | solution.py:166
  148.5 1.4 reshape.49
  149.9 9.6 %all-to-all-start.1 = ((bf16[64,45,128]{2,1,0:T(8,128)(2,1)}), bf16[64,45,128]{2,1,0:T(8,128)(2,1)S(1)}, u32[]{:S(2)}, u32[]{:S(2)}) async-start(bf16[64,45,128]{2,1,0:T(8,128)(2,1)} %reshape.49), calls=%async_computation.1 | async-start | bytes 1572864 | tf_op jit(solution)/shard_map/all_to_all | solution.py:184
  159.7 22.7 %all-to-all-done.1 = bf16[64,45,128]{2,1,0:T(8,128)(2,1)S(1)} async-done(((bf16[64,45,128]{2,1,0:T(8,128)(2,1)}), bf16[64,45,128]{2,1,0:T(8,128)(2,1)S(1)}, u32[]{:S(2)}, u32[]{:S(2)}) %all-to-all-start.1) | async-done | bytes 737312 | tf_op jit(solution)/shard_map/all_to_all | solution.py:184
  183.0 1.1 fusion.8
  (58 shorter events, 9.5 us)
Async XLA Ops:
  1.4 13.2 %copy-start = (bf16[640,2560]{1,0:T(8,128)(2,1)S(1)}, bf16[640,2560]{1,0:T(8,128)(2,1)}, u32[]{:S(2)}) copy-start(bf16[640,2560]{1,0:T(8,128)(2,1)} %param.18) | copy-start | bytes 9830404
  14.6 8.7 %copy-start.4 = (s32[64,6]{0,1:T(8,128)S(1)}, s32[64,6]{0,1:T(8,128)}, u32[]{:S(2)}) copy-start(s32[64,6]{0,1:T(8,128)} %param.20) | copy-start | bytes 4612
  16.2 0.9 copy-start.1
  17.2 6.8 %collective-permute-start.2 = (f32[32,640]{1,0:T(8,128)S(1)}, f32[32,640]{1,0:T(8,128)S(1)}, u32[]{:S(2)}, u32[]{:S(2)}) collective-permute-start(f32[32,640]{1,0:T(8,128)S(1)} %get-tuple-element.19), channel_id=1, source_target_pairs={{0,1},{1,2},{2,3},{3,0},{4,5},{5,6},{6,7},{7,4},{8,9},{9,10},{10,1... | collective-permute-start | bytes 245768 | tf_op jit(solution)/shard_map/ppermute | solution.py:166
  19.3 4.8 %collective-permute-start.4 = (f32[32,640]{1,0:T(8,128)S(1)}, f32[32,640]{1,0:T(8,128)S(1)}, u32[]{:S(2)}, u32[]{:S(2)}) collective-permute-start(f32[32,640]{1,0:T(8,128)S(1)} %get-tuple-element.20), channel_id=1, source_target_pairs={{0,3},{1,0},{2,1},{3,2},{4,7},{5,4},{6,5},{7,6},{8,11},{9,8},{10,9... | collective-permute-start | bytes 245768 | tf_op jit(solution)/shard_map/ppermute | solution.py:166
  20.6 8.9 %collective-permute-start = (f32[64,640]{1,0:T(8,128)S(1)}, f32[64,640]{1,0:T(8,128)S(1)}, u32[]{:S(2)}, u32[]{:S(2)}) collective-permute-start(f32[64,640]{1,0:T(8,128)S(1)} %get-tuple-element.16), channel_id=1, source_target_pairs={{0,1},{1,2},{2,3},{3,0},{4,5},{5,6},{6,7},{7,4},{8,9},{9,10},{10,1... | collective-permute-start | bytes 491528 | tf_op jit(solution)/shard_map/ppermute | solution.py:166
  20.7 8.8 %collective-permute-start.1 = (f32[64,640]{1,0:T(8,128)S(1)}, f32[64,640]{1,0:T(8,128)S(1)}, u32[]{:S(2)}, u32[]{:S(2)}) collective-permute-start(f32[64,640]{1,0:T(8,128)S(1)} %get-tuple-element.18), channel_id=1, source_target_pairs={{0,3},{1,0},{2,1},{3,2},{4,7},{5,4},{6,5},{7,6},{8,11},{9,8},{10,9... | collective-permute-start | bytes 491528 | tf_op jit(solution)/shard_map/ppermute | solution.py:166
  24.0 5.6 %collective-permute-start.3 = (f32[32,640]{1,0:T(8,128)S(1)}, f32[32,640]{1,0:T(8,128)S(1)}, u32[]{:S(2)}, u32[]{:S(2)}) collective-permute-start(f32[32,640]{1,0:T(8,128)S(1)} %collective-permute-done.2), channel_id=1, source_target_pairs={{0,1},{1,2},{2,3},{3,0},{4,5},{5,6},{6,7},{7,4},{8,9},{9,10},{10,1... | collective-permute-start | bytes 245768 | tf_op jit(solution)/shard_map/ppermute | solution.py:166
  24.1 5.5 %collective-permute-start.5 = (f32[32,640]{1,0:T(8,128)S(1)}, f32[32,640]{1,0:T(8,128)S(1)}, u32[]{:S(2)}, u32[]{:S(2)}) collective-permute-start(f32[32,640]{1,0:T(8,128)S(1)} %collective-permute-done.4), channel_id=1, source_target_pairs={{0,3},{1,0},{2,1},{3,2},{4,7},{5,4},{6,5},{7,6},{8,11},{9,8},{10,9... | collective-permute-start | bytes 245768 | tf_op jit(solution)/shard_map/ppermute | solution.py:166
  30.7 4.7 %collective-permute-start.6 = (f32[64,1]{0,1:T(1,128)S(1)}, f32[64,1]{0,1:T(1,128)S(1)}, u32[]{:S(2)}, u32[]{:S(2)}) collective-permute-start(f32[64,1]{0,1:T(1,128)S(1)} %bitcast.92), channel_id=1, source_target_pairs={{0,1},{1,2},{2,3},{3,0},{4,5},{5,6},{6,7},{7,4},{8,9},{9,10},{10,1... | collective-permute-start | bytes 776 | tf_op jit(solution)/shard_map/ppermute | solution.py:166
  30.8 4.6 %collective-permute-start.7 = (f32[64,1]{0,1:T(1,128)S(1)}, f32[64,1]{0,1:T(1,128)S(1)}, u32[]{:S(2)}, u32[]{:S(2)}) collective-permute-start(f32[64,1]{0,1:T(1,128)S(1)} %bitcast.93), channel_id=1, source_target_pairs={{0,2},{1,3},{2,0},{3,1},{4,6},{5,7},{6,4},{7,5},{8,10},{9,11},{10,... | collective-permute-start | bytes 776 | tf_op jit(solution)/shard_map/ppermute | solution.py:166
  34.4 2.4 %collective-permute-start.8 = (f32[64,1]{0,1:T(1,128)S(1)}, f32[64,1]{0,1:T(1,128)S(1)}, u32[]{:S(2)}, u32[]{:S(2)}) collective-permute-start(f32[64,1]{0,1:T(1,128)S(1)} %bitcast.94), channel_id=1, source_target_pairs={{0,3},{1,0},{2,1},{3,2},{4,7},{5,4},{6,5},{7,6},{8,11},{9,8},{10,9... | collective-permute-start | bytes 776 | tf_op jit(solution)/shard_map/ppermute | solution.py:166
  77.3 3.7 %copy-start.2 = (bf16[1,384,2560]{2,1,0:T(8,128)(2,1)S(1)}, bf16[1,384,2560]{2,1,0:T(8,128)(2,1)}, u32[]{:S(2)}) copy-start(bf16[1,384,2560]{2,1,0:T(8,128)(2,1)} %param.23) | copy-start | bytes 5898244
  78.3 19.2 %collective-permute-start.9 = (bf16[64,9,640]{2,0,1:T(8,128)(2,1)}, bf16[64,9,640]{2,0,1:T(8,128)(2,1)}, u32[]{:S(2)}, u32[]{:S(2)}) collective-permute-start(bf16[64,9,640]{2,0,1:T(8,128)(2,1)} %copy.58), channel_id=1, source_target_pairs={{0,1},{1,2},{2,3},{3,0},{4,5},{5,6},{6,7},{7,4},{8,9},{9,10},{10,1... | collective-permute-start | bytes 2211848 | tf_op jit(solution)/shard_map/ppermute | solution.py:166
  78.3 20.3 %collective-permute-start.11 = (bf16[64,9,640]{2,0,1:T(8,128)(2,1)}, bf16[64,9,640]{2,0,1:T(8,128)(2,1)}, u32[]{:S(2)}, u32[]{:S(2)}) collective-permute-start(bf16[64,9,640]{2,0,1:T(8,128)(2,1)} %copy.58), channel_id=1, source_target_pairs={{0,3},{1,0},{2,1},{3,2},{4,7},{5,4},{6,5},{7,6},{8,11},{9,8},{10,9... | collective-permute-start | bytes 2211848 | tf_op jit(solution)/shard_map/ppermute | solution.py:166
  98.5 10.2 %collective-permute-start.10 = (bf16[32,9,640]{2,0,1:T(8,128)(2,1)S(1)}, bf16[32,9,640]{2,0,1:T(8,128)(2,1)S(1)}, u32[]{:S(2)}, u32[]{:S(2)}) collective-permute-start(bf16[32,9,640]{2,0,1:T(8,128)(2,1)S(1)} %slice.50), channel_id=1, source_target_pairs={{0,1},{1,2},{2,3},{3,0},{4,5},{5,6},{6,7},{7,4},{8,9},{9,10},{10,1... | collective-permute-start | bytes 1105928 | tf_op jit(solution)/shard_map/ppermute | solution.py:166
  99.7 9.1 %collective-permute-start.12 = (bf16[32,9,640]{2,0,1:T(8,128)(2,1)S(1)}, bf16[32,9,640]{2,0,1:T(8,128)(2,1)S(1)}, u32[]{:S(2)}, u32[]{:S(2)}) collective-permute-start(bf16[32,9,640]{2,0,1:T(8,128)(2,1)S(1)} %slice.51), channel_id=1, source_target_pairs={{0,3},{1,0},{2,1},{3,2},{4,7},{5,4},{6,5},{7,6},{8,11},{9,8},{10,9... | collective-permute-start | bytes 1105928 | tf_op jit(solution)/shard_map/ppermute | solution.py:166
  109.7 2.1 %copy-start.3 = (bf16[384,4,640]{2,1,0:T(4,128)(2,1)S(1)}, bf16[384,4,640]{2,1,0:T(4,128)(2,1)}, u32[]{:S(2)}) copy-start(bf16[384,4,640]{2,1,0:T(4,128)(2,1)} %reshape_squeeze.3) | copy-start | bytes 5898244
  113.9 10.1 %collective-permute-start.15 = (bf16[32,9,640]{2,0,1:T(8,128)(2,1)S(1)}, bf16[32,9,640]{2,0,1:T(8,128)(2,1)S(1)}, u32[]{:S(2)}, u32[]{:S(2)}) collective-permute-start(bf16[32,9,640]{2,0,1:T(8,128)(2,1)S(1)} %get-tuple-element.14), channel_id=1, source_target_pairs={{0,1},{1,2},{2,3},{3,0},{4,5},{5,6},{6,7},{7,4},{8,9},{9,10},{10,1... | collective-permute-start | bytes 1105928 | tf_op jit(solution)/shard_map/ppermute | solution.py:166
  113.9 10.0 %collective-permute-start.17 = (bf16[32,9,640]{2,0,1:T(8,128)(2,1)S(1)}, bf16[32,9,640]{2,0,1:T(8,128)(2,1)S(1)}, u32[]{:S(2)}, u32[]{:S(2)}) collective-permute-start(bf16[32,9,640]{2,0,1:T(8,128)(2,1)S(1)} %get-tuple-element.15), channel_id=1, source_target_pairs={{0,3},{1,0},{2,1},{3,2},{4,7},{5,4},{6,5},{7,6},{8,11},{9,8},{10,9... | collective-permute-start | bytes 1105928 | tf_op jit(solution)/shard_map/ppermute | solution.py:166
  117.4 30.2 %collective-permute-start.13 = (bf16[64,9,640]{2,0,1:T(8,128)(2,1)S(1)}, bf16[64,9,640]{2,0,1:T(8,128)(2,1)S(1)}, u32[]{:S(2)}, u32[]{:S(2)}) collective-permute-start(bf16[64,9,640]{2,0,1:T(8,128)(2,1)S(1)} %get-tuple-element.13), channel_id=1, source_target_pairs={{0,1},{1,2},{2,3},{3,0},{4,5},{5,6},{6,7},{7,4},{8,9},{9,10},{10,1... | collective-permute-start | bytes 2211848 | tf_op jit(solution)/shard_map/ppermute | solution.py:166
  117.4 30.2 %collective-permute-start.14 = (bf16[64,9,640]{2,0,1:T(8,128)(2,1)S(1)}, bf16[64,9,640]{2,0,1:T(8,128)(2,1)S(1)}, u32[]{:S(2)}, u32[]{:S(2)}) collective-permute-start(bf16[64,9,640]{2,0,1:T(8,128)(2,1)S(1)} %get-tuple-element.12), channel_id=1, source_target_pairs={{0,3},{1,0},{2,1},{3,2},{4,7},{5,4},{6,5},{7,6},{8,11},{9,8},{10,9... | collective-permute-start | bytes 2211848 | tf_op jit(solution)/shard_map/ppermute | solution.py:166
  123.9 23.7 %collective-permute-start.16 = (bf16[32,9,640]{2,0,1:T(8,128)(2,1)S(1)}, bf16[32,9,640]{2,0,1:T(8,128)(2,1)S(1)}, u32[]{:S(2)}, u32[]{:S(2)}) collective-permute-start(bf16[32,9,640]{2,0,1:T(8,128)(2,1)S(1)} %collective-permute-done.15), channel_id=1, source_target_pairs={{0,1},{1,2},{2,3},{3,0},{4,5},{5,6},{6,7},{7,4},{8,9},{9,10},{10,1... | collective-permute-start | bytes 1105928 | tf_op jit(solution)/shard_map/ppermute | solution.py:166
  123.9 23.7 %collective-permute-start.18 = (bf16[32,9,640]{2,0,1:T(8,128)(2,1)S(1)}, bf16[32,9,640]{2,0,1:T(8,128)(2,1)S(1)}, u32[]{:S(2)}, u32[]{:S(2)}) collective-permute-start(bf16[32,9,640]{2,0,1:T(8,128)(2,1)S(1)} %collective-permute-done.17), channel_id=1, source_target_pairs={{0,3},{1,0},{2,1},{3,2},{4,7},{5,4},{6,5},{7,6},{8,11},{9,8},{10,9... | collective-permute-start | bytes 1105928 | tf_op jit(solution)/shard_map/ppermute | solution.py:166
  148.5 11.0 %copy-start.5 = (f32[64,6]{0,1:T(8,128)S(1)}, f32[64,6]{0,1:T(8,128)}, u32[]{:S(2)}) copy-start(f32[64,6]{0,1:T(8,128)} %param.21) | copy-start | bytes 4612
  149.9 32.5 %all-to-all-start.1 = ((bf16[64,45,128]{2,1,0:T(8,128)(2,1)}), bf16[64,45,128]{2,1,0:T(8,128)(2,1)S(1)}, u32[]{:S(2)}, u32[]{:S(2)}) async-start(bf16[64,45,128]{2,1,0:T(8,128)(2,1)} %reshape.49), calls=%async_computation.1 | async-start | bytes 1572864 | tf_op jit(solution)/shard_map/all_to_all | solution.py:184

commit v7 on v4

--- a/solution.py
+++ b/solution.py
@@ -34,8 +34,6 @@
         better = length > best_len
         return jnp.where(better, r, best_row), jnp.where(better, length, best_len)
 
-    long_row, long_len = lax.fori_loop(0, rows, longest, (jnp.int32(0), len_ref[0]))
-
     def short_copy(r, which, buf):
         return pltpu.make_async_copy(
             kv_hbm.at[which, local_page(r, 0), pl.ds(0, SHORT), :],
@@ -43,17 +41,19 @@
             sem.at[which, r],
         )
 
+    @pl.loop(0, rows)
+    def _(r):
+        short_copy(r, 0, short_k).start()
+        short_copy(r, 1, short_v).start()
+
+    long_row, long_len = lax.fori_loop(0, rows, longest, (jnp.int32(0), len_ref[0]))
+
     def long_copy(j, which, buf):
         return pltpu.make_async_copy(
             kv_hbm.at[which, local_page(long_row, j)],
             buf.at[pl.ds(j * page_size, page_size), :],
             sem.at[2 + which, j],
         )
-
-    @pl.loop(0, rows)
-    def _(r):
-        short_copy(r, 0, short_k).start()
-        short_copy(r, 1, short_v).start()
 
     @pl.loop(0, table_width)
     def _(j):

time: 183 us -> 184 us (level)
  no operation moved by 1% of the time
where the time goes in v7:
time: 184 us; the launch traced here: 183 us
  waiting for transfers between devices  66.9 us (36%)
  blocking collectives  39.2 us (21%)
  starting transfers between devices  34 us (18%)
  local copies, waits for them, and re-layouts  16.7 us (9%)
  Pallas kernels  13.3 us (7%)
  matrix products  10.9 us (6%)
  other arithmetic  1.93 us (1%)
    ppermute x16, waiting for transfers between devices, ring_shift(): lax.ppermute(x, axis_name, [(i, (i + shift) % size) for i in range(size)])  44.1 us
    all_to_all x1, blocking collectives, dense_all_to_all(): lax.all_to_all(flat, axis_name, split_axis=0, concat_axis=0, tiled=True)  39.2 us
    ppermute x16, starting transfers between devices, ring_shift(): lax.ppermute(x, axis_name, [(i, (i + shift) % size) for i in range(size)])  24.4 us
    all_to_all x1, waiting for transfers between devices, dense_all_to_all(): lax.all_to_all(flat, axis_name, split_axis=0, concat_axis=0, tiled=True)  22.7 us
    pallas_call x1, Pallas kernels, local_attention(): pl.pallas_call(attention_kernel, out_shape=jax.ShapeDtypeStruct(query.sha...  13.3 us
    all_to_all x1, starting transfers between devices, dense_all_to_all(): lax.all_to_all(flat, axis_name, split_axis=0, concat_axis=0, tiled=True)  9.55 us
    dot_general x4, matrix products, per_device(): jnp.einsum('snc,cgf->sngf', piece, weight, preferred_element_type=jnp.flo...  5.84 us
    dynamic_slice x1, local copies, waits for them, and re-layouts, per_device(): lax.dynamic_index_in_dim(split_w1, (tensor_index - shift) % tensor_size,...  4.22 us
  transfers between devices with their start and end apart: 17, of which 8 were waited for; matrix products, arithmetic and copies ran while one was open for 7% of the time, Pallas kernels for 0%

profile of v7, /device:TPU:1, one launch (start us, length us, event | category | flops | bytes accessed | tf_op | source)
XLA Modules:
  0.0 183.2 jit_solution(6702152330424524508)
XLA Ops:
  0.0 1.4 copy.52.table_ref
  1.4 13.3 %shard_map.118 = bf16[64,640]{1,0:T(8,128)(2,1)} custom-call(s32[64,32]{1,0:T(8,128)} %copy.52.table_ref, s32[64]{0:T(128)} %len_ref.1, s32[1]{0:T(128)} %bitcast.base_ref, bf16[64,640]{1,0:T(8,128)(2,1)} %q_ref.1, bf16[2,64,128]{2,1,0:T(8,128)(2,1)} %new_kv_ref.1, bf16[2,95,128,128]{3,2,1,0:T(8,128)(2,1)} %kv_hbm.1), custom_call_target="tpu_custom_call" | custom-call | flops 335544320 | bytes 4194304 | tf_op jit(solution)/shard_map/pallas_call | solution.py:145
  14.7 1.6 fusion
  17.1 2.1 %collective-permute-start = (f32[64,640]{1,0:T(8,128)S(1)}, f32[64,640]{1,0:T(8,128)S(1)}, u32[]{:S(2)}, u32[]{:S(2)}) collective-permute-start(f32[64,640]{1,0:T(8,128)S(1)} %get-tuple-element.16), channel_id=1, source_target_pairs={{0,1},{1,2},{2,3},{3,0},{4,5},{5,6},{6,7},{7,4},{8,9},{9,10},{10,1... | collective-permute-start | bytes 491528 | tf_op jit(solution)/shard_map/ppermute | solution.py:166
  19.3 2.4 %collective-permute-start.1 = (f32[64,640]{1,0:T(8,128)S(1)}, f32[64,640]{1,0:T(8,128)S(1)}, u32[]{:S(2)}, u32[]{:S(2)}) collective-permute-start(f32[64,640]{1,0:T(8,128)S(1)} %get-tuple-element.18), channel_id=1, source_target_pairs={{0,2},{1,3},{2,0},{3,1},{4,6},{5,7},{6,4},{7,5},{8,10},{9,11},{10,... | collective-permute-start | bytes 491528 | tf_op jit(solution)/shard_map/ppermute | solution.py:166
  21.7 1.2 collective-permute-start.2
  23.6 5.3 %collective-permute-done.1 = f32[64,640]{1,0:T(8,128)S(1)} collective-permute-done((f32[64,640]{1,0:T(8,128)S(1)}, f32[64,640]{1,0:T(8,128)S(1)}, u32[]{:S(2)}, u32[]{:S(2)}) %collective-permute-start.1) | collective-permute-done | bytes 163872 | tf_op jit(solution)/shard_map/ppermute | solution.py:166
  28.9 1.1 multiply_reduce_fusion
  30.0 1.0 collective-permute-start.3
  31.0 1.9 %collective-permute-start.4 = (f32[64,1]{0,1:T(1,128)S(1)}, f32[64,1]{0,1:T(1,128)S(1)}, u32[]{:S(2)}, u32[]{:S(2)}) collective-permute-start(f32[64,1]{0,1:T(1,128)S(1)} %bitcast.91), channel_id=1, source_target_pairs={{0,2},{1,3},{2,0},{3,1},{4,6},{5,7},{6,4},{7,5},{8,10},{9,11},{10,... | collective-permute-start | bytes 776 | tf_op jit(solution)/shard_map/ppermute | solution.py:166
  33.0 1.3 collective-permute-start.5
  36.4 39.2 %all_to_all.10 = bf16[64,45,128]{2,1,0:T(8,128)(2,1)S(1)} all-to-all(bf16[64,45,128]{2,1,0:T(8,128)(2,1)S(1)} %reshape_reshape.6), channel_id=1, replica_groups=mesh['dp'=64,'tensor'=4] {'dp'}, dimensions={0} | all-to-all | bytes 1474560 | tf_op jit(solution)/shard_map/all_to_all | solution.py:184
  77.3 2.7 %collective-permute-start.8 = (bf16[64,9,640]{2,0,1:T(8,128)(2,1)}, bf16[64,9,640]{2,0,1:T(8,128)(2,1)}, u32[]{:S(2)}, u32[]{:S(2)}) collective-permute-start(bf16[64,9,640]{2,0,1:T(8,128)(2,1)} %copy.58), channel_id=1, source_target_pairs={{0,3},{1,0},{2,1},{3,2},{4,7},{5,4},{6,5},{7,6},{8,11},{9,8},{10,9... | collective-permute-start | bytes 2211848 | tf_op jit(solution)/shard_map/ppermute | solution.py:166
  80.0 2.0 %reshape_squeeze.3 = bf16[384,4,640]{2,1,0:T(4,128)(2,1)} reshape(bf16[1,384,2560]{2,1,0:T(8,128)(2,1)S(1)} %copy-done.2) | data formatting | bytes 3932160 | tf_op jit(solution)/shard_map/reshape;squeeze | solution.py:276
  82.0 4.2 %constant_dynamic-slice_fusion = (bf16[1,640,2,384]{3,2,1,0:T(2,128)(2,1)S(1)}, bf16[1,640,2,384]{3,2,1,0:T(2,128)(2,1)S(1)}, bf16[1,640,2,384]{3,2,1,0:T(2,128)(2,1)S(1)}, bf16[1,640,2,384]{3,2,1,0:T(2,128)(2,1)S(1)}) fusion(bf16[4,640,2,384]{3,2,1,0:T(2,128)(2,1)} %bitcast.88, s32[]{:T(128)S(6)} %select_n.94, s32[]{:T(128)S(6)} %select_n.92, ...), kind=kLoop, calls=%fused_computation.58 | loop fusion | bytes 7864336 | tf_op jit(solution)/shard_map/jit(dynamic_index_in_dim)/dynamic_slice | solution.py:287
  86.2 10.3 %collective-permute-done.6 = bf16[64,9,640]{2,0,1:T(8,128)(2,1)} collective-permute-done((bf16[64,9,640]{2,0,1:T(8,128)(2,1)}, bf16[64,9,640]{2,0,1:T(8,128)(2,1)}, u32[]{:S(2)}, u32[]{:S(2)}) %collective-permute-start.6) | collective-permute-done | bytes 737312 | tf_op jit(solution)/shard_map/ppermute | solution.py:166
  96.5 1.0 slice.32
  97.6 1.0 slice.33
  98.6 2.7 %collective-permute-start.9 = (bf16[32,9,640]{2,0,1:T(8,128)(2,1)S(1)}, bf16[32,9,640]{2,0,1:T(8,128)(2,1)S(1)}, u32[]{:S(2)}, u32[]{:S(2)}) collective-permute-start(bf16[32,9,640]{2,0,1:T(8,128)(2,1)S(1)} %slice.33), channel_id=1, source_target_pairs={{0,3},{1,0},{2,1},{3,2},{4,7},{5,4},{6,5},{7,6},{8,11},{9,8},{10,9... | collective-permute-start | bytes 1105928 | tf_op jit(solution)/shard_map/ppermute | solution.py:166
  102.2 2.0 %fusion.12 = f32[64,9,2,384]{3,0,2,1:T(8,128)S(1)} fusion(bf16[1,640,2,384]{3,2,1,0:T(2,128)(2,1)S(1)} %get-tuple-element.9, bf16[64,9,640]{2,0,1:T(8,128)(2,1)} %collective-permute-done.6), kind=kOutput, calls=%fused_computation.21 | convolution fusion | flops 566231040 | bytes 3489792 | tf_op jit(solution)/shard_map/snc,cgf->sngf/dot_general | solution.py:290
  104.2 3.5 %collective-permute-done.7 = bf16[32,9,640]{2,0,1:T(8,128)(2,1)S(1)} collective-permute-done((bf16[32,9,640]{2,0,1:T(8,128)(2,1)S(1)}, bf16[32,9,640]{2,0,1:T(8,128)(2,1)S(1)}, u32[]{:S(2)}, u32[]{:S(2)}) %collective-permute-start.7) | collective-permute-done | bytes 368672 | tf_op jit(solution)/shard_map/ppermute | solution.py:166
  108.7 2.1 %add_add_fusion = f32[64,9,2,384]{3,0,2,1:T(8,128)S(1)} fusion(f32[64,9,2,384]{3,0,2,1:T(8,128)S(1)} %fusion.11, f32[64,9,2,384]{3,0,2,1:T(8,128)S(1)} %fusion.13, f32[64,9,2,384]{3,0,2,1:T(8,128)S(1)} %fusion.12, bf16[1,640,2,384]{3,2,1,0:T(2,128)(2,1)S(1)} %get-tuple-element.7, bf16[64,9,640]{2,0,1:T(8,128)(2,1)} %collective-permute-done.8), kind=kOutput, calls=%fused_computation.6 | convolution fusion | flops 567558144 | bytes 8798208 | tf_op jit(solution)/shard_map/snc,cgf->sngf/dot_general | solution.py:290
  110.8 1.7 convolution_convert_fusion
  113.1 3.4 %collective-permute-start.14 = (bf16[32,9,640]{2,0,1:T(8,128)(2,1)S(1)}, bf16[32,9,640]{2,0,1:T(8,128)(2,1)S(1)}, u32[]{:S(2)}, u32[]{:S(2)}) collective-permute-start(bf16[32,9,640]{2,0,1:T(8,128)(2,1)S(1)} %get-tuple-element.15), channel_id=1, source_target_pairs={{0,3},{1,0},{2,1},{3,2},{4,7},{5,4},{6,5},{7,6},{8,11},{9,8},{10,9... | collective-permute-start | bytes 1105928 | tf_op jit(solution)/shard_map/ppermute | solution.py:166
  116.4 2.7 %collective-permute-start.11 = (bf16[64,9,640]{2,0,1:T(8,128)(2,1)S(1)}, bf16[64,9,640]{2,0,1:T(8,128)(2,1)S(1)}, u32[]{:S(2)}, u32[]{:S(2)}) collective-permute-start(bf16[64,9,640]{2,0,1:T(8,128)(2,1)S(1)} %get-tuple-element.12), channel_id=1, source_target_pairs={{0,3},{1,0},{2,1},{3,2},{4,7},{5,4},{6,5},{7,6},{8,11},{9,8},{10,9... | collective-permute-start | bytes 2211848 | tf_op jit(solution)/shard_map/ppermute | solution.py:166
  119.1 3.8 %collective-permute-done.12 = bf16[32,9,640]{2,0,1:T(8,128)(2,1)S(1)} collective-permute-done((bf16[32,9,640]{2,0,1:T(8,128)(2,1)S(1)}, bf16[32,9,640]{2,0,1:T(8,128)(2,1)S(1)}, u32[]{:S(2)}, u32[]{:S(2)}) %collective-permute-start.12) | collective-permute-done | bytes 368672 | tf_op jit(solution)/shard_map/ppermute | solution.py:166
  122.9 2.7 %collective-permute-start.15 = (bf16[32,9,640]{2,0,1:T(8,128)(2,1)S(1)}, bf16[32,9,640]{2,0,1:T(8,128)(2,1)S(1)}, u32[]{:S(2)}, u32[]{:S(2)}) collective-permute-start(bf16[32,9,640]{2,0,1:T(8,128)(2,1)S(1)} %collective-permute-done.14), channel_id=1, source_target_pairs={{0,3},{1,0},{2,1},{3,2},{4,7},{5,4},{6,5},{7,6},{8,11},{9,8},{10,9... | collective-permute-start | bytes 1105928 | tf_op jit(solution)/shard_map/ppermute | solution.py:166
  125.6 21.0 %collective-permute-done.13 = bf16[32,9,640]{2,0,1:T(8,128)(2,1)S(1)} collective-permute-done((bf16[32,9,640]{2,0,1:T(8,128)(2,1)S(1)}, bf16[32,9,640]{2,0,1:T(8,128)(2,1)S(1)}, u32[]{:S(2)}, u32[]{:S(2)}) %collective-permute-start.13) | collective-permute-done | bytes 368672 | tf_op jit(solution)/shard_map/ppermute | solution.py:166
  147.5 1.4 reshape.48
  148.9 9.5 %all-to-all-start.1 = ((bf16[64,45,128]{2,1,0:T(8,128)(2,1)}), bf16[64,45,128]{2,1,0:T(8,128)(2,1)S(1)}, u32[]{:S(2)}, u32[]{:S(2)}) async-start(bf16[64,45,128]{2,1,0:T(8,128)(2,1)} %reshape.48), calls=%async_computation.1 | async-start | bytes 1572864 | tf_op jit(solution)/shard_map/all_to_all | solution.py:184
  158.7 22.7 %all-to-all-done.1 = bf16[64,45,128]{2,1,0:T(8,128)(2,1)S(1)} async-done(((bf16[64,45,128]{2,1,0:T(8,128)(2,1)}), bf16[64,45,128]{2,1,0:T(8,128)(2,1)S(1)}, u32[]{:S(2)}, u32[]{:S(2)}) %all-to-all-start.1) | async-done | bytes 737312 | tf_op jit(solution)/shard_map/all_to_all | solution.py:184
  182.0 1.1 fusion.8
  (51 shorter events, 9.4 us)
Async XLA Ops:
  1.4 13.3 %copy-start = (bf16[640,2560]{1,0:T(8,128)(2,1)S(1)}, bf16[640,2560]{1,0:T(8,128)(2,1)}, u32[]{:S(2)}) copy-start(bf16[640,2560]{1,0:T(8,128)(2,1)} %param.18) | copy-start | bytes 9830404
  14.7 8.2 %copy-start.4 = (s32[64,6]{0,1:T(8,128)S(1)}, s32[64,6]{0,1:T(8,128)}, u32[]{:S(2)}) copy-start(s32[64,6]{0,1:T(8,128)} %param.20) | copy-start | bytes 4612
  16.3 0.8 copy-start.1
  17.1 6.4 %collective-permute-start = (f32[64,640]{1,0:T(8,128)S(1)}, f32[64,640]{1,0:T(8,128)S(1)}, u32[]{:S(2)}, u32[]{:S(2)}) collective-permute-start(f32[64,640]{1,0:T(8,128)S(1)} %get-tuple-element.16), channel_id=1, source_target_pairs={{0,1},{1,2},{2,3},{3,0},{4,5},{5,6},{6,7},{7,4},{8,9},{9,10},{10,1... | collective-permute-start | bytes 491528 | tf_op jit(solution)/shard_map/ppermute | solution.py:166
  19.3 9.6 %collective-permute-start.1 = (f32[64,640]{1,0:T(8,128)S(1)}, f32[64,640]{1,0:T(8,128)S(1)}, u32[]{:S(2)}, u32[]{:S(2)}) collective-permute-start(f32[64,640]{1,0:T(8,128)S(1)} %get-tuple-element.18), channel_id=1, source_target_pairs={{0,2},{1,3},{2,0},{3,1},{4,6},{5,7},{6,4},{7,5},{8,10},{9,11},{10,... | collective-permute-start | bytes 491528 | tf_op jit(solution)/shard_map/ppermute | solution.py:166
  21.7 7.2 %collective-permute-start.2 = (f32[64,640]{1,0:T(8,128)S(1)}, f32[64,640]{1,0:T(8,128)S(1)}, u32[]{:S(2)}, u32[]{:S(2)}) collective-permute-start(f32[64,640]{1,0:T(8,128)S(1)} %get-tuple-element.17), channel_id=1, source_target_pairs={{0,3},{1,0},{2,1},{3,2},{4,7},{5,4},{6,5},{7,6},{8,11},{9,8},{10,9... | collective-permute-start | bytes 491528 | tf_op jit(solution)/shard_map/ppermute | solution.py:166
  30.0 5.3 %collective-permute-start.3 = (f32[64,1]{0,1:T(1,128)S(1)}, f32[64,1]{0,1:T(1,128)S(1)}, u32[]{:S(2)}, u32[]{:S(2)}) collective-permute-start(f32[64,1]{0,1:T(1,128)S(1)} %bitcast.90), channel_id=1, source_target_pairs={{0,1},{1,2},{2,3},{3,0},{4,5},{5,6},{6,7},{7,4},{8,9},{9,10},{10,1... | collective-permute-start | bytes 776 | tf_op jit(solution)/shard_map/ppermute | solution.py:166
  31.0 4.2 %collective-permute-start.4 = (f32[64,1]{0,1:T(1,128)S(1)}, f32[64,1]{0,1:T(1,128)S(1)}, u32[]{:S(2)}, u32[]{:S(2)}) collective-permute-start(f32[64,1]{0,1:T(1,128)S(1)} %bitcast.91), channel_id=1, source_target_pairs={{0,2},{1,3},{2,0},{3,1},{4,6},{5,7},{6,4},{7,5},{8,10},{9,11},{10,... | collective-permute-start | bytes 776 | tf_op jit(solution)/shard_map/ppermute | solution.py:166
  33.0 2.4 %collective-permute-start.5 = (f32[64,1]{0,1:T(1,128)S(1)}, f32[64,1]{0,1:T(1,128)S(1)}, u32[]{:S(2)}, u32[]{:S(2)}) collective-permute-start(f32[64,1]{0,1:T(1,128)S(1)} %bitcast.92), channel_id=1, source_target_pairs={{0,3},{1,0},{2,1},{3,2},{4,7},{5,4},{6,5},{7,6},{8,11},{9,8},{10,9... | collective-permute-start | bytes 776 | tf_op jit(solution)/shard_map/ppermute | solution.py:166
  76.3 3.7 %copy-start.2 = (bf16[1,384,2560]{2,1,0:T(8,128)(2,1)S(1)}, bf16[1,384,2560]{2,1,0:T(8,128)(2,1)}, u32[]{:S(2)}) copy-start(bf16[1,384,2560]{2,1,0:T(8,128)(2,1)} %param.23) | copy-start | bytes 5898244
  77.3 19.2 %collective-permute-start.6 = (bf16[64,9,640]{2,0,1:T(8,128)(2,1)}, bf16[64,9,640]{2,0,1:T(8,128)(2,1)}, u32[]{:S(2)}, u32[]{:S(2)}) collective-permute-start(bf16[64,9,640]{2,0,1:T(8,128)(2,1)} %copy.58), channel_id=1, source_target_pairs={{0,1},{1,2},{2,3},{3,0},{4,5},{5,6},{6,7},{7,4},{8,9},{9,10},{10,1... | collective-permute-start | bytes 2211848 | tf_op jit(solution)/shard_map/ppermute | solution.py:166
  77.3 20.3 %collective-permute-start.8 = (bf16[64,9,640]{2,0,1:T(8,128)(2,1)}, bf16[64,9,640]{2,0,1:T(8,128)(2,1)}, u32[]{:S(2)}, u32[]{:S(2)}) collective-permute-start(bf16[64,9,640]{2,0,1:T(8,128)(2,1)} %copy.58), channel_id=1, source_target_pairs={{0,3},{1,0},{2,1},{3,2},{4,7},{5,4},{6,5},{7,6},{8,11},{9,8},{10,9... | collective-permute-start | bytes 2211848 | tf_op jit(solution)/shard_map/ppermute | solution.py:166
  97.5 10.2 %collective-permute-start.7 = (bf16[32,9,640]{2,0,1:T(8,128)(2,1)S(1)}, bf16[32,9,640]{2,0,1:T(8,128)(2,1)S(1)}, u32[]{:S(2)}, u32[]{:S(2)}) collective-permute-start(bf16[32,9,640]{2,0,1:T(8,128)(2,1)S(1)} %slice.32), channel_id=1, source_target_pairs={{0,1},{1,2},{2,3},{3,0},{4,5},{5,6},{6,7},{7,4},{8,9},{9,10},{10,1... | collective-permute-start | bytes 1105928 | tf_op jit(solution)/shard_map/ppermute | solution.py:166
  98.6 9.1 %collective-permute-start.9 = (bf16[32,9,640]{2,0,1:T(8,128)(2,1)S(1)}, bf16[32,9,640]{2,0,1:T(8,128)(2,1)S(1)}, u32[]{:S(2)}, u32[]{:S(2)}) collective-permute-start(bf16[32,9,640]{2,0,1:T(8,128)(2,1)S(1)} %slice.33), channel_id=1, source_target_pairs={{0,3},{1,0},{2,1},{3,2},{4,7},{5,4},{6,5},{7,6},{8,11},{9,8},{10,9... | collective-permute-start | bytes 1105928 | tf_op jit(solution)/shard_map/ppermute | solution.py:166
  108.6 2.2 %copy-start.3 = (bf16[384,4,640]{2,1,0:T(4,128)(2,1)S(1)}, bf16[384,4,640]{2,1,0:T(4,128)(2,1)}, u32[]{:S(2)}) copy-start(bf16[384,4,640]{2,1,0:T(4,128)(2,1)} %reshape_squeeze.3) | copy-start | bytes 5898244
  112.9 10.1 %collective-permute-start.12 = (bf16[32,9,640]{2,0,1:T(8,128)(2,1)S(1)}, bf16[32,9,640]{2,0,1:T(8,128)(2,1)S(1)}, u32[]{:S(2)}, u32[]{:S(2)}) collective-permute-start(bf16[32,9,640]{2,0,1:T(8,128)(2,1)S(1)} %get-tuple-element.14), channel_id=1, source_target_pairs={{0,1},{1,2},{2,3},{3,0},{4,5},{5,6},{6,7},{7,4},{8,9},{9,10},{10,1... | collective-permute-start | bytes 1105928 | tf_op jit(solution)/shard_map/ppermute | solution.py:166
  113.1 9.9 %collective-permute-start.14 = (bf16[32,9,640]{2,0,1:T(8,128)(2,1)S(1)}, bf16[32,9,640]{2,0,1:T(8,128)(2,1)S(1)}, u32[]{:S(2)}, u32[]{:S(2)}) collective-permute-start(bf16[32,9,640]{2,0,1:T(8,128)(2,1)S(1)} %get-tuple-element.15), channel_id=1, source_target_pairs={{0,3},{1,0},{2,1},{3,2},{4,7},{5,4},{6,5},{7,6},{8,11},{9,8},{10,9... | collective-permute-start | bytes 1105928 | tf_op jit(solution)/shard_map/ppermute | solution.py:166
  116.4 30.2 %collective-permute-start.10 = (bf16[64,9,640]{2,0,1:T(8,128)(2,1)S(1)}, bf16[64,9,640]{2,0,1:T(8,128)(2,1)S(1)}, u32[]{:S(2)}, u32[]{:S(2)}) collective-permute-start(bf16[64,9,640]{2,0,1:T(8,128)(2,1)S(1)} %get-tuple-element.13), channel_id=1, source_target_pairs={{0,1},{1,2},{2,3},{3,0},{4,5},{5,6},{6,7},{7,4},{8,9},{9,10},{10,1... | collective-permute-start | bytes 2211848 | tf_op jit(solution)/shard_map/ppermute | solution.py:166
  116.4 30.2 %collective-permute-start.11 = (bf16[64,9,640]{2,0,1:T(8,128)(2,1)S(1)}, bf16[64,9,640]{2,0,1:T(8,128)(2,1)S(1)}, u32[]{:S(2)}, u32[]{:S(2)}) collective-permute-start(bf16[64,9,640]{2,0,1:T(8,128)(2,1)S(1)} %get-tuple-element.12), channel_id=1, source_target_pairs={{0,3},{1,0},{2,1},{3,2},{4,7},{5,4},{6,5},{7,6},{8,11},{9,8},{10,9... | collective-permute-start | bytes 2211848 | tf_op jit(solution)/shard_map/ppermute | solution.py:166
  122.9 23.7 %collective-permute-start.13 = (bf16[32,9,640]{2,0,1:T(8,128)(2,1)S(1)}, bf16[32,9,640]{2,0,1:T(8,128)(2,1)S(1)}, u32[]{:S(2)}, u32[]{:S(2)}) collective-permute-start(bf16[32,9,640]{2,0,1:T(8,128)(2,1)S(1)} %collective-permute-done.12), channel_id=1, source_target_pairs={{0,1},{1,2},{2,3},{3,0},{4,5},{5,6},{6,7},{7,4},{8,9},{9,10},{10,1... | collective-permute-start | bytes 1105928 | tf_op jit(solution)/shard_map/ppermute | solution.py:166
  122.9 23.7 %collective-permute-start.15 = (bf16[32,9,640]{2,0,1:T(8,128)(2,1)S(1)}, bf16[32,9,640]{2,0,1:T(8,128)(2,1)S(1)}, u32[]{:S(2)}, u32[]{:S(2)}) collective-permute-start(bf16[32,9,640]{2,0,1:T(8,128)(2,1)S(1)} %collective-permute-done.14), channel_id=1, source_target_pairs={{0,3},{1,0},{2,1},{3,2},{4,7},{5,4},{6,5},{7,6},{8,11},{9,8},{10,9... | collective-permute-start | bytes 1105928 | tf_op jit(solution)/shard_map/ppermute | solution.py:166
  147.5 11.0 %copy-start.5 = (f32[64,6]{0,1:T(8,128)S(1)}, f32[64,6]{0,1:T(8,128)}, u32[]{:S(2)}) copy-start(f32[64,6]{0,1:T(8,128)} %param.21) | copy-start | bytes 4612
  148.9 32.5 %all-to-all-start.1 = ((bf16[64,45,128]{2,1,0:T(8,128)(2,1)}), bf16[64,45,128]{2,1,0:T(8,128)(2,1)S(1)}, u32[]{:S(2)}, u32[]{:S(2)}) async-start(bf16[64,45,128]{2,1,0:T(8,128)(2,1)} %reshape.48), calls=%async_computation.1 | async-start | bytes 1572864 | tf_op jit(solution)/shard_map/all_to_all | solution.py:184
